TPU v7x, 32 devices: a whole 2x2x4 slice. The times are simulated.
32 devices in a mesh: grp: 2 (over x), dev: 16 (over z, y, core).
Axes of the slice: x: 2, y: 2, z: 4, core: 2. Of those that a mesh axis runs over, the one named last changes fastest.
Arguments:
- a_blocks: bfloat16 [16384, 768], P(('grp', 'dev')), may hold values from -1.5 to 1.5
- a_cols: int32 [256, 12], P(('grp', 'dev')), may hold values from 0 to 255, as said below
- p_blocks: bfloat16 [16384, 256], P(('grp', 'dev')), may hold values from -0.375 to 0.375
- p_cols: int32 [256, 4], P(('grp', 'dev')), may hold values from 0 to 63, as said below
Outputs:
- c_coarse: bfloat16 [2, 2048, 896], P(None, 'dev')
Inputs may be any that keep to these rules, and one draw needn't show every extreme that they name: a_cols[i,0] = i, and every entry of block row i lies from (i // 8 - 1) * 8 to (i // 8 + 2) * 8 - 1. p_cols[i,0] = (i // 8) * 2 + (i % 8) * 2 // 8, the aggregate of fine block row i; the entries of one row are distinct and lie from (i // 8 - 1) * 2 to (i // 8 + 2) * 2 - 1.
All inputs are finite; a program needn't handle non-finite values.
Results may differ from a plain program's by a relative error of at most 0.005.
Values may be sent and summed in bfloat16 or wider, within the bound.
No kernel may reach another device: no remote copies, remote signals or barrier semaphores. Data moves between devices by JAX's collectives and lax.ppermute only.
A program may use at most 64 MiB of HBM per device.

v0:
```python
import jax
import jax.numpy as jnp
from jax import lax
from jax.sharding import PartitionSpec as P

B = 64
KA = 12
KP = 4
NC = 2
RB = 8


def with_halo(cells, sides, width):
    for axis, dim in sides:
        count = lax.axis_size(axis)
        ends = count - 1
        head = lax.slice_in_dim(cells, 0, width, axis=dim)
        tail = lax.slice_in_dim(cells, cells.shape[dim] - width, cells.shape[dim], axis=dim)
        cells = jnp.concatenate(
            [
                lax.ppermute(tail, axis, [(i, (i + 1) % count) for i in range(ends)]),
                cells,
                lax.ppermute(head, axis, [((i + 1) % count, i) for i in range(ends)]),
            ],
            axis=dim,
        )
    return cells


def shifted(x, axis, by):
    peers = lax.axis_size(axis)
    pairs = [(i, i + by) for i in range(peers) if 0 <= i + by < peers]
    return lax.ppermute(x, axis, pairs)


def partner_2(x, axis, bit):
    return lax.ppermute(x, axis, [(i, i ^ 1 << bit) for i in range(lax.axis_size(axis))])


def one_hot(values, levels):
    return (values[..., None] == jnp.arange(levels, dtype=jnp.int32)).astype(jnp.bfloat16)


def local(a_blocks, a_cols, p_blocks, p_cols):
    device = lax.axis_index(("grp", "dev"))
    p_rows = p_blocks.reshape(RB, B, KP * B)
    p_near, pcol_near = (
        with_halo(p_rows, ((("grp", "dev"), 0),), RB),
        with_halo(p_cols, ((("grp", "dev"), 0),), RB),
    )
    local_cols = a_cols - (device - 1) * RB
    picked = jnp.take(p_near, local_cols, axis=0).reshape(RB, KA, B, KP, B)
    target = jnp.take(pcol_near, local_cols, axis=0) - (device - 2) * NC
    column_hot = one_hot(target, 5 * NC)
    a_rows = a_blocks.reshape(RB, B, KA * B)

    def product_row(inputs):
        a_row, p_row, hot_row = inputs
        spread = jnp.einsum(
            "kslt,klj->ksjt", p_row, hot_row, preferred_element_type=jnp.float32
        ).astype(jnp.bfloat16)
        panel = spread.reshape(KA * B, 5 * NC * B)
        return jnp.dot(a_row, panel, preferred_element_type=jnp.float32).astype(jnp.bfloat16)

    coupled = lax.map(product_row, (a_rows, picked, column_hot))
    own_block = p_near[RB : 2 * RB].reshape(RB, B, KP, B)
    row_hot = one_hot(pcol_near[RB : 2 * RB] - (device - 1) * NC, 3 * NC)
    scattered = jnp.einsum(
        "irms,imo->iros", own_block, row_hot, preferred_element_type=jnp.float32
    ).astype(jnp.bfloat16)
    partial_value = lax.dot_general(
        scattered.reshape(RB * B, 3 * NC * B),
        coupled.reshape(RB * B, 5 * NC * B),
        (((0,), (0,)), ((), ())),
        preferred_element_type=jnp.float32,
    )
    partial_value = partial_value.reshape(3, NC * B, 5 * NC * B)
    from_right = shifted(partial_value[0], ("grp", "dev"), -1)
    from_left = shifted(partial_value[2], ("grp", "dev"), 1)
    span = NC * B
    combined = jnp.pad(partial_value[1], ((0, 0), (span, span)))
    combined = combined + jnp.pad(from_right, ((0, 0), (2 * span, 0)))
    combined = combined + jnp.pad(from_left, ((0, 0), (0, 2 * span)))
    rows_here = combined.astype(jnp.bfloat16)[None]
    group = lax.axis_index("grp")
    joined = rows_here
    for section_bit in range(lax.axis_size("grp").bit_length() - 1):
        partner = partner_2(joined, "grp", section_bit)
        is_upper = group // 2**section_bit % 2 == 1
        joined = jnp.where(
            is_upper,
            jnp.concatenate([partner, joined], axis=0),
            jnp.concatenate([joined, partner], axis=0),
        )
    return joined


def solution(mesh):
    placed = (
        P(("grp", "dev"), None),
        P(("grp", "dev"), None),
        P(("grp", "dev"), None),
        P(("grp", "dev"), None),
    )
    return jax.shard_map(
        local, mesh=mesh, in_specs=placed, out_specs=P(None, "dev", None), check_vma=False
    )
```

profile of v0, /device:TPU:0, one launch (start us, length us, event | category | flops | bytes accessed | tf_op | source)
XLA Modules:
  0.0 129.6 jit_solution(10601509217071770021)
XLA Ops:
  0.0 2.4 %collective-permute-start.2 = (bf16[8,64,256]{2,1,0:T(8,128)(2,1)}, bf16[8,64,256]{2,1,0:T(8,128)(2,1)S(1)}, u32[]{:S(2)}, u32[]{:S(2)}) collective-permute-start(bf16[8,64,256]{2,1,0:T(8,128)(2,1)} %bitcast.48), channel_id=1, source_target_pairs={{0,1},{1,2},{2,3},{3,4},{4,5},{5,6},{6,7},{7,8},{8,9},{9,10},{10,1... | collective-permute-start | bytes 786440 | tf_op jit(solution)/shard_map/ppermute | solution.py:21
  3.7 5.1 %collective-permute-start = (s32[8,4]{0,1:T(4,128)}, s32[8,4]{0,1:T(4,128)S(1)}, u32[]{:S(2)}, u32[]{:S(2)}) collective-permute-start(s32[8,4]{0,1:T(4,128)} %param.9), channel_id=1, source_target_pairs={{0,1},{1,2},{2,3},{3,4},{4,5},{5,6},{6,7},{7,8},{8,9},{9,10},{10,1... | collective-permute-start | bytes 392 | tf_op jit(solution)/shard_map/ppermute | solution.py:21
  17.9 2.6 %gather_fusion.1 = bf16[96,64,256]{2,1,0:T(8,128)(2,1)} fusion(bf16[24,64,256]{2,1,0:T(8,128)(2,1)S(1)} %pad_maximum_fusion, s32[1024]{0:T(1024)S(1)} %pad_clamp_fusion), kind=kCustom, calls=%fused_computation.1 | custom fusion | bytes 6291840 | tf_op jit(solution)/shard_map/jit(_take)/gather | solution.py:52
  20.5 10.2 %gather.12 = bf16[8,12,64,4,64]{4,3,2,1,0:T(4,128)(2,1)} reshape(bf16[96,64,256]{2,1,0:T(8,128)(2,1)} %gather_fusion.1) | data formatting | bytes 6291456 | tf_op jit(solution)/shard_map/jit(_take)/gather | solution.py:52
  30.7 8.3 %broadcast_select_fusion = bf16[8,12,64,4,64]{4,3,2,1,0:T(4,128)(2,1)} fusion(bf16[8,12,64,4,64]{4,3,2,1,0:T(4,128)(2,1)} %gather.12, pred[8,12]{1,0:T(8,128)(4,1)S(1)} %get-tuple-element.43), kind=kLoop, calls=%fused_computation.14 | loop fusion | flops 1572864 | bytes 6291552 | tf_op jit(solution)/shard_map/jit(_take)/select_n | solution.py:52
  39.0 56.1 %while.10 = (s32[]{:T(128)}, bf16[8,64,640]{2,1,0:T(8,128)(2,1)}, bf16[8,64,768]{2,1,0:T(8,128)(2,1)}, bf16[8,12,4,10]{3,2,1,0:T(4,128)(2,1)}, bf16[8,12,64,4,64]{4,3,2,1,0:T(4,128)(2,1)}, /*index=5*/s32[]{:T(128)}) while((s32[]{:T(128)}, bf16[8,64,640]{2,1,0:T(8,128)(2,1)}, bf16[8,64,768]{2,1,0:T(8,128)(2,1)}, ...), condition=%wide.region_1.2_spmd, body=%wide.region_0.1_spmd.sunk | while | flops 67379200 | bytes 4913221 | solution.py:65
  39.0 2.2 %convert_bitcast_fusion.2 = bf16[12,64,10,64]{3,2,1,0:T(8,128)(2,1)S(1)} fusion(bf16[8,12,64,4,64]{4,3,2,1,0:T(4,128)(2,1)} %get-tuple-element.95, s32[]{:T(128)} %get-tuple-element.85, bf16[8,12,4,10]{3,2,1,0:T(4,128)(2,1)} %get-tuple-element.94), kind=kOutput, calls=%fused_computation.2.clone.1 | convolution fusion | flops 4423680 | bytes 1782784 | tf_op jit(solution)/shard_map/while/body/eval_jaxpr/kslt,klj->ksjt/dot_general | solution.py:59
  41.2 2.6 %reshape.64 = bf16[768,640]{1,0:T(8,128)(2,1)} reshape(bf16[12,64,10,64]{3,2,1,0:T(8,128)(2,1)S(1)} %convert_bitcast_fusion.2) | data formatting | bytes 1966080 | tf_op jit(solution)/shard_map/while/body/eval_jaxpr/reshape | solution.py:62
  43.8 2.2 %fusion.31 = bf16[8,64,640]{2,1,0:T(8,128)(2,1)} fusion(bf16[8,64,640]{2,1,0:T(8,128)(2,1)} %get-tuple-element.86, s32[]{:T(128)} %get-tuple-element.85, bf16[768,640]{1,0:T(8,128)(2,1)} %reshape.64, bf16[8,64,768]{2,1,0:T(8,128)(2,1)} %get-tuple-element.93), kind=kOutput, calls=%fused_computation.5.clone.1 | convolution fusion | flops 62955520 | bytes 1164288 | tf_op jit(solution)/shard_map/while/body/eval_jaxpr/dot_general | solution.py:63
  46.0 2.2 %convert_bitcast_fusion.2 = bf16[12,64,10,64]{3,2,1,0:T(8,128)(2,1)S(1)} fusion(bf16[8,12,64,4,64]{4,3,2,1,0:T(4,128)(2,1)} %get-tuple-element.95, s32[]{:T(128)} %get-tuple-element.85, bf16[8,12,4,10]{3,2,1,0:T(4,128)(2,1)} %get-tuple-element.94), kind=kOutput, calls=%fused_computation.2.clone.1 | convolution fusion | flops 4423680 | bytes 1782784 | tf_op jit(solution)/shard_map/while/body/eval_jaxpr/kslt,klj->ksjt/dot_general | solution.py:59
  48.2 2.6 %reshape.64 = bf16[768,640]{1,0:T(8,128)(2,1)} reshape(bf16[12,64,10,64]{3,2,1,0:T(8,128)(2,1)S(1)} %convert_bitcast_fusion.2) | data formatting | bytes 1966080 | tf_op jit(solution)/shard_map/while/body/eval_jaxpr/reshape | solution.py:62
  50.8 2.2 %fusion.31 = bf16[8,64,640]{2,1,0:T(8,128)(2,1)} fusion(bf16[8,64,640]{2,1,0:T(8,128)(2,1)} %get-tuple-element.86, s32[]{:T(128)} %get-tuple-element.85, bf16[768,640]{1,0:T(8,128)(2,1)} %reshape.64, bf16[8,64,768]{2,1,0:T(8,128)(2,1)} %get-tuple-element.93), kind=kOutput, calls=%fused_computation.5.clone.1 | convolution fusion | flops 62955520 | bytes 1164288 | tf_op jit(solution)/shard_map/while/body/eval_jaxpr/dot_general | solution.py:63
  53.0 2.2 %convert_bitcast_fusion.2 = bf16[12,64,10,64]{3,2,1,0:T(8,128)(2,1)S(1)} fusion(bf16[8,12,64,4,64]{4,3,2,1,0:T(4,128)(2,1)} %get-tuple-element.95, s32[]{:T(128)} %get-tuple-element.85, bf16[8,12,4,10]{3,2,1,0:T(4,128)(2,1)} %get-tuple-element.94), kind=kOutput, calls=%fused_computation.2.clone.1 | convolution fusion | flops 4423680 | bytes 1782784 | tf_op jit(solution)/shard_map/while/body/eval_jaxpr/kslt,klj->ksjt/dot_general | solution.py:59
  55.2 2.6 %reshape.64 = bf16[768,640]{1,0:T(8,128)(2,1)} reshape(bf16[12,64,10,64]{3,2,1,0:T(8,128)(2,1)S(1)} %convert_bitcast_fusion.2) | data formatting | bytes 1966080 | tf_op jit(solution)/shard_map/while/body/eval_jaxpr/reshape | solution.py:62
  60.0 2.2 %convert_bitcast_fusion.2 = bf16[12,64,10,64]{3,2,1,0:T(8,128)(2,1)S(1)} fusion(bf16[8,12,64,4,64]{4,3,2,1,0:T(4,128)(2,1)} %get-tuple-element.95, s32[]{:T(128)} %get-tuple-element.85, bf16[8,12,4,10]{3,2,1,0:T(4,128)(2,1)} %get-tuple-element.94), kind=kOutput, calls=%fused_computation.2.clone.1 | convolution fusion | flops 4423680 | bytes 1782784 | tf_op jit(solution)/shard_map/while/body/eval_jaxpr/kslt,klj->ksjt/dot_general | solution.py:59
  62.3 2.6 %reshape.64 = bf16[768,640]{1,0:T(8,128)(2,1)} reshape(bf16[12,64,10,64]{3,2,1,0:T(8,128)(2,1)S(1)} %convert_bitcast_fusion.2) | data formatting | bytes 1966080 | tf_op jit(solution)/shard_map/while/body/eval_jaxpr/reshape | solution.py:62
  64.9 2.2 %fusion.31 = bf16[8,64,640]{2,1,0:T(8,128)(2,1)} fusion(bf16[8,64,640]{2,1,0:T(8,128)(2,1)} %get-tuple-element.86, s32[]{:T(128)} %get-tuple-element.85, bf16[768,640]{1,0:T(8,128)(2,1)} %reshape.64, bf16[8,64,768]{2,1,0:T(8,128)(2,1)} %get-tuple-element.93), kind=kOutput, calls=%fused_computation.5.clone.1 | convolution fusion | flops 62955520 | bytes 1164288 | tf_op jit(solution)/shard_map/while/body/eval_jaxpr/dot_general | solution.py:63
  67.1 2.2 %convert_bitcast_fusion.2 = bf16[12,64,10,64]{3,2,1,0:T(8,128)(2,1)S(1)} fusion(bf16[8,12,64,4,64]{4,3,2,1,0:T(4,128)(2,1)} %get-tuple-element.95, s32[]{:T(128)} %get-tuple-element.85, bf16[8,12,4,10]{3,2,1,0:T(4,128)(2,1)} %get-tuple-element.94), kind=kOutput, calls=%fused_computation.2.clone.1 | convolution fusion | flops 4423680 | bytes 1782784 | tf_op jit(solution)/shard_map/while/body/eval_jaxpr/kslt,klj->ksjt/dot_general | solution.py:59
  69.3 2.6 %reshape.64 = bf16[768,640]{1,0:T(8,128)(2,1)} reshape(bf16[12,64,10,64]{3,2,1,0:T(8,128)(2,1)S(1)} %convert_bitcast_fusion.2) | data formatting | bytes 1966080 | tf_op jit(solution)/shard_map/while/body/eval_jaxpr/reshape | solution.py:62
  71.9 2.2 %fusion.31 = bf16[8,64,640]{2,1,0:T(8,128)(2,1)} fusion(bf16[8,64,640]{2,1,0:T(8,128)(2,1)} %get-tuple-element.86, s32[]{:T(128)} %get-tuple-element.85, bf16[768,640]{1,0:T(8,128)(2,1)} %reshape.64, bf16[8,64,768]{2,1,0:T(8,128)(2,1)} %get-tuple-element.93), kind=kOutput, calls=%fused_computation.5.clone.1 | convolution fusion | flops 62955520 | bytes 1164288 | tf_op jit(solution)/shard_map/while/body/eval_jaxpr/dot_general | solution.py:63
  74.1 2.2 %convert_bitcast_fusion.2 = bf16[12,64,10,64]{3,2,1,0:T(8,128)(2,1)S(1)} fusion(bf16[8,12,64,4,64]{4,3,2,1,0:T(4,128)(2,1)} %get-tuple-element.95, s32[]{:T(128)} %get-tuple-element.85, bf16[8,12,4,10]{3,2,1,0:T(4,128)(2,1)} %get-tuple-element.94), kind=kOutput, calls=%fused_computation.2.clone.1 | convolution fusion | flops 4423680 | bytes 1782784 | tf_op jit(solution)/shard_map/while/body/eval_jaxpr/kslt,klj->ksjt/dot_general | solution.py:59
  76.3 2.6 %reshape.64 = bf16[768,640]{1,0:T(8,128)(2,1)} reshape(bf16[12,64,10,64]{3,2,1,0:T(8,128)(2,1)S(1)} %convert_bitcast_fusion.2) | data formatting | bytes 1966080 | tf_op jit(solution)/shard_map/while/body/eval_jaxpr/reshape | solution.py:62
  78.9 2.2 %fusion.31 = bf16[8,64,640]{2,1,0:T(8,128)(2,1)} fusion(bf16[8,64,640]{2,1,0:T(8,128)(2,1)} %get-tuple-element.86, s32[]{:T(128)} %get-tuple-element.85, bf16[768,640]{1,0:T(8,128)(2,1)} %reshape.64, bf16[8,64,768]{2,1,0:T(8,128)(2,1)} %get-tuple-element.93), kind=kOutput, calls=%fused_computation.5.clone.1 | convolution fusion | flops 62955520 | bytes 1164288 | tf_op jit(solution)/shard_map/while/body/eval_jaxpr/dot_general | solution.py:63
  81.1 2.2 %convert_bitcast_fusion.2 = bf16[12,64,10,64]{3,2,1,0:T(8,128)(2,1)S(1)} fusion(bf16[8,12,64,4,64]{4,3,2,1,0:T(4,128)(2,1)} %get-tuple-element.95, s32[]{:T(128)} %get-tuple-element.85, bf16[8,12,4,10]{3,2,1,0:T(4,128)(2,1)} %get-tuple-element.94), kind=kOutput, calls=%fused_computation.2.clone.1 | convolution fusion | flops 4423680 | bytes 1782784 | tf_op jit(solution)/shard_map/while/body/eval_jaxpr/kslt,klj->ksjt/dot_general | solution.py:59
  83.3 2.6 %reshape.64 = bf16[768,640]{1,0:T(8,128)(2,1)} reshape(bf16[12,64,10,64]{3,2,1,0:T(8,128)(2,1)S(1)} %convert_bitcast_fusion.2) | data formatting | bytes 1966080 | tf_op jit(solution)/shard_map/while/body/eval_jaxpr/reshape | solution.py:62
  85.9 2.2 %fusion.31 = bf16[8,64,640]{2,1,0:T(8,128)(2,1)} fusion(bf16[8,64,640]{2,1,0:T(8,128)(2,1)} %get-tuple-element.86, s32[]{:T(128)} %get-tuple-element.85, bf16[768,640]{1,0:T(8,128)(2,1)} %reshape.64, bf16[8,64,768]{2,1,0:T(8,128)(2,1)} %get-tuple-element.93), kind=kOutput, calls=%fused_computation.5.clone.1 | convolution fusion | flops 62955520 | bytes 1164288 | tf_op jit(solution)/shard_map/while/body/eval_jaxpr/dot_general | solution.py:63
  88.1 2.2 %convert_bitcast_fusion.2 = bf16[12,64,10,64]{3,2,1,0:T(8,128)(2,1)S(1)} fusion(bf16[8,12,64,4,64]{4,3,2,1,0:T(4,128)(2,1)} %get-tuple-element.95, s32[]{:T(128)} %get-tuple-element.85, bf16[8,12,4,10]{3,2,1,0:T(4,128)(2,1)} %get-tuple-element.94), kind=kOutput, calls=%fused_computation.2.clone.1 | convolution fusion | flops 4423680 | bytes 1782784 | tf_op jit(solution)/shard_map/while/body/eval_jaxpr/kslt,klj->ksjt/dot_general | solution.py:59
  90.3 2.6 %reshape.64 = bf16[768,640]{1,0:T(8,128)(2,1)} reshape(bf16[12,64,10,64]{3,2,1,0:T(8,128)(2,1)S(1)} %convert_bitcast_fusion.2) | data formatting | bytes 1966080 | tf_op jit(solution)/shard_map/while/body/eval_jaxpr/reshape | solution.py:62
  92.9 2.2 %fusion.31 = bf16[8,64,640]{2,1,0:T(8,128)(2,1)} fusion(bf16[8,64,640]{2,1,0:T(8,128)(2,1)} %get-tuple-element.86, s32[]{:T(128)} %get-tuple-element.85, bf16[768,640]{1,0:T(8,128)(2,1)} %reshape.64, bf16[8,64,768]{2,1,0:T(8,128)(2,1)} %get-tuple-element.93), kind=kOutput, calls=%fused_computation.5.clone.1 | convolution fusion | flops 62955520 | bytes 1164288 | tf_op jit(solution)/shard_map/while/body/eval_jaxpr/dot_general | solution.py:63
  98.1 4.9 %collective-permute-start.5 = (f32[128,640]{1,0:T(8,128)S(1)}, f32[128,640]{1,0:T(8,128)S(1)}, u32[]{:S(2)}, u32[]{:S(2)}) collective-permute-start(f32[128,640]{1,0:T(8,128)S(1)} %get-tuple-element.46), channel_id=1, source_target_pairs={{0,1},{1,2},{2,3},{3,4},{4,5},{5,6},{6,7},{7,8},{8,9},{9,10},{10,1... | collective-permute-start | bytes 983048 | tf_op jit(solution)/shard_map/ppermute | solution.py:33
  104.3 20.5 %collective-permute-start.6 = (bf16[1,128,896]{2,1,0:T(8,128)(2,1)S(1)}, bf16[1,128,896]{2,1,0:T(8,128)(2,1)S(1)}, u32[]{:S(2)}, u32[]{:S(2)}) collective-permute-start(bf16[1,128,896]{2,1,0:T(8,128)(2,1)S(1)} %fusion.11), channel_id=1, source_target_pairs={{0,16},{16,0},{1,17},{17,1},{2,18},{18,2},{3,19},{19,3},{4,20},{20... | collective-permute-start | bytes 688136 | tf_op jit(solution)/shard_map/ppermute | solution.py:37
  124.7 4.0 %collective-permute-done.6 = bf16[1,128,896]{2,1,0:T(8,128)(2,1)S(1)} collective-permute-done((bf16[1,128,896]{2,1,0:T(8,128)(2,1)S(1)}, bf16[1,128,896]{2,1,0:T(8,128)(2,1)S(1)}, u32[]{:S(2)}, u32[]{:S(2)}) %collective-permute-start.6) | collective-permute-done | bytes 229408 | tf_op jit(solution)/shard_map/ppermute | solution.py:37
  (32 shorter events, 17.5 us)
Async XLA Ops:
  0.0 16.9 %collective-permute-start.2 = (bf16[8,64,256]{2,1,0:T(8,128)(2,1)}, bf16[8,64,256]{2,1,0:T(8,128)(2,1)S(1)}, u32[]{:S(2)}, u32[]{:S(2)}) collective-permute-start(bf16[8,64,256]{2,1,0:T(8,128)(2,1)} %bitcast.48), channel_id=1, source_target_pairs={{0,1},{1,2},{2,3},{3,4},{4,5},{5,6},{6,7},{7,8},{8,9},{9,10},{10,1... | collective-permute-start | bytes 786440 | tf_op jit(solution)/shard_map/ppermute | solution.py:21
  2.4 14.5 %collective-permute-start.3 = (bf16[8,64,256]{2,1,0:T(8,128)(2,1)}, bf16[8,64,256]{2,1,0:T(8,128)(2,1)S(1)}, u32[]{:S(2)}, u32[]{:S(2)}) collective-permute-start(bf16[8,64,256]{2,1,0:T(8,128)(2,1)} %bitcast.49), channel_id=1, source_target_pairs={{1,0},{2,1},{3,2},{4,3},{5,4},{6,5},{7,6},{8,7},{9,8},{10,9},{11,1... | collective-permute-start | bytes 786440 | tf_op jit(solution)/shard_map/ppermute | solution.py:23
  3.7 10.5 %collective-permute-start = (s32[8,4]{0,1:T(4,128)}, s32[8,4]{0,1:T(4,128)S(1)}, u32[]{:S(2)}, u32[]{:S(2)}) collective-permute-start(s32[8,4]{0,1:T(4,128)} %param.9), channel_id=1, source_target_pairs={{0,1},{1,2},{2,3},{3,4},{4,5},{5,6},{6,7},{7,8},{8,9},{9,10},{10,1... | collective-permute-start | bytes 392 | tf_op jit(solution)/shard_map/ppermute | solution.py:21
  8.9 5.4 %collective-permute-start.1 = (s32[8,4]{0,1:T(4,128)}, s32[8,4]{0,1:T(4,128)S(1)}, u32[]{:S(2)}, u32[]{:S(2)}) collective-permute-start(s32[8,4]{0,1:T(4,128)} %param.9), channel_id=1, source_target_pairs={{1,0},{2,1},{3,2},{4,3},{5,4},{6,5},{7,6},{8,7},{9,8},{10,9},{11,1... | collective-permute-start | bytes 392 | tf_op jit(solution)/shard_map/ppermute | solution.py:23
  96.8 6.2 %collective-permute-start.4 = (f32[128,640]{1,0:T(8,128)S(1)}, f32[128,640]{1,0:T(8,128)S(1)}, u32[]{:S(2)}, u32[]{:S(2)}) collective-permute-start(f32[128,640]{1,0:T(8,128)S(1)} %get-tuple-element.47), channel_id=1, source_target_pairs={{1,0},{2,1},{3,2},{4,3},{5,4},{6,5},{7,6},{8,7},{9,8},{10,9},{11,1... | collective-permute-start | bytes 983048 | tf_op jit(solution)/shard_map/ppermute | solution.py:33
  98.1 6.2 %collective-permute-start.5 = (f32[128,640]{1,0:T(8,128)S(1)}, f32[128,640]{1,0:T(8,128)S(1)}, u32[]{:S(2)}, u32[]{:S(2)}) collective-permute-start(f32[128,640]{1,0:T(8,128)S(1)} %get-tuple-element.46), channel_id=1, source_target_pairs={{0,1},{1,2},{2,3},{3,4},{4,5},{5,6},{6,7},{7,8},{8,9},{9,10},{10,1... | collective-permute-start | bytes 983048 | tf_op jit(solution)/shard_map/ppermute | solution.py:33
  104.3 24.5 %collective-permute-start.6 = (bf16[1,128,896]{2,1,0:T(8,128)(2,1)S(1)}, bf16[1,128,896]{2,1,0:T(8,128)(2,1)S(1)}, u32[]{:S(2)}, u32[]{:S(2)}) collective-permute-start(bf16[1,128,896]{2,1,0:T(8,128)(2,1)S(1)} %fusion.11), channel_id=1, source_target_pairs={{0,16},{16,0},{1,17},{17,1},{2,18},{18,2},{3,19},{19,3},{4,20},{20... | collective-permute-start | bytes 688136 | tf_op jit(solution)/shard_map/ppermute | solution.py:37
where the time goes:
time: 131 us; the launch traced here: 130 us
  matrix products  37.3 us (28%)
  starting transfers between devices  36.8 us (28%)
  local copies, waits for them, and re-layouts  36.7 us (28%)
  other arithmetic  13.2 us (10%)
  waiting for transfers between devices  5.22 us (4%)
    reshape x8, local copies, waits for them, and re-layouts, product_row(): panel = spread.reshape(KA * B, 5 * NC * B)  20.9 us
    ppermute x1, starting transfers between devices, partner_2(): lax.ppermute(x, axis, [(i, i ^ 1 << bit) for i in range(lax.axis_size(axi...  20.5 us
    dot_general x8, matrix products, product_row(): jnp.einsum('kslt,klj->ksjt', p_row, hot_row, preferred_element_type=jnp.f...  17.6 us
    dot_general x8, matrix products, product_row(): jnp.dot(a_row, panel, preferred_element_type=jnp.float32)  17.5 us
    gather x2, local copies, waits for them, and re-layouts, local(): picked = jnp.take(p_near, local_cols, axis=0).reshape(RB, KA, B, KP, B)  12.8 us
    select_n x1, other arithmetic, local(): picked = jnp.take(p_near, local_cols, axis=0).reshape(RB, KA, B, KP, B)  8.33 us
    ppermute x2, starting transfers between devices, with_halo(): lax.ppermute(tail, axis, [(i, (i + 1) % count) for i in range(ends)])  7.55 us
    ppermute x2, starting transfers between devices, shifted(): return lax.ppermute(x, axis, pairs)  6.22 us
  transfers between devices with their start and end apart: 7, of which 2 were waited for; matrix products, arithmetic and copies ran while one was open for 5% of the time, Pallas kernels for 0%

commit v1 on v0

v1 whole, which is shorter than its diff:
```python
import jax
import jax.numpy as jnp
from jax import lax
from jax.sharding import PartitionSpec as P

B = 64
KA = 12
KP = 4
NC = 2
RB = 8
LINE = ("grp", "dev")
WIDEN = False


def mm(spec, x, y):
    if WIDEN:
        x, y = x.astype(jnp.float32), y.astype(jnp.float32)
    return jnp.einsum(spec, x, y, preferred_element_type=jnp.float32)


def shifted(x, axis, by):
    peers = lax.axis_size(axis)
    pairs = [(i, i + by) for i in range(peers) if 0 <= i + by < peers]
    return lax.ppermute(x, axis, pairs)


def partner_2(x, axis, bit):
    return lax.ppermute(x, axis, [(i, i ^ 1 << bit) for i in range(lax.axis_size(axis))])


def spread(blocks, cols, width):
    slots = jnp.arange(width, dtype=jnp.int32)[None, None, :, None]
    out = jnp.zeros(blocks.shape[:2] + (width, B), blocks.dtype)
    for l in range(KP):
        hit = cols[:, l][:, None, None, None] == slots
        out = jnp.where(hit, blocks[:, :, l : l + 1, :], out)
    return out


def local(a_blocks, a_cols, p_blocks, p_cols):
    q = lax.axis_index(LINE)
    rel = (p_cols - (q - 1) * NC).astype(jnp.bfloat16)
    tag = jnp.zeros((16, KP * B), jnp.bfloat16).at[:RB, :KP].set(rel)
    payload = jnp.concatenate([p_blocks, tag], axis=0)
    from_left = shifted(payload, LINE, 1)
    from_right = shifted(payload, LINE, -1)

    def rows(x):
        return x[: RB * B].reshape(RB, B, KP, B)

    def cols(x, shift):
        return x[RB * B : RB * B + RB, :KP].astype(jnp.int32) + shift

    p_near = jnp.concatenate([rows(from_left), rows(payload), rows(from_right)], axis=0)
    pc_near = jnp.concatenate([cols(from_left, 0), cols(payload, NC), cols(from_right, 2 * NC)], axis=0)
    ps = spread(p_near, pc_near, 5 * NC).reshape(3 * RB * B, 5 * NC * B)

    local_cols = a_cols - (q - 1) * RB
    hot = (local_cols[:, :, None] == jnp.arange(3 * RB, dtype=jnp.int32)).astype(jnp.bfloat16)
    a4 = a_blocks.reshape(RB, B, KA, B)
    dense = mm("iskt,ikr->isrt", a4, hot)
    dense = dense.reshape(RB * B, 3 * RB * B)
    hi = dense.astype(jnp.bfloat16)
    lo = (dense - hi.astype(jnp.float32)).astype(jnp.bfloat16)
    ap = mm("ar,rc->ac", hi, ps) + mm("ar,rc->ac", lo, ps)
    ap = ap.astype(jnp.bfloat16)

    own = p_blocks.reshape(RB, B, KP, B)
    scattered = spread(own, p_cols - (q - 1) * NC, 3 * NC).reshape(RB * B, 3 * NC * B)
    partial_value = mm("ro,rc->oc", scattered, ap)
    partial_value = partial_value.reshape(3, NC * B, 5 * NC * B)
    from_right_p = shifted(partial_value[0], LINE, -1)
    from_left_p = shifted(partial_value[2], LINE, 1)
    span = NC * B
    combined = jnp.pad(partial_value[1], ((0, 0), (span, span)))
    combined = combined + jnp.pad(from_right_p, ((0, 0), (2 * span, 0)))
    combined = combined + jnp.pad(from_left_p, ((0, 0), (0, 2 * span)))
    rows_here = combined.astype(jnp.bfloat16)[None]
    group = lax.axis_index("grp")
    joined = rows_here
    for section_bit in range(lax.axis_size("grp").bit_length() - 1):
        partner = partner_2(joined, "grp", section_bit)
        is_upper = group // 2**section_bit % 2 == 1
        joined = jnp.where(
            is_upper,
            jnp.concatenate([partner, joined], axis=0),
            jnp.concatenate([joined, partner], axis=0),
        )
    return joined


def solution(mesh):
    placed = (P(LINE, None),) * 4
    return jax.shard_map(
        local, mesh=mesh, in_specs=placed, out_specs=P(None, "dev", None), check_vma=False
    )
```

time: 131 us -> 74.3 us (0.57)
  matrix products: 37.3 us -> 12.6 us
  starting transfers between devices: 36.8 us -> 22.3 us
  local copies, waits for them, and re-layouts: 36.7 us -> 24.5 us
  other arithmetic: 13.2 us -> 7.54 us
    dot_general x18 -> x3, matrix products: 37.3 us -> 12.6 us  [mm(): return jnp.einsum(spec, x, y, preferred_element_type=jnp.float32)]
    reshape x9 -> x4, local copies, waits for them, and re-layouts: 21.5 us -> 3.02 us  [the longest x1 2.21 us: local(): a4 = a_blocks.reshape(RB, B, KA, B)]
    gather x5 -> x0, local copies, waits for them, and re-layouts: 13.5 us -> none  [the longest x2 12.8 us: local(): picked = jnp.take(p_near, local_cols, axis=0).reshape(RB, KA, B, KP, B)]
    ppermute x4 -> x0, starting transfers between devices: 10.1 us -> none  [the longest x2 7.55 us: with_halo(): lax.ppermute(tail, axis, [(i, (i + 1) % count) for i in range(ends)])]
    convert_element_type x0 -> x2, local copies, waits for them, and re-layouts: none -> 8.28 us  [the longest x1 5.32 us: local(): lo = (dense - hi.astype(jnp.float32)).astype(jnp.bfloat16)]
    ppermute x1, starting transfers between devices: 20.5 us -> 12.2 us  [partner_2(): lax.ppermute(x, axis, [(i, i ^ 1 << bit) for i in range(lax.axis_size(axi...]
    select_n x0 -> x2, local copies, waits for them, and re-layouts: none -> 7.5 us  [spread(): out = jnp.where(hit, blocks[:, :, l:l + 1, :], out)]
    select_n x1 -> x2, other arithmetic: 8.33 us -> 3.77 us  [spread(): out = jnp.where(hit, blocks[:, :, l:l + 1, :], out)]
  transfers between devices with their start and end apart: 7 -> 5, of which waited for: 2 -> 2; matrix products, arithmetic and copies ran while one was open for 5% -> 29% of each run, Pallas kernels for 0% -> 0%
where the time goes in v1:
time: 74.3 us; the launch traced here: 73.7 us
  local copies, waits for them, and re-layouts  24.5 us (33%)
  starting transfers between devices  22.3 us (30%)
  matrix products  12.6 us (17%)
  other arithmetic  7.54 us (10%)
  waiting for transfers between devices  6.45 us (9%)
    dot_general x3, matrix products, mm(): return jnp.einsum(spec, x, y, preferred_element_type=jnp.float32)  12.6 us
    ppermute x1, starting transfers between devices, partner_2(): lax.ppermute(x, axis, [(i, i ^ 1 << bit) for i in range(lax.axis_size(axi...  12.2 us
    ppermute x4, starting transfers between devices, shifted(): return lax.ppermute(x, axis, pairs)  10.2 us
    select_n x2, local copies, waits for them, and re-layouts, spread(): out = jnp.where(hit, blocks[:, :, l:l + 1, :], out)  7.5 us
    convert_element_type x1, local copies, waits for them, and re-layouts, local(): lo = (dense - hi.astype(jnp.float32)).astype(jnp.bfloat16)  5.32 us
    ppermute x1, waiting for transfers between devices, partner_2(): lax.ppermute(x, axis, [(i, i ^ 1 << bit) for i in range(lax.axis_size(axi...  4.23 us
    select_n x2, other arithmetic, spread(): out = jnp.where(hit, blocks[:, :, l:l + 1, :], out)  3.77 us
    convert_element_type x1, local copies, waits for them, and re-layouts, local(): hi = dense.astype(jnp.bfloat16)  2.97 us
  transfers between devices with their start and end apart: 5, of which 2 were waited for; matrix products, arithmetic and copies ran while one was open for 29% of the time, Pallas kernels for 0%

profile of v1, /device:TPU:0, one launch (start us, length us, event | category | flops | bytes accessed | tf_op | source)
XLA Modules:
  0.0 73.7 jit_solution(12198755453274781423)
XLA Ops:
  0.0 1.2 %copy.22 = bf16[512,256]{0,1:T(8,128)(2,1)S(1)} copy(bf16[512,256]{1,0:T(8,128)(2,1)} %param.8) | data formatting | bytes 524288 | tf_op args[2]
  1.2 0.7 convert_add_fusion.1
  1.9 0.8 %fusion.4 = bf16[528,256]{0,1:T(8,128)(2,1)} fusion(bf16[8,4]{0,1:T(4,128)(2,1)S(1)} %get-tuple-element.20, bf16[512,256]{0,1:T(8,128)(2,1)S(1)} %copy.22), kind=kLoop, calls=%fused_computation.16 | loop fusion | flops 811008 | bytes 532544 | tf_op jit(solution)/shard_map/concatenate | solution.py:44
  2.6 1.3 %collective-permute-start.1 = (bf16[528,256]{0,1:T(8,128)(2,1)}, bf16[528,256]{0,1:T(8,128)(2,1)}, u32[]{:S(2)}, u32[]{:S(2)}) collective-permute-start(bf16[528,256]{0,1:T(8,128)(2,1)} %fusion.4), channel_id=1, source_target_pairs={{1,0},{2,1},{3,2},{4,3},{5,4},{6,5},{7,6},{8,7},{9,8},{10,9},{11,1... | collective-permute-start | bytes 811016 | tf_op jit(solution)/shard_map/ppermute | solution.py:24
  3.9 3.8 %collective-permute-start = (bf16[528,256]{0,1:T(8,128)(2,1)}, bf16[528,256]{0,1:T(8,128)(2,1)}, u32[]{:S(2)}, u32[]{:S(2)}) collective-permute-start(bf16[528,256]{0,1:T(8,128)(2,1)} %fusion.4), channel_id=1, source_target_pairs={{0,1},{1,2},{2,3},{3,4},{4,5},{5,6},{6,7},{7,8},{8,9},{9,10},{10,1... | collective-permute-start | bytes 811016 | tf_op jit(solution)/shard_map/ppermute | solution.py:24
  7.7 0.3 reshape.314
  8.0 0.7 slice_bitcast_fusion.7
  8.7 2.2 %reshape.319 = bf16[8,64,12,64]{3,2,1,0:T(8,128)(2,1)} reshape(bf16[512,768]{1,0:T(8,128)(2,1)S(1)} %copy-done.3) | data formatting | bytes 1572864 | tf_op jit(solution)/shard_map/reshape | solution.py:60
  11.0 4.4 %fusion = (bf16[8,64,24,64]{3,2,1,0:T(8,128)(2,1)}, bf16[8,64,24,64]{3,2,1,0:T(8,128)(2,1)S(1)}) fusion(bf16[8,64,12,64]{3,2,1,0:T(8,128)(2,1)} %reshape.319, s32[8,12]{1,0:T(8,128)S(1)} %broadcast_subtract_fusion), kind=kOutput, calls=%fused_computation.2 | convolution fusion | flops 22022400 | bytes 3932544 | tf_op jit(solution)/shard_map/iskt,ikr->isrt/dot_general | solution.py:18
  15.4 1.1 %select_select_fusion.1 = bf16[8,64,6,64]{1,0,3,2:T(8,128)(2,1)} fusion(pred[8,6]{0,1:T(8,128)(4,1)S(1)} %get-tuple-element.41, pred[8,6]{0,1:T(8,128)(4,1)S(1)} %get-tuple-element.42, pred[8,6]{0,1:T(8,128)(4,1)S(1)} %get-tuple-element.43, pred[8,6]{0,1:T(8,128)(4,1)S(1)} %get-tuple-element.44, bf16[8,64,64]{1,0,2:T(8,128)(2,1)S(1)} %get-tuple-element.30, ...), kind=kLoop, calls=%fused_computation.7 | loop fusion | flops 786432 | bytes 655552 | tf_op jit(solution)/shard_map/jit(_where)/select_n | solution.py:36
  16.6 2.4 %select_n.109 = bf16[512,384]{0,1:T(8,128)(2,1)} reshape(bf16[8,64,6,64]{1,0,3,2:T(8,128)(2,1)} %select_select_fusion.1) | data formatting | bytes 786432 | tf_op jit(solution)/shard_map/jit(_where)/select_n | solution.py:36
  18.9 5.3 %convert_element_type.50 = bf16[512,1536]{1,0:T(8,128)(2,1)} reshape(bf16[8,64,24,64]{3,2,1,0:T(8,128)(2,1)} %get-tuple-element.17) | data formatting | bytes 3145728 | tf_op jit(solution)/shard_map/convert_element_type | solution.py:64
  24.2 3.0 %convert_element_type.43 = bf16[512,1536]{1,0:T(8,128)(2,1)} reshape(bf16[8,64,24,64]{3,2,1,0:T(8,128)(2,1)S(1)} %get-tuple-element.18) | data formatting | bytes 3145728 | tf_op jit(solution)/shard_map/convert_element_type | solution.py:63
  27.2 1.0 %slice.123 = bf16[512,256]{0,1:T(8,128)(2,1)S(1)} slice(bf16[528,256]{0,1:T(8,128)(2,1)} %collective-permute-done.1), slice={[0:512], [0:256]} | slice | bytes 524288 | tf_op jit(solution)/shard_map/slice | solution.py:49
  28.2 0.3 reshape.317
  28.5 0.6 convert_add_fusion
  29.2 0.7 slice_convert_fusion
  29.9 1.0 %slice.122 = bf16[512,256]{0,1:T(8,128)(2,1)S(1)} slice(bf16[528,256]{0,1:T(8,128)(2,1)} %collective-permute-done), slice={[0:512], [0:256]} | slice | bytes 524288 | tf_op jit(solution)/shard_map/slice | solution.py:49
  30.9 0.3 reshape.316
  31.4 0.1 constant_dynamic-update-slice_fusion
  31.6 0.3 slice_bitcast_fusion.3
  31.9 2.6 %select_select_fusion = bf16[24,64,10,64]{1,0,3,2:T(8,128)(2,1)} fusion(pred[24,10]{0,1:T(8,128)(4,1)S(1)} %get-tuple-element.45, pred[24,10]{0,1:T(8,128)(4,1)S(1)} %get-tuple-element.46, pred[24,10]{0,1:T(8,128)(4,1)S(1)} %get-tuple-element.47, pred[24,10]{0,1:T(8,128)(4,1)S(1)} %get-tuple-element.48, bf16[24,64,64]{1,0,2:T(8,128)(2,1)S(1)} %get-tuple-element.23, ...), kind=kLoop, calls=%fused_computation.3 | loop fusion | flops 3932160 | bytes 2753472 | tf_op jit(solution)/shard_map/jit(_where)/select_n | solution.py:36
  34.5 5.1 %select_n.114 = bf16[1536,640]{0,1:T(8,128)(2,1)S(1)} reshape(bf16[24,64,10,64]{1,0,3,2:T(8,128)(2,1)} %select_select_fusion) | data formatting | bytes 3932160 | tf_op jit(solution)/shard_map/jit(_where)/select_n | solution.py:36
  39.7 4.0 %fusion.11 = f32[512,640]{1,0:T(8,128)} fusion(bf16[512,1536]{1,0:T(8,128)(2,1)} %convert_element_type.43, bf16[1536,640]{0,1:T(8,128)(2,1)S(1)} %select_n.114), kind=kOutput, calls=%fused_computation.52 | convolution fusion | flops 1006632960 | bytes 4849664 | tf_op jit(solution)/shard_map/ar,rc->ac/dot_general | solution.py:18
  43.7 4.2 %fusion.2 = f32[384,640]{1,0:T(8,128)} fusion(bf16[512,384]{0,1:T(8,128)(2,1)} %select_n.109, f32[512,640]{1,0:T(8,128)} %fusion.11, bf16[512,1536]{1,0:T(8,128)(2,1)S(1)} %copy-done.2, bf16[1536,640]{0,1:T(8,128)(2,1)S(1)} %select_n.114), kind=kOutput, calls=%fused_computation.6 | convolution fusion | flops 1258946560 | bytes 6225920 | tf_op jit(solution)/shard_map/ro,rc->oc/dot_general | solution.py:18
  47.9 1.2 %fusion.10 = (f32[128,640]{1,0:T(8,128)S(1)}, f32[128,640]{1,0:T(8,128)S(1)}, f32[128,640]{1,0:T(8,128)S(1)}) fusion(f32[384,640]{1,0:T(8,128)} %fusion.2), kind=kLoop, calls=%fused_computation.51 | loop fusion | bytes 1966080 | tf_op jit(solution)/shard_map/slice | solution.py:75
  49.1 3.8 %collective-permute-start.3 = (f32[128,640]{1,0:T(8,128)S(1)}, f32[128,640]{1,0:T(8,128)S(1)}, u32[]{:S(2)}, u32[]{:S(2)}) collective-permute-start(f32[128,640]{1,0:T(8,128)S(1)} %get-tuple-element.27), channel_id=1, source_target_pairs={{0,1},{1,2},{2,3},{3,4},{4,5},{5,6},{6,7},{7,8},{8,9},{9,10},{10,1... | collective-permute-start | bytes 983048 | tf_op jit(solution)/shard_map/ppermute | solution.py:24
  52.9 1.3 %collective-permute-start.2 = (f32[128,640]{1,0:T(8,128)S(1)}, f32[128,640]{1,0:T(8,128)S(1)}, u32[]{:S(2)}, u32[]{:S(2)}) collective-permute-start(f32[128,640]{1,0:T(8,128)S(1)} %get-tuple-element.28), channel_id=1, source_target_pairs={{1,0},{2,1},{3,2},{4,3},{5,4},{6,5},{7,6},{8,7},{9,8},{10,9},{11,1... | collective-permute-start | bytes 983048 | tf_op jit(solution)/shard_map/ppermute | solution.py:24
  54.2 2.2 %collective-permute-done.2 = f32[128,640]{1,0:T(8,128)S(1)} collective-permute-done((f32[128,640]{1,0:T(8,128)S(1)}, f32[128,640]{1,0:T(8,128)S(1)}, u32[]{:S(2)}, u32[]{:S(2)}) %collective-permute-start.2) | collective-permute-done | bytes 327712 | tf_op jit(solution)/shard_map/ppermute | solution.py:24
  56.5 12.2 %collective-permute-start.4 = (bf16[1,128,896]{2,1,0:T(8,128)(2,1)S(1)}, bf16[1,128,896]{2,1,0:T(8,128)(2,1)S(1)}, u32[]{:S(2)}, u32[]{:S(2)}) collective-permute-start(bf16[1,128,896]{2,1,0:T(8,128)(2,1)S(1)} %fusion.5), channel_id=1, source_target_pairs={{0,16},{16,0},{1,17},{17,1},{2,18},{18,2},{3,19},{19,3},{4,20},{20... | collective-permute-start | bytes 688136 | tf_op jit(solution)/shard_map/ppermute | solution.py:28
  68.7 4.2 %collective-permute-done.4 = bf16[1,128,896]{2,1,0:T(8,128)(2,1)S(1)} collective-permute-done((bf16[1,128,896]{2,1,0:T(8,128)(2,1)S(1)}, bf16[1,128,896]{2,1,0:T(8,128)(2,1)S(1)}, u32[]{:S(2)}, u32[]{:S(2)}) %collective-permute-start.4) | collective-permute-done | bytes 229408 | tf_op jit(solution)/shard_map/ppermute | solution.py:28
  72.9 0.8 %maximum_select_fusion = bf16[2,128,896]{2,1,0:T(8,128)(2,1)} fusion(bf16[1,128,896]{2,1,0:T(8,128)(2,1)S(1)} %fusion.5, bf16[1,128,896]{2,1,0:T(8,128)(2,1)S(1)} %collective-permute-done.4, pred[]{:T(512)S(6)} %eq.178), kind=kLoop, calls=%fused_computation.10 | loop fusion | flops 688128 | bytes 917505 | tf_op jit(solution)/shard_map/jit(_where)/select_n | solution.py:84
  (26 shorter events, 0.4 us)
Async XLA Ops:
  0.0 8.7 %copy-start.3 = (bf16[512,768]{1,0:T(8,128)(2,1)S(1)}, bf16[512,768]{1,0:T(8,128)(2,1)}, u32[]{:S(2)}) copy-start(bf16[512,768]{1,0:T(8,128)(2,1)} %param.6) | copy-start | bytes 2359300
  2.6 24.6 %collective-permute-start.1 = (bf16[528,256]{0,1:T(8,128)(2,1)}, bf16[528,256]{0,1:T(8,128)(2,1)}, u32[]{:S(2)}, u32[]{:S(2)}) collective-permute-start(bf16[528,256]{0,1:T(8,128)(2,1)} %fusion.4), channel_id=1, source_target_pairs={{1,0},{2,1},{3,2},{4,3},{5,4},{6,5},{7,6},{8,7},{9,8},{10,9},{11,1... | collective-permute-start | bytes 811016 | tf_op jit(solution)/shard_map/ppermute | solution.py:24
  3.9 25.2 %collective-permute-start = (bf16[528,256]{0,1:T(8,128)(2,1)}, bf16[528,256]{0,1:T(8,128)(2,1)}, u32[]{:S(2)}, u32[]{:S(2)}) collective-permute-start(bf16[528,256]{0,1:T(8,128)(2,1)} %fusion.4), channel_id=1, source_target_pairs={{0,1},{1,2},{2,3},{3,4},{4,5},{5,6},{6,7},{7,8},{8,9},{9,10},{10,1... | collective-permute-start | bytes 811016 | tf_op jit(solution)/shard_map/ppermute | solution.py:24
  8.0 2.9 %copy-start = (bf16[8,64,4,64]{1,0,3,2:T(8,128)(2,1)}, bf16[8,64,4,64]{1,0,3,2:T(8,128)(2,1)S(1)}, u32[]{:S(2)}) copy-start(bf16[8,64,4,64]{1,0,3,2:T(8,128)(2,1)S(1)} %reshape.314) | copy-start | bytes 786436
  8.0 2.9 %copy-start.5 = (s32[8,12]{1,0:T(8,128)S(1)}, s32[8,12]{1,0:T(8,128)}, u32[]{:S(2)}) copy-start(s32[8,12]{1,0:T(8,128)} %param.7) | copy-start | bytes 1156
  11.0 4.5 %copy-start.4 = (bf16[8,64,64]{1,0,2:T(8,128)(2,1)S(1)}, bf16[8,64,64]{1,0,2:T(8,128)(2,1)}, u32[]{:S(2)}) copy-start(bf16[8,64,64]{1,0,2:T(8,128)(2,1)} %get-tuple-element.32) | copy-start | bytes 196612
  27.2 4.1 %copy-start.1 = (bf16[8,64,4,64]{1,0,3,2:T(8,128)(2,1)S(1)}, bf16[8,64,4,64]{1,0,3,2:T(8,128)(2,1)}, u32[]{:S(2)}) copy-start(bf16[8,64,4,64]{1,0,3,2:T(8,128)(2,1)} %copy-done) | copy-start | bytes 786436
  39.7 4.0 %copy-start.2 = (bf16[512,1536]{1,0:T(8,128)(2,1)S(1)}, bf16[512,1536]{1,0:T(8,128)(2,1)}, u32[]{:S(2)}) copy-start(bf16[512,1536]{1,0:T(8,128)(2,1)} %convert_element_type.50) | copy-start | bytes 4718596
  49.1 5.1 %collective-permute-start.3 = (f32[128,640]{1,0:T(8,128)S(1)}, f32[128,640]{1,0:T(8,128)S(1)}, u32[]{:S(2)}, u32[]{:S(2)}) collective-permute-start(f32[128,640]{1,0:T(8,128)S(1)} %get-tuple-element.27), channel_id=1, source_target_pairs={{0,1},{1,2},{2,3},{3,4},{4,5},{5,6},{6,7},{7,8},{8,9},{9,10},{10,1... | collective-permute-start | bytes 983048 | tf_op jit(solution)/shard_map/ppermute | solution.py:24
  52.9 3.5 %collective-permute-start.2 = (f32[128,640]{1,0:T(8,128)S(1)}, f32[128,640]{1,0:T(8,128)S(1)}, u32[]{:S(2)}, u32[]{:S(2)}) collective-permute-start(f32[128,640]{1,0:T(8,128)S(1)} %get-tuple-element.28), channel_id=1, source_target_pairs={{1,0},{2,1},{3,2},{4,3},{5,4},{6,5},{7,6},{8,7},{9,8},{10,9},{11,1... | collective-permute-start | bytes 983048 | tf_op jit(solution)/shard_map/ppermute | solution.py:24
  56.5 16.4 %collective-permute-start.4 = (bf16[1,128,896]{2,1,0:T(8,128)(2,1)S(1)}, bf16[1,128,896]{2,1,0:T(8,128)(2,1)S(1)}, u32[]{:S(2)}, u32[]{:S(2)}) collective-permute-start(bf16[1,128,896]{2,1,0:T(8,128)(2,1)S(1)} %fusion.5), channel_id=1, source_target_pairs={{0,16},{16,0},{1,17},{17,1},{2,18},{18,2},{3,19},{19,3},{4,20},{20... | collective-permute-start | bytes 688136 | tf_op jit(solution)/shard_map/ppermute | solution.py:28

commit v2 on v1

--- a/solution.py
+++ b/solution.py
@@ -28,13 +28,15 @@
     return lax.ppermute(x, axis, [(i, i ^ 1 << bit) for i in range(lax.axis_size(axis))])
 
 
-def spread(blocks, cols, width):
-    slots = jnp.arange(width, dtype=jnp.int32)[None, None, :, None]
-    out = jnp.zeros(blocks.shape[:2] + (width, B), blocks.dtype)
-    for l in range(KP):
-        hit = cols[:, l][:, None, None, None] == slots
-        out = jnp.where(hit, blocks[:, :, l : l + 1, :], out)
-    return out
+def spread2d(flat, cols, width):
+    per_row = jnp.repeat(cols, B, axis=0)
+    pieces = []
+    for j in range(width):
+        piece = jnp.zeros((flat.shape[0], B), flat.dtype)
+        for l in range(KP):
+            piece = jnp.where(per_row[:, l : l + 1] == j, flat[:, l * B : (l + 1) * B], piece)
+        pieces.append(piece)
+    return jnp.concatenate(pieces, axis=1)
 
 
 def local(a_blocks, a_cols, p_blocks, p_cols):
@@ -45,28 +47,29 @@
     from_left = shifted(payload, LINE, 1)
     from_right = shifted(payload, LINE, -1)
 
-    def rows(x):
-        return x[: RB * B].reshape(RB, B, KP, B)
-
     def cols(x, shift):
         return x[RB * B : RB * B + RB, :KP].astype(jnp.int32) + shift
 
-    p_near = jnp.concatenate([rows(from_left), rows(payload), rows(from_right)], axis=0)
-    pc_near = jnp.concatenate([cols(from_left, 0), cols(payload, NC), cols(from_right, 2 * NC)], axis=0)
-    ps = spread(p_near, pc_near, 5 * NC).reshape(3 * RB * B, 5 * NC * B)
+    p_near = jnp.concatenate([from_left[: RB * B], p_blocks, from_right[: RB * B]], axis=0)
+    pc_near = jnp.concatenate([cols(from_left, 0), p_cols - (q - 2) * NC, cols(from_right, 2 * NC)], axis=0)
+    ps = spread2d(p_near, pc_near, 5 * NC)
 
-    local_cols = a_cols - (q - 1) * RB
-    hot = (local_cols[:, :, None] == jnp.arange(3 * RB, dtype=jnp.int32)).astype(jnp.bfloat16)
-    a4 = a_blocks.reshape(RB, B, KA, B)
-    dense = mm("iskt,ikr->isrt", a4, hot)
-    dense = dense.reshape(RB * B, 3 * RB * B)
+    local_cols = jnp.repeat(a_cols - (q - 1) * RB, B, axis=0)
+    dense = []
+    for r in range(3 * RB):
+        block = jnp.zeros((RB * B, B), jnp.float32)
+        for k in range(KA):
+            block = block + jnp.where(
+                local_cols[:, k : k + 1] == r, a_blocks[:, k * B : (k + 1) * B].astype(jnp.float32), 0.0
+            )
+        dense.append(block)
+    dense = jnp.concatenate(dense, axis=1)
     hi = dense.astype(jnp.bfloat16)
     lo = (dense - hi.astype(jnp.float32)).astype(jnp.bfloat16)
     ap = mm("ar,rc->ac", hi, ps) + mm("ar,rc->ac", lo, ps)
     ap = ap.astype(jnp.bfloat16)
 
-    own = p_blocks.reshape(RB, B, KP, B)
-    scattered = spread(own, p_cols - (q - 1) * NC, 3 * NC).reshape(RB * B, 3 * NC * B)
+    scattered = spread2d(p_blocks, p_cols - (q - 1) * NC, 3 * NC)
     partial_value = mm("ro,rc->oc", scattered, ap)
     partial_value = partial_value.reshape(3, NC * B, 5 * NC * B)
     from_right_p = shifted(partial_value[0], LINE, -1)

time: 74.3 us -> 121 us (1.63)
  other arithmetic: 7.54 us -> 66.6 us
  local copies, waits for them, and re-layouts: 24.5 us -> 12.1 us
  starting transfers between devices: 22.3 us -> 28.9 us
  matrix products: 12.6 us -> 7.38 us
  waiting for transfers between devices: 6.45 us -> 5.22 us
    add x0 -> x24, other arithmetic: none -> 54.1 us  [local(): block + jnp.where(local_cols[:, k:k + 1] == r, a_blocks[:, k * B:(k + 1)...]
    convert_element_type x2 -> x0, local copies, waits for them, and re-layouts: 8.28 us -> none  [the longest x1 5.32 us: local(): lo = (dense - hi.astype(jnp.float32)).astype(jnp.bfloat16)]
    select_n x2 -> x0, local copies, waits for them, and re-layouts: 7.5 us -> none  [spread(): out = jnp.where(hit, blocks[:, :, l:l + 1, :], out)]
    ppermute x1, starting transfers between devices: 12.2 us -> 18.1 us  [partner_2(): lax.ppermute(x, axis, [(i, i ^ 1 << bit) for i in range(lax.axis_size(axi...]
    concatenate x1 -> x2, local copies, waits for them, and re-layouts: 0.13 us -> 5.92 us  [the longest x1 4.87 us: local(): dense = jnp.concatenate(dense, axis=1)]
    dot_general x3 -> x2, matrix products: 12.6 us -> 7.38 us  [mm(): return jnp.einsum(spec, x, y, preferred_element_type=jnp.float32)]
    eq x4, other arithmetic: 0.03 us -> 3.06 us  [the longest x2 2.17 us: local(): local_cols[:, k:k + 1] == r]
    reshape x4 -> x3, local copies, waits for them, and re-layouts: 3.02 us -> 0.25 us  [the longest x2 0.17 us: spread2d(): per_row = jnp.repeat(cols, B, axis=0)]
  transfers between devices with their start and end apart: 5 -> 5, of which waited for: 2 -> 2; matrix products, arithmetic and copies ran while one was open for 29% -> 56% of each run, Pallas kernels for 0% -> 0%
where the time goes in v2:
time: 121 us; the launch traced here: 120 us
  other arithmetic  66.6 us (55%)
  starting transfers between devices  28.9 us (24%)
  local copies, waits for them, and re-layouts  12.1 us (10%)
  matrix products  7.38 us (6%)
  waiting for transfers between devices  5.22 us (4%)
    add x24, other arithmetic, local(): block + jnp.where(local_cols[:, k:k + 1] == r, a_blocks[:, k * B:(k + 1)...  54.1 us
    ppermute x1, starting transfers between devices, partner_2(): lax.ppermute(x, axis, [(i, i ^ 1 << bit) for i in range(lax.axis_size(axi...  18.1 us
    ppermute x4, starting transfers between devices, shifted(): return lax.ppermute(x, axis, pairs)  10.8 us
    dot_general x2, matrix products, mm(): return jnp.einsum(spec, x, y, preferred_element_type=jnp.float32)  7.38 us
    concatenate x1, local copies, waits for them, and re-layouts, local(): dense = jnp.concatenate(dense, axis=1)  4.87 us
    ppermute x1, waiting for transfers between devices, partner_2(): lax.ppermute(x, axis, [(i, i ^ 1 << bit) for i in range(lax.axis_size(axi...  4 us
    select_n x3, other arithmetic, spread2d(): jnp.where(per_row[:, l:l + 1] == j, flat[:, l * B:(l + 1) * B], piece)  3.56 us
    unnamed x7, local copies, waits for them, and re-layouts  2.44 us
  transfers between devices with their start and end apart: 5, of which 2 were waited for; matrix products, arithmetic and copies ran while one was open for 56% of the time, Pallas kernels for 0%

profile of v2, /device:TPU:0, one launch (start us, length us, event | category | flops | bytes accessed | tf_op | source)
XLA Modules:
  0.0 120.4 jit_solution(16117200619985705115)
XLA Ops:
  3.9 3.8 %collective-permute-start = (bf16[528,256]{0,1:T(8,128)(2,1)}, bf16[528,256]{0,1:T(8,128)(2,1)}, u32[]{:S(2)}, u32[]{:S(2)}) collective-permute-start(bf16[528,256]{0,1:T(8,128)(2,1)} %fusion.9), channel_id=1, source_target_pairs={{0,1},{1,2},{2,3},{3,4},{4,5},{5,6},{6,7},{7,8},{8,9},{9,10},{10,1... | collective-permute-start | bytes 811016 | tf_op jit(solution)/shard_map/ppermute | solution.py:24
  11.1 1.9 %select_select_fusion = (bf16[512,64]{1,0:T(8,128)(2,1)S(1)}, bf16[512,64]{1,0:T(8,128)(2,1)S(1)}) fusion(pred[512]{0:T(512)(128)(4,1)S(1)} %get-tuple-element.660, pred[512]{0:T(512)(128)(4,1)S(1)} %get-tuple-element.359, pred[512]{0:T(512)(128)(4,1)S(1)} %get-tuple-element.354, pred[512]{0:T(512)(128)(4,1)S(1)} %get-tuple-element.345, ...), kind=kLoop, calls=%fused_computation.577 | loop fusion | flops 262144 | bytes 397312 | tf_op jit(solution)/shard_map/jit(_where)/select_n | solution.py:37
  13.1 2.3 %fusion.229 = f32[512,64]{1,0:T(8,128)} fusion(pred[512]{0:T(512)(128)(4,1)S(1)} %get-tuple-element.433, pred[512]{0:T(512)(128)(4,1)S(1)} %get-tuple-element.545, pred[512]{0:T(512)(128)(4,1)S(1)} %get-tuple-element.568, pred[512]{0:T(512)(128)(4,1)S(1)} %get-tuple-element.534, pred[512]{0:T(512)(128)(4,1)S(1)} %get-tuple-element.487, ...), kind=kLoop, calls=%fused_computation.521 | loop fusion | flops 1146880 | bytes 923648 | tf_op jit(solution)/shard_map/add | solution.py:62
  15.3 2.3 %fusion.240 = f32[512,64]{1,0:T(8,128)} fusion(pred[512]{0:T(512)(128)(4,1)S(1)} %get-tuple-element.432, pred[512]{0:T(512)(128)(4,1)S(1)} %get-tuple-element.544, pred[512]{0:T(512)(128)(4,1)S(1)} %get-tuple-element.567, pred[512]{0:T(512)(128)(4,1)S(1)} %get-tuple-element.533, pred[512]{0:T(512)(128)(4,1)S(1)} %get-tuple-element.486, ...), kind=kLoop, calls=%fused_computation.532 | loop fusion | flops 1146880 | bytes 923648 | tf_op jit(solution)/shard_map/add | solution.py:62
  17.6 2.2 %fusion.251 = f32[512,64]{1,0:T(8,128)} fusion(pred[512]{0:T(512)(128)(4,1)S(1)} %get-tuple-element.430, pred[512]{0:T(512)(128)(4,1)S(1)} %get-tuple-element.543, pred[512]{0:T(512)(128)(4,1)S(1)} %get-tuple-element.566, pred[512]{0:T(512)(128)(4,1)S(1)} %get-tuple-element.532, pred[512]{0:T(512)(128)(4,1)S(1)} %get-tuple-element.485, ...), kind=kLoop, calls=%fused_computation.543 | loop fusion | flops 1146880 | bytes 923648 | tf_op jit(solution)/shard_map/add | solution.py:62
  19.8 2.2 %fusion.262 = f32[512,64]{1,0:T(8,128)} fusion(pred[512]{0:T(512)(128)(4,1)S(1)} %get-tuple-element.431, pred[512]{0:T(512)(128)(4,1)S(1)} %get-tuple-element.542, pred[512]{0:T(512)(128)(4,1)S(1)} %get-tuple-element.565, pred[512]{0:T(512)(128)(4,1)S(1)} %get-tuple-element.531, pred[512]{0:T(512)(128)(4,1)S(1)} %get-tuple-element.484, ...), kind=kLoop, calls=%fused_computation.554 | loop fusion | flops 1146880 | bytes 923648 | tf_op jit(solution)/shard_map/add | solution.py:62
  22.1 2.3 %fusion.31 = f32[512,64]{1,0:T(8,128)} fusion(pred[512]{0:T(512)(128)(4,1)S(1)} %get-tuple-element.541, pred[512]{0:T(512)(128)(4,1)S(1)} %get-tuple-element.564, pred[512]{0:T(512)(128)(4,1)S(1)} %get-tuple-element.530, pred[512]{0:T(512)(128)(4,1)S(1)} %get-tuple-element.483, pred[512]{0:T(512)(128)(4,1)S(1)} %get-tuple-element.397, ...), kind=kLoop, calls=%fused_computation.323 | loop fusion | flops 1146880 | bytes 923648 | tf_op jit(solution)/shard_map/add | solution.py:62
  24.3 2.2 %fusion.42 = f32[512,64]{1,0:T(8,128)} fusion(pred[512]{0:T(512)(128)(4,1)S(1)} %get-tuple-element.540, pred[512]{0:T(512)(128)(4,1)S(1)} %get-tuple-element.563, pred[512]{0:T(512)(128)(4,1)S(1)} %get-tuple-element.529, pred[512]{0:T(512)(128)(4,1)S(1)} %get-tuple-element.482, pred[512]{0:T(512)(128)(4,1)S(1)} %get-tuple-element.396, ...), kind=kLoop, calls=%fused_computation.334 | loop fusion | flops 1146880 | bytes 923648 | tf_op jit(solution)/shard_map/add | solution.py:62
  26.6 2.3 %fusion.108 = f32[512,64]{1,0:T(8,128)} fusion(pred[512]{0:T(512)(128)(4,1)S(1)} %get-tuple-element.444, pred[512]{0:T(512)(128)(4,1)S(1)} %get-tuple-element.556, pred[512]{0:T(512)(128)(4,1)S(1)} %get-tuple-element.523, pred[512]{0:T(512)(128)(4,1)S(1)} %get-tuple-element.476, pred[512]{0:T(512)(128)(4,1)S(1)} %get-tuple-element.390, ...), kind=kLoop, calls=%fused_computation.400 | loop fusion | flops 1146880 | bytes 923648 | tf_op jit(solution)/shard_map/add | solution.py:62
  28.8 2.3 %fusion.196 = f32[512,64]{1,0:T(8,128)} fusion(pred[512]{0:T(512)(128)(4,1)S(1)} %get-tuple-element.436, pred[512]{0:T(512)(128)(4,1)S(1)} %get-tuple-element.548, pred[512]{0:T(512)(128)(4,1)S(1)} %get-tuple-element.571, pred[512]{0:T(512)(128)(4,1)S(1)} %get-tuple-element.537, pred[512]{0:T(512)(128)(4,1)S(1)} %get-tuple-element.382, ...), kind=kLoop, calls=%fused_computation.488 | loop fusion | flops 1146880 | bytes 923648 | tf_op jit(solution)/shard_map/add | solution.py:62
  31.1 2.3 %fusion.207 = f32[512,64]{1,0:T(8,128)} fusion(pred[512]{0:T(512)(128)(4,1)S(1)} %get-tuple-element.435, pred[512]{0:T(512)(128)(4,1)S(1)} %get-tuple-element.547, pred[512]{0:T(512)(128)(4,1)S(1)} %get-tuple-element.570, pred[512]{0:T(512)(128)(4,1)S(1)} %get-tuple-element.536, pred[512]{0:T(512)(128)(4,1)S(1)} %get-tuple-element.381, ...), kind=kLoop, calls=%fused_computation.499 | loop fusion | flops 1146880 | bytes 923648 | tf_op jit(solution)/shard_map/add | solution.py:62
  33.4 2.3 %fusion.218 = f32[512,64]{1,0:T(8,128)} fusion(pred[512]{0:T(512)(128)(4,1)S(1)} %get-tuple-element.434, pred[512]{0:T(512)(128)(4,1)S(1)} %get-tuple-element.546, pred[512]{0:T(512)(128)(4,1)S(1)} %get-tuple-element.569, pred[512]{0:T(512)(128)(4,1)S(1)} %get-tuple-element.535, pred[512]{0:T(512)(128)(4,1)S(1)} %get-tuple-element.380, ...), kind=kLoop, calls=%fused_computation.510 | loop fusion | flops 1146880 | bytes 923648 | tf_op jit(solution)/shard_map/add | solution.py:62
  35.6 2.3 %fusion.273 = f32[512,64]{1,0:T(8,128)} fusion(pred[512]{0:T(512)(128)(4,1)S(1)} %get-tuple-element.450, pred[512]{0:T(512)(128)(4,1)S(1)} %get-tuple-element.558, pred[512]{0:T(512)(128)(4,1)S(1)} %get-tuple-element.577, pred[512]{0:T(512)(128)(4,1)S(1)} %get-tuple-element.539, pred[512]{0:T(512)(128)(4,1)S(1)} %get-tuple-element.488, ...), kind=kLoop, calls=%fused_computation.565 | loop fusion | flops 1146880 | bytes 923648 | tf_op jit(solution)/shard_map/add | solution.py:62
  37.9 2.3 %fusion.53 = f32[512,64]{1,0:T(8,128)} fusion(pred[512]{0:T(512)(128)(4,1)S(1)} %get-tuple-element.449, pred[512]{0:T(512)(128)(4,1)S(1)} %get-tuple-element.562, pred[512]{0:T(512)(128)(4,1)S(1)} %get-tuple-element.528, pred[512]{0:T(512)(128)(4,1)S(1)} %get-tuple-element.481, pred[512]{0:T(512)(128)(4,1)S(1)} %get-tuple-element.395, ...), kind=kLoop, calls=%fused_computation.345 | loop fusion | flops 1146880 | bytes 923648 | tf_op jit(solution)/shard_map/add | solution.py:62
  40.1 2.3 %fusion.64 = f32[512,64]{1,0:T(8,128)} fusion(pred[512]{0:T(512)(128)(4,1)S(1)} %get-tuple-element.448, pred[512]{0:T(512)(128)(4,1)S(1)} %get-tuple-element.561, pred[512]{0:T(512)(128)(4,1)S(1)} %get-tuple-element.527, pred[512]{0:T(512)(128)(4,1)S(1)} %get-tuple-element.480, pred[512]{0:T(512)(128)(4,1)S(1)} %get-tuple-element.394, ...), kind=kLoop, calls=%fused_computation.356 | loop fusion | flops 1146880 | bytes 923648 | tf_op jit(solution)/shard_map/add | solution.py:62
  42.4 2.3 %fusion.75 = f32[512,64]{1,0:T(8,128)} fusion(pred[512]{0:T(512)(128)(4,1)S(1)} %get-tuple-element.447, pred[512]{0:T(512)(128)(4,1)S(1)} %get-tuple-element.560, pred[512]{0:T(512)(128)(4,1)S(1)} %get-tuple-element.526, pred[512]{0:T(512)(128)(4,1)S(1)} %get-tuple-element.479, pred[512]{0:T(512)(128)(4,1)S(1)} %get-tuple-element.393, ...), kind=kLoop, calls=%fused_computation.367 | loop fusion | flops 1146880 | bytes 923648 | tf_op jit(solution)/shard_map/add | solution.py:62
  44.6 2.2 %fusion.86 = f32[512,64]{1,0:T(8,128)} fusion(pred[512]{0:T(512)(128)(4,1)S(1)} %get-tuple-element.446, pred[512]{0:T(512)(128)(4,1)S(1)} %get-tuple-element.559, pred[512]{0:T(512)(128)(4,1)S(1)} %get-tuple-element.525, pred[512]{0:T(512)(128)(4,1)S(1)} %get-tuple-element.478, pred[512]{0:T(512)(128)(4,1)S(1)} %get-tuple-element.392, ...), kind=kLoop, calls=%fused_computation.378 | loop fusion | flops 1146880 | bytes 923648 | tf_op jit(solution)/shard_map/add | solution.py:62
  46.9 2.3 %fusion.97 = f32[512,64]{1,0:T(8,128)} fusion(pred[512]{0:T(512)(128)(4,1)S(1)} %get-tuple-element.445, pred[512]{0:T(512)(128)(4,1)S(1)} %get-tuple-element.557, pred[512]{0:T(512)(128)(4,1)S(1)} %get-tuple-element.524, pred[512]{0:T(512)(128)(4,1)S(1)} %get-tuple-element.477, pred[512]{0:T(512)(128)(4,1)S(1)} %get-tuple-element.391, ...), kind=kLoop, calls=%fused_computation.389 | loop fusion | flops 1146880 | bytes 923648 | tf_op jit(solution)/shard_map/add | solution.py:62
  49.1 2.2 %fusion.119 = f32[512,64]{1,0:T(8,128)} fusion(pred[512]{0:T(512)(128)(4,1)S(1)} %get-tuple-element.443, pred[512]{0:T(512)(128)(4,1)S(1)} %get-tuple-element.555, pred[512]{0:T(512)(128)(4,1)S(1)} %get-tuple-element.522, pred[512]{0:T(512)(128)(4,1)S(1)} %get-tuple-element.475, pred[512]{0:T(512)(128)(4,1)S(1)} %get-tuple-element.389, ...), kind=kLoop, calls=%fused_computation.411 | loop fusion | flops 1146880 | bytes 923648 | tf_op jit(solution)/shard_map/add | solution.py:62
  51.4 2.3 %fusion.130 = f32[512,64]{1,0:T(8,128)} fusion(pred[512]{0:T(512)(128)(4,1)S(1)} %get-tuple-element.442, pred[512]{0:T(512)(128)(4,1)S(1)} %get-tuple-element.554, pred[512]{0:T(512)(128)(4,1)S(1)} %get-tuple-element.521, pred[512]{0:T(512)(128)(4,1)S(1)} %get-tuple-element.474, pred[512]{0:T(512)(128)(4,1)S(1)} %get-tuple-element.388, ...), kind=kLoop, calls=%fused_computation.422 | loop fusion | flops 1146880 | bytes 923648 | tf_op jit(solution)/shard_map/add | solution.py:62
  53.7 2.3 %fusion.141 = f32[512,64]{1,0:T(8,128)} fusion(pred[512]{0:T(512)(128)(4,1)S(1)} %get-tuple-element.441, pred[512]{0:T(512)(128)(4,1)S(1)} %get-tuple-element.553, pred[512]{0:T(512)(128)(4,1)S(1)} %get-tuple-element.576, pred[512]{0:T(512)(128)(4,1)S(1)} %get-tuple-element.473, pred[512]{0:T(512)(128)(4,1)S(1)} %get-tuple-element.387, ...), kind=kLoop, calls=%fused_computation.433 | loop fusion | flops 1146880 | bytes 923648 | tf_op jit(solution)/shard_map/add | solution.py:62
  55.9 2.3 %fusion.152 = f32[512,64]{1,0:T(8,128)} fusion(pred[512]{0:T(512)(128)(4,1)S(1)} %get-tuple-element.440, pred[512]{0:T(512)(128)(4,1)S(1)} %get-tuple-element.552, pred[512]{0:T(512)(128)(4,1)S(1)} %get-tuple-element.575, pred[512]{0:T(512)(128)(4,1)S(1)} %get-tuple-element.472, pred[512]{0:T(512)(128)(4,1)S(1)} %get-tuple-element.386, ...), kind=kLoop, calls=%fused_computation.444 | loop fusion | flops 1146880 | bytes 923648 | tf_op jit(solution)/shard_map/add | solution.py:62
  58.2 2.3 %fusion.163 = f32[512,64]{1,0:T(8,128)} fusion(pred[512]{0:T(512)(128)(4,1)S(1)} %get-tuple-element.439, pred[512]{0:T(512)(128)(4,1)S(1)} %get-tuple-element.551, pred[512]{0:T(512)(128)(4,1)S(1)} %get-tuple-element.574, pred[512]{0:T(512)(128)(4,1)S(1)} %get-tuple-element.471, pred[512]{0:T(512)(128)(4,1)S(1)} %get-tuple-element.385, ...), kind=kLoop, calls=%fused_computation.455 | loop fusion | flops 1146880 | bytes 923648 | tf_op jit(solution)/shard_map/add | solution.py:62
  60.4 2.2 %fusion.174 = f32[512,64]{1,0:T(8,128)} fusion(pred[512]{0:T(512)(128)(4,1)S(1)} %get-tuple-element.438, pred[512]{0:T(512)(128)(4,1)S(1)} %get-tuple-element.550, pred[512]{0:T(512)(128)(4,1)S(1)} %get-tuple-element.573, pred[512]{0:T(512)(128)(4,1)S(1)} %get-tuple-element.470, pred[512]{0:T(512)(128)(4,1)S(1)} %get-tuple-element.384, ...), kind=kLoop, calls=%fused_computation.466 | loop fusion | flops 1146880 | bytes 923648 | tf_op jit(solution)/shard_map/add | solution.py:62
  62.7 2.3 %fusion.185 = f32[512,64]{1,0:T(8,128)} fusion(pred[512]{0:T(512)(128)(4,1)S(1)} %get-tuple-element.437, pred[512]{0:T(512)(128)(4,1)S(1)} %get-tuple-element.549, pred[512]{0:T(512)(128)(4,1)S(1)} %get-tuple-element.572, pred[512]{0:T(512)(128)(4,1)S(1)} %get-tuple-element.538, pred[512]{0:T(512)(128)(4,1)S(1)} %get-tuple-element.383, ...), kind=kLoop, calls=%fused_computation.477 | loop fusion | flops 1146880 | bytes 923648 | tf_op jit(solution)/shard_map/add | solution.py:62
  64.9 2.3 %fusion.20 = f32[512,64]{1,0:T(8,128)} fusion(pred[512]{0:T(512)(128)(4,1)S(1)} %get-tuple-element.429, pred[512]{0:T(512)(128)(4,1)S(1)} %get-tuple-element.428, pred[512]{0:T(512)(128)(4,1)S(1)} %get-tuple-element.427, pred[512]{0:T(512)(128)(4,1)S(1)} %get-tuple-element.426, pred[512]{0:T(512)(128)(4,1)S(1)} %get-tuple-element.425, ...), kind=kLoop, calls=%fused_computation.312 | loop fusion | flops 1146880 | bytes 923648 | tf_op jit(solution)/shard_map/add | solution.py:62
  69.9 4.9 %concatenate.27 = f32[512,1536]{1,0:T(8,128)S(1)} concatenate(f32[512,64]{1,0:T(8,128)} %fusion.20, f32[512,64]{1,0:T(8,128)} %fusion.31, f32[512,64]{1,0:T(8,128)} %fusion.42, f32[512,64]{1,0:T(8,128)} %fusion.53, f32[512,64]{1,0:T(8,128)} %fusion.64, f32[512,64]{1,0:T(8,128)} %fusion.75, f32[512,64]{1,0:T(8,128)} %fusion.86, f32[512,64]{1,0:T(8,128)} %fusion.97, ...), dimensions={1} | concatenate | bytes 6291456 | tf_op jit(solution)/shard_map/concatenate | solution.py:66
  81.8 2.5 %fusion.6 = f32[512,640]{1,0:T(8,128)} fusion(bf16[1536,640]{0,1:T(8,128)(2,1)S(1)} %select_dynamic-update-slice_fusion, f32[512,1536]{1,0:T(8,128)S(1)} %concatenate.27), kind=kOutput, calls=%fused_computation.295 | convolution fusion | flops 1007419392 | bytes 6422528 | tf_op jit(solution)/shard_map/ar,rc->ac/dot_general | solution.py:18
  84.3 4.9 %fusion.3 = f32[384,640]{1,0:T(8,128)} fusion(bf16[512,384]{1,0:T(8,128)(2,1)} %concatenate.26, f32[512,640]{1,0:T(8,128)} %fusion.6, bf16[1536,640]{0,1:T(8,128)(2,1)} %copy-done.2, f32[512,1536]{1,0:T(8,128)S(1)} %concatenate.27), kind=kOutput, calls=%fused_computation.292 | convolution fusion | flops 1262092288 | bytes 7798784 | tf_op jit(solution)/shard_map/ro,rc->oc/dot_general | solution.py:18
  91.7 4.4 %collective-permute-start.3 = (f32[128,640]{1,0:T(8,128)S(1)}, f32[128,640]{1,0:T(8,128)S(1)}, u32[]{:S(2)}, u32[]{:S(2)}) collective-permute-start(f32[128,640]{1,0:T(8,128)S(1)} %get-tuple-element.372), channel_id=1, source_target_pairs={{0,1},{1,2},{2,3},{3,4},{4,5},{5,6},{6,7},{7,8},{8,9},{9,10},{10,1... | collective-permute-start | bytes 983048 | tf_op jit(solution)/shard_map/ppermute | solution.py:24
  97.4 18.1 %collective-permute-start.4 = (bf16[1,128,896]{2,1,0:T(8,128)(2,1)S(1)}, bf16[1,128,896]{2,1,0:T(8,128)(2,1)S(1)}, u32[]{:S(2)}, u32[]{:S(2)}) collective-permute-start(bf16[1,128,896]{2,1,0:T(8,128)(2,1)S(1)} %fusion.274), channel_id=1, source_target_pairs={{0,16},{16,0},{1,17},{17,1},{2,18},{18,2},{3,19},{19,3},{4,20},{20... | collective-permute-start | bytes 688136 | tf_op jit(solution)/shard_map/ppermute | solution.py:28
  115.6 4.0 %collective-permute-done.4 = bf16[1,128,896]{2,1,0:T(8,128)(2,1)S(1)} collective-permute-done((bf16[1,128,896]{2,1,0:T(8,128)(2,1)S(1)}, bf16[1,128,896]{2,1,0:T(8,128)(2,1)S(1)}, u32[]{:S(2)}, u32[]{:S(2)}) %collective-permute-start.4) | collective-permute-done | bytes 229408 | tf_op jit(solution)/shard_map/ppermute | solution.py:28
  (49 shorter events, 21.5 us)
Async XLA Ops:
  0.0 13.0 %copy-start = (bf16[512,768]{1,0:T(8,128)(2,1)S(1)}, bf16[512,768]{1,0:T(8,128)(2,1)}, u32[]{:S(2)}) copy-start(bf16[512,768]{1,0:T(8,128)(2,1)} %param.6) | copy-start | bytes 2359300
  2.6 72.2 %collective-permute-start.1 = (bf16[528,256]{0,1:T(8,128)(2,1)}, bf16[528,256]{0,1:T(8,128)(2,1)}, u32[]{:S(2)}, u32[]{:S(2)}) collective-permute-start(bf16[528,256]{0,1:T(8,128)(2,1)} %fusion.9), channel_id=1, source_target_pairs={{1,0},{2,1},{3,2},{4,3},{5,4},{6,5},{7,6},{8,7},{9,8},{10,9},{11,1... | collective-permute-start | bytes 811016 | tf_op jit(solution)/shard_map/ppermute | solution.py:24
  3.9 71.6 %collective-permute-start = (bf16[528,256]{0,1:T(8,128)(2,1)}, bf16[528,256]{0,1:T(8,128)(2,1)}, u32[]{:S(2)}, u32[]{:S(2)}) collective-permute-start(bf16[528,256]{0,1:T(8,128)(2,1)} %fusion.9), channel_id=1, source_target_pairs={{0,1},{1,2},{2,3},{3,4},{4,5},{5,6},{6,7},{7,8},{8,9},{9,10},{10,1... | collective-permute-start | bytes 811016 | tf_op jit(solution)/shard_map/ppermute | solution.py:24
  62.7 4.5 %copy-start.1 = (bf16[512,256]{1,0:T(8,128)(2,1)S(1)}, bf16[512,256]{1,0:T(8,128)(2,1)}, u32[]{:S(2)}) copy-start(bf16[512,256]{1,0:T(8,128)(2,1)} %param.8) | copy-start | bytes 786436
  80.5 1.3 %copy-start.2 = (bf16[1536,640]{0,1:T(8,128)(2,1)}, bf16[1536,640]{0,1:T(8,128)(2,1)S(1)}, u32[]{:S(2)}) copy-start(bf16[1536,640]{0,1:T(8,128)(2,1)S(1)} %select_dynamic-update-slice_fusion) | copy-start | bytes 5898244
  90.4 5.8 %collective-permute-start.2 = (f32[128,640]{1,0:T(8,128)S(1)}, f32[128,640]{1,0:T(8,128)S(1)}, u32[]{:S(2)}, u32[]{:S(2)}) collective-permute-start(f32[128,640]{1,0:T(8,128)S(1)} %get-tuple-element.373), channel_id=1, source_target_pairs={{1,0},{2,1},{3,2},{4,3},{5,4},{6,5},{7,6},{8,7},{9,8},{10,9},{11,1... | collective-permute-start | bytes 983048 | tf_op jit(solution)/shard_map/ppermute | solution.py:24
  91.7 5.7 %collective-permute-start.3 = (f32[128,640]{1,0:T(8,128)S(1)}, f32[128,640]{1,0:T(8,128)S(1)}, u32[]{:S(2)}, u32[]{:S(2)}) collective-permute-start(f32[128,640]{1,0:T(8,128)S(1)} %get-tuple-element.372), channel_id=1, source_target_pairs={{0,1},{1,2},{2,3},{3,4},{4,5},{5,6},{6,7},{7,8},{8,9},{9,10},{10,1... | collective-permute-start | bytes 983048 | tf_op jit(solution)/shard_map/ppermute | solution.py:24
  97.4 22.1 %collective-permute-start.4 = (bf16[1,128,896]{2,1,0:T(8,128)(2,1)S(1)}, bf16[1,128,896]{2,1,0:T(8,128)(2,1)S(1)}, u32[]{:S(2)}, u32[]{:S(2)}) collective-permute-start(bf16[1,128,896]{2,1,0:T(8,128)(2,1)S(1)} %fusion.274), channel_id=1, source_target_pairs={{0,16},{16,0},{1,17},{17,1},{2,18},{18,2},{3,19},{19,3},{4,20},{20... | collective-permute-start | bytes 688136 | tf_op jit(solution)/shard_map/ppermute | solution.py:28

commit v3 on v1

v3 whole, which is shorter than its diff:
```python
import jax
import jax.numpy as jnp
from jax import lax
from jax.experimental import pallas as pl
from jax.experimental.pallas import tpu as pltpu
from jax.sharding import PartitionSpec as P

B = 64
KA = 12
KP = 4
NC = 2
RB = 8
LINE = ("grp", "dev")
HALF = 128


def shifted(x, axis, by):
    peers = lax.axis_size(axis)
    pairs = [(i, i + by) for i in range(peers) if 0 <= i + by < peers]
    return lax.ppermute(x, axis, pairs)


def partner_2(x, axis, bit):
    return lax.ppermute(x, axis, [(i, i ^ 1 << bit) for i in range(lax.axis_size(axis))])


def chunk(j):
    return pl.ds(pl.multiple_of(j * HALF, HALF), HALF)


def rows_at(r):
    return pl.ds(pl.multiple_of(r * B, B), B)


def product_kernel(lc_ref, pc_ref, po_ref, a_ref, pl_ref, pm_ref, pr_ref, out_ref, ps_ref, panel_ref, ap_ref, st_ref):
    side = lax.broadcasted_iota(jnp.int32, (B, HALF), 1) // B
    ps_ref[...] = jnp.zeros(ps_ref.shape, ps_ref.dtype)
    sources = (pl_ref, pm_ref, pr_ref)
    for r in range(3 * RB):
        blk = sources[r // RB][(r % RB) * B : (r % RB + 1) * B, :].astype(jnp.float32)
        halves = [blk[:, 0:HALF], blk[:, HALF : 2 * HALF]]
        swapped = [pltpu.roll(h, B, 1) for h in halves]
        for l in range(KP):
            j = pc_ref[r, l]
            h = j % 2
            val = jnp.where(h == l % 2, halves[l // 2], swapped[l // 2])
            cols = chunk(j // 2)
            cur = ps_ref[r * B : (r + 1) * B, cols].astype(jnp.float32)
            ps_ref[r * B : (r + 1) * B, cols] = jnp.where(side == h, val, cur).astype(ps_ref.dtype)
    for i in range(RB):
        for k in range(KA):
            panel_ref[k * B : (k + 1) * B, :] = ps_ref[rows_at(lc_ref[i, k]), :]
        ap = jnp.dot(a_ref[i * B : (i + 1) * B, :], panel_ref[...], preferred_element_type=jnp.float32)
        ap_ref[i * B : (i + 1) * B, :] = ap.astype(ap_ref.dtype)
    pt = pm_ref[...].astype(jnp.float32).T
    st_ref[...] = jnp.zeros(st_ref.shape, st_ref.dtype)
    for i in range(RB):
        cols = slice((i // 2) * HALF, (i // 2 + 1) * HALF)
        for l in range(KP):
            dest = rows_at(po_ref[i, l])
            cur = st_ref[dest, cols]
            st_ref[dest, cols] = jnp.where(side == i % 2, pt[l * B : (l + 1) * B, cols], cur)
    out_ref[...] = jnp.dot(
        st_ref[...].astype(jnp.bfloat16), ap_ref[...], preferred_element_type=jnp.float32
    )


def products(lc, pc, po, a_blocks, left, own, right):
    smem = pl.BlockSpec(memory_space=pltpu.SMEM)
    vmem = pl.BlockSpec(memory_space=pltpu.VMEM)
    near = 3 * RB * B
    return pl.pallas_call(
        product_kernel,
        out_shape=jax.ShapeDtypeStruct((3 * NC * B, 5 * NC * B), jnp.float32),
        in_specs=[smem] * 3 + [vmem] * 4,
        out_specs=vmem,
        scratch_shapes=[
            pltpu.VMEM((near, 5 * NC * B), jnp.bfloat16),
            pltpu.VMEM((KA * B, 5 * NC * B), jnp.bfloat16),
            pltpu.VMEM((RB * B, 5 * NC * B), jnp.bfloat16),
            pltpu.VMEM((3 * NC * B, RB * B), jnp.float32),
        ],
        cost_estimate=pl.CostEstimate(
            flops=2 * RB * B * KA * B * 5 * NC * B + 2 * 3 * NC * B * RB * B * 5 * NC * B,
            bytes_accessed=4 * 1024 * 1024,
            transcendentals=0,
        ),
    )(lc, pc, po, a_blocks, left, own, right)


def local(a_blocks, a_cols, p_blocks, p_cols):
    q = lax.axis_index(LINE)
    rel = (p_cols - (q - 1) * NC).astype(jnp.bfloat16)
    tag = jnp.zeros((16, KP * B), jnp.bfloat16).at[:RB, :KP].set(rel)
    payload = jnp.concatenate([p_blocks, tag], axis=0)
    from_left = shifted(payload, LINE, 1)
    from_right = shifted(payload, LINE, -1)

    def cols(x, shift):
        return x[RB * B : RB * B + RB, :KP].astype(jnp.int32) + shift

    pc = jnp.concatenate([cols(from_left, 0), p_cols - (q - 2) * NC, cols(from_right, 2 * NC)], axis=0)
    lc = a_cols - (q - 1) * RB
    po = p_cols - (q - 1) * NC
    partial_value = products(lc, pc, po, a_blocks, from_left, p_blocks, from_right)

    partial_value = partial_value.reshape(3, NC * B, 5 * NC * B)
    from_right_p = shifted(partial_value[0], LINE, -1)
    from_left_p = shifted(partial_value[2], LINE, 1)
    span = NC * B
    combined = jnp.pad(partial_value[1], ((0, 0), (span, span)))
    combined = combined + jnp.pad(from_right_p, ((0, 0), (2 * span, 0)))
    combined = combined + jnp.pad(from_left_p, ((0, 0), (0, 2 * span)))
    rows_here = combined.astype(jnp.bfloat16)[None]
    group = lax.axis_index("grp")
    joined = rows_here
    for section_bit in range(lax.axis_size("grp").bit_length() - 1):
        partner = partner_2(joined, "grp", section_bit)
        is_upper = group // 2**section_bit % 2 == 1
        joined = jnp.where(
            is_upper,
            jnp.concatenate([partner, joined], axis=0),
            jnp.concatenate([joined, partner], axis=0),
        )
    return joined


def solution(mesh):
    placed = (P(LINE, None),) * 4
    return jax.shard_map(
        local, mesh=mesh, in_specs=placed, out_specs=P(None, "dev", None), check_vma=False
    )
```

time: 74.3 us -> 48.9 us (0.66)
  local copies, waits for them, and re-layouts: 24.5 us -> 2.05 us
  matrix products: 12.6 us -> 0 us
  starting transfers between devices: 22.3 us -> 28.6 us
  Pallas kernels: 0 us -> 5.45 us
  other arithmetic: 7.54 us -> 3.73 us
  waiting for transfers between devices: 6.45 us -> 8.69 us
    dot_general x3 -> x0, matrix products: 12.6 us -> none  [mm(): return jnp.einsum(spec, x, y, preferred_element_type=jnp.float32)]
    convert_element_type x2 -> x0, local copies, waits for them, and re-layouts: 8.28 us -> none  [the longest x1 5.32 us: local(): lo = (dense - hi.astype(jnp.float32)).astype(jnp.bfloat16)]
    select_n x2 -> x0, local copies, waits for them, and re-layouts: 7.5 us -> none  [spread(): out = jnp.where(hit, blocks[:, :, l:l + 1, :], out)]
    pallas_call x0 -> x1, Pallas kernels: none -> 5.45 us  [products(): pl.pallas_call(product_kernel, out_shape=jax.ShapeDtypeStruct((3 * NC * B...]
    ppermute x4, starting transfers between devices: 10.2 us -> 14.2 us  [shifted(): return lax.ppermute(x, axis, pairs)]
    select_n x2 -> x0, other arithmetic: 3.77 us -> none  [spread(): out = jnp.where(hit, blocks[:, :, l:l + 1, :], out)]
    reshape x4 -> x0, local copies, waits for them, and re-layouts: 3.02 us -> none  [the longest x1 2.21 us: local(): a4 = a_blocks.reshape(RB, B, KA, B)]
    ppermute x4, waiting for transfers between devices: 2.22 us -> 4.69 us  [shifted(): return lax.ppermute(x, axis, pairs)]
  transfers between devices with their start and end apart: 5 -> 5, of which waited for: 2 -> 3; matrix products, arithmetic and copies ran while one was open for 29% -> 1% of each run, Pallas kernels for 0% -> 0%
where the time goes in v3:
time: 48.9 us; the launch traced here: 48.6 us
  starting transfers between devices  28.6 us (58%)
  waiting for transfers between devices  8.69 us (18%)
  Pallas kernels  5.45 us (11%)
  other arithmetic  3.73 us (8%)
  local copies, waits for them, and re-layouts  2.05 us (4%)
    ppermute x1, starting transfers between devices, partner_2(): lax.ppermute(x, axis, [(i, i ^ 1 << bit) for i in range(lax.axis_size(axi...  14.4 us
    ppermute x4, starting transfers between devices, shifted(): return lax.ppermute(x, axis, pairs)  14.2 us
    pallas_call x1, Pallas kernels, products(): pl.pallas_call(product_kernel, out_shape=jax.ShapeDtypeStruct((3 * NC * B...  5.45 us
    ppermute x4, waiting for transfers between devices, shifted(): return lax.ppermute(x, axis, pairs)  4.69 us
    ppermute x1, waiting for transfers between devices, partner_2(): lax.ppermute(x, axis, [(i, i ^ 1 << bit) for i in range(lax.axis_size(axi...  4 us
    slice x1, local copies, waits for them, and re-layouts, local(): combined = jnp.pad(partial_value[1], ((0, 0), (span, span)))  1.23 us
    concatenate x1, other arithmetic, local(): payload = jnp.concatenate([p_blocks, tag], axis=0)  0.98 us
  transfers between devices with their start and end apart: 5, of which 3 were waited for; matrix products, arithmetic and copies ran while one was open for 1% of the time, Pallas kernels for 0%

profile of v3, /device:TPU:0, one launch (start us, length us, event | category | flops | bytes accessed | tf_op | source)
XLA Modules:
  0.0 48.6 jit_solution(16629432841487803366)
XLA Ops:
  0.0 0.0 copy-start.1
  0.0 0.7 %copy-done.1 = s32[8,4]{0,1:T(4,128)S(1)} copy-done((s32[8,4]{0,1:T(4,128)S(1)}, s32[8,4]{0,1:T(4,128)}, u32[]{:S(2)}) %copy-start.1) | copy-done | bytes 152
  0.7 0.1 copy.11
  0.8 0.6 %fusion.3 = (bf16[8,4]{1,0:T(8,128)(2,1)S(1)}, s32[8,4]{1,0:T(8,128)}, s32[8,4]{1,0:T(8,128)S(1)}) fusion(s32[8,4]{1,0:T(8,128)S(1)} %copy.11, s32[]{:T(128)S(6)} %mul.15, s32[]{:T(128)S(6)} %mul.16), kind=kLoop, calls=%fused_computation.12 | loop fusion | flops 96 | bytes 456 | tf_op jit(solution)/shard_map/convert_element_type | solution.py:93
  1.4 0.0 copy-start
  1.4 1.0 %fusion.1 = bf16[528,256]{1,0:T(8,128)(2,1)S(1)} fusion(bf16[8,4]{1,0:T(8,128)(2,1)S(1)} %get-tuple-element.17, bf16[512,256]{1,0:T(8,128)(2,1)} %pm_ref.1), kind=kLoop, calls=%fused_computation.4 | loop fusion | flops 811008 | bytes 532544 | tf_op jit(solution)/shard_map/concatenate | solution.py:95
  2.4 1.3 %collective-permute-start.1 = (bf16[528,256]{1,0:T(8,128)(2,1)S(1)}, bf16[528,256]{1,0:T(8,128)(2,1)S(1)}, u32[]{:S(2)}, u32[]{:S(2)}) collective-permute-start(bf16[528,256]{1,0:T(8,128)(2,1)S(1)} %fusion.1), channel_id=1, source_target_pairs={{1,0},{2,1},{3,2},{4,3},{5,4},{6,5},{7,6},{8,7},{9,8},{10,9},{11,1... | collective-permute-start | bytes 811016 | tf_op jit(solution)/shard_map/ppermute | solution.py:20
  3.6 3.0 %collective-permute-start = (bf16[528,256]{1,0:T(8,128)(2,1)S(1)}, bf16[528,256]{1,0:T(8,128)(2,1)S(1)}, u32[]{:S(2)}, u32[]{:S(2)}) collective-permute-start(bf16[528,256]{1,0:T(8,128)(2,1)S(1)} %fusion.1), channel_id=1, source_target_pairs={{0,1},{1,2},{2,3},{3,4},{4,5},{5,6},{6,7},{7,8},{8,9},{9,10},{10,1... | collective-permute-start | bytes 811016 | tf_op jit(solution)/shard_map/ppermute | solution.py:20
  6.7 0.0 copy-done
  6.7 0.6 %broadcast_subtract_fusion.2.lc_ref = s32[8,12]{1,0:T(8,128)} fusion(s32[8,12]{1,0:T(8,128)S(1)} %copy-done, s32[]{:T(128)S(6)} %mul.14), kind=kLoop, calls=%fused_computation.11 | loop fusion | flops 96 | bytes 772 | tf_op jit(solution)/shard_map/sub | solution.py:103
  7.3 0.0 collective-permute-done.1.pr_ref
  7.3 0.0 copy-start.2
  7.3 0.5 %collective-permute-done.pl_ref = bf16[528,256]{1,0:T(8,128)(2,1)S(1)} collective-permute-done((bf16[528,256]{1,0:T(8,128)(2,1)S(1)}, bf16[528,256]{1,0:T(8,128)(2,1)S(1)}, u32[]{:S(2)}, u32[]{:S(2)}) %collective-permute-start) | collective-permute-done | bytes 270368 | tf_op jit(solution)/shard_map/ppermute | solution.py:20
  7.8 0.0 copy-start.3
  7.9 0.6 %pad_add_fusion.pc_ref = s32[24,4]{1,0:T(8,128)} fusion(s32[8,4]{1,0:T(8,128)S(1)} %convert_add_fusion, s32[8,4]{1,0:T(8,128)S(1)} %get-tuple-element.22, s32[8,4]{1,0:T(8,128)S(1)} %slice_convert_fusion), kind=kLoop, calls=%fused_computation.6 | loop fusion | flops 192 | bytes 768 | tf_op jit(solution)/shard_map/concatenate | solution.py:102
  8.5 0.0 copy-done.2
  8.5 0.0 copy-done.3
  8.6 5.4 %shard_map.46 = f32[384,640]{1,0:T(8,128)} custom-call(s32[8,12]{1,0:T(8,128)} %broadcast_subtract_fusion.2.lc_ref, s32[24,4]{1,0:T(8,128)} %pad_add_fusion.pc_ref, s32[8,4]{1,0:T(8,128)} %get-tuple-element.18.po_ref, bf16[512,768]{1,0:T(8,128)(2,1)} %a_ref.1, bf16[528,256]{1,0:T(8,128)(2,1)} %copy-done.3, bf16[512,256]{1,0:T(8,128)(2,1)} %pm_ref.1, ...), custom_call_target="tpu_custom_call" | custom-call | flops 754974720 | bytes 4194304 | tf_op jit(solution)/shard_map/pallas_call | solution.py:72
  14.0 1.2 %fusion.4 = (f32[128,640]{1,0:T(8,128)S(1)}, f32[128,640]{1,0:T(8,128)S(1)}, f32[128,640]{1,0:T(8,128)S(1)}) fusion(f32[384,640]{1,0:T(8,128)} %shard_map.46), kind=kLoop, calls=%fused_computation.13 | loop fusion | bytes 1966080 | tf_op jit(solution)/shard_map/slice | solution.py:111
  15.2 8.6 %collective-permute-start.3 = (f32[128,640]{1,0:T(8,128)S(1)}, f32[128,640]{1,0:T(8,128)S(1)}, u32[]{:S(2)}, u32[]{:S(2)}) collective-permute-start(f32[128,640]{1,0:T(8,128)S(1)} %get-tuple-element.20), channel_id=1, source_target_pairs={{0,1},{1,2},{2,3},{3,4},{4,5},{5,6},{6,7},{7,8},{8,9},{9,10},{10,1... | collective-permute-start | bytes 983048 | tf_op jit(solution)/shard_map/ppermute | solution.py:20
  23.9 1.3 %collective-permute-start.2 = (f32[128,640]{1,0:T(8,128)S(1)}, f32[128,640]{1,0:T(8,128)S(1)}, u32[]{:S(2)}, u32[]{:S(2)}) collective-permute-start(f32[128,640]{1,0:T(8,128)S(1)} %get-tuple-element.21), channel_id=1, source_target_pairs={{1,0},{2,1},{3,2},{4,3},{5,4},{6,5},{7,6},{8,7},{9,8},{10,9},{11,1... | collective-permute-start | bytes 983048 | tf_op jit(solution)/shard_map/ppermute | solution.py:20
  25.2 0.0 collective-permute-done.3
  25.2 4.2 %collective-permute-done.2 = f32[128,640]{1,0:T(8,128)S(1)} collective-permute-done((f32[128,640]{1,0:T(8,128)S(1)}, f32[128,640]{1,0:T(8,128)S(1)}, u32[]{:S(2)}, u32[]{:S(2)}) %collective-permute-start.2) | collective-permute-done | bytes 327712 | tf_op jit(solution)/shard_map/ppermute | solution.py:20
  29.4 14.4 %collective-permute-start.4 = (bf16[1,128,896]{2,1,0:T(8,128)(2,1)S(1)}, bf16[1,128,896]{2,1,0:T(8,128)(2,1)S(1)}, u32[]{:S(2)}, u32[]{:S(2)}) collective-permute-start(bf16[1,128,896]{2,1,0:T(8,128)(2,1)S(1)} %fusion.2), channel_id=1, source_target_pairs={{0,16},{16,0},{1,17},{17,1},{2,18},{18,2},{3,19},{19,3},{4,20},{20... | collective-permute-start | bytes 688136 | tf_op jit(solution)/shard_map/ppermute | solution.py:24
  43.8 4.0 %collective-permute-done.4 = bf16[1,128,896]{2,1,0:T(8,128)(2,1)S(1)} collective-permute-done((bf16[1,128,896]{2,1,0:T(8,128)(2,1)S(1)}, bf16[1,128,896]{2,1,0:T(8,128)(2,1)S(1)}, u32[]{:S(2)}, u32[]{:S(2)}) %collective-permute-start.4) | collective-permute-done | bytes 229408 | tf_op jit(solution)/shard_map/ppermute | solution.py:24
  47.8 0.8 %maximum_select_fusion = bf16[2,128,896]{2,1,0:T(8,128)(2,1)} fusion(bf16[1,128,896]{2,1,0:T(8,128)(2,1)S(1)} %fusion.2, bf16[1,128,896]{2,1,0:T(8,128)(2,1)S(1)} %collective-permute-done.4, pred[]{:T(512)S(6)} %eq.5), kind=kLoop, calls=%fused_computation.2 | loop fusion | flops 688128 | bytes 917505 | tf_op jit(solution)/shard_map/jit(_where)/select_n | solution.py:120
  (3 shorter events, 0.1 us)
Async XLA Ops:
  0.0 0.7 %copy-start.1 = (s32[8,4]{0,1:T(4,128)S(1)}, s32[8,4]{0,1:T(4,128)}, u32[]{:S(2)}) copy-start(s32[8,4]{0,1:T(4,128)} %param.9) | copy-start | bytes 388
  1.4 5.3 %copy-start = (s32[8,12]{1,0:T(8,128)S(1)}, s32[8,12]{1,0:T(8,128)}, u32[]{:S(2)}) copy-start(s32[8,12]{1,0:T(8,128)} %param.7) | copy-start | bytes 1156
  2.4 5.0 %collective-permute-start.1 = (bf16[528,256]{1,0:T(8,128)(2,1)S(1)}, bf16[528,256]{1,0:T(8,128)(2,1)S(1)}, u32[]{:S(2)}, u32[]{:S(2)}) collective-permute-start(bf16[528,256]{1,0:T(8,128)(2,1)S(1)} %fusion.1), channel_id=1, source_target_pairs={{1,0},{2,1},{3,2},{4,3},{5,4},{6,5},{7,6},{8,7},{9,8},{10,9},{11,1... | collective-permute-start | bytes 811016 | tf_op jit(solution)/shard_map/ppermute | solution.py:20
  3.6 4.2 %collective-permute-start = (bf16[528,256]{1,0:T(8,128)(2,1)S(1)}, bf16[528,256]{1,0:T(8,128)(2,1)S(1)}, u32[]{:S(2)}, u32[]{:S(2)}) collective-permute-start(bf16[528,256]{1,0:T(8,128)(2,1)S(1)} %fusion.1), channel_id=1, source_target_pairs={{0,1},{1,2},{2,3},{3,4},{4,5},{5,6},{6,7},{7,8},{8,9},{9,10},{10,1... | collective-permute-start | bytes 811016 | tf_op jit(solution)/shard_map/ppermute | solution.py:20
  7.3 1.2 %copy-start.2 = (bf16[528,256]{1,0:T(8,128)(2,1)}, bf16[528,256]{1,0:T(8,128)(2,1)S(1)}, u32[]{:S(2)}) copy-start(bf16[528,256]{1,0:T(8,128)(2,1)S(1)} %collective-permute-done.1.pr_ref) | copy-start | bytes 811012
  7.8 0.7 %copy-start.3 = (bf16[528,256]{1,0:T(8,128)(2,1)}, bf16[528,256]{1,0:T(8,128)(2,1)S(1)}, u32[]{:S(2)}) copy-start(bf16[528,256]{1,0:T(8,128)(2,1)S(1)} %collective-permute-done.pl_ref) | copy-start | bytes 811012
  15.2 9.9 %collective-permute-start.3 = (f32[128,640]{1,0:T(8,128)S(1)}, f32[128,640]{1,0:T(8,128)S(1)}, u32[]{:S(2)}, u32[]{:S(2)}) collective-permute-start(f32[128,640]{1,0:T(8,128)S(1)} %get-tuple-element.20), channel_id=1, source_target_pairs={{0,1},{1,2},{2,3},{3,4},{4,5},{5,6},{6,7},{7,8},{8,9},{9,10},{10,1... | collective-permute-start | bytes 983048 | tf_op jit(solution)/shard_map/ppermute | solution.py:20
  23.9 5.5 %collective-permute-start.2 = (f32[128,640]{1,0:T(8,128)S(1)}, f32[128,640]{1,0:T(8,128)S(1)}, u32[]{:S(2)}, u32[]{:S(2)}) collective-permute-start(f32[128,640]{1,0:T(8,128)S(1)} %get-tuple-element.21), channel_id=1, source_target_pairs={{1,0},{2,1},{3,2},{4,3},{5,4},{6,5},{7,6},{8,7},{9,8},{10,9},{11,1... | collective-permute-start | bytes 983048 | tf_op jit(solution)/shard_map/ppermute | solution.py:20
  29.4 18.4 %collective-permute-start.4 = (bf16[1,128,896]{2,1,0:T(8,128)(2,1)S(1)}, bf16[1,128,896]{2,1,0:T(8,128)(2,1)S(1)}, u32[]{:S(2)}, u32[]{:S(2)}) collective-permute-start(bf16[1,128,896]{2,1,0:T(8,128)(2,1)S(1)} %fusion.2), channel_id=1, source_target_pairs={{0,16},{16,0},{1,17},{17,1},{2,18},{18,2},{3,19},{19,3},{4,20},{20... | collective-permute-start | bytes 688136 | tf_op jit(solution)/shard_map/ppermute | solution.py:24

commit v4 on v3

--- a/solution.py
+++ b/solution.py
@@ -105,24 +105,34 @@
     partial_value = products(lc, pc, po, a_blocks, from_left, p_blocks, from_right)
 
     partial_value = partial_value.reshape(3, NC * B, 5 * NC * B)
-    from_right_p = shifted(partial_value[0], LINE, -1)
-    from_left_p = shifted(partial_value[2], LINE, 1)
+    n_grp, n_dev = lax.axis_size("grp"), lax.axis_size("dev")
+    n = n_grp * n_dev
+    group = lax.axis_index("grp")
+
+    def moved(x, rows_of):
+        outs = []
+        for delta in range(n_grp):
+            pairs = []
+            for src in range(n):
+                dst = rows_of(src)
+                if 0 <= dst < n:
+                    pairs.append((src, (dst // n_dev + delta) % n_grp * n_dev + dst % n_dev))
+            outs.append(lax.ppermute(x, LINE, pairs) if pairs != [(i, i) for i in range(n)] else x)
+        return outs
+
+    own = moved(partial_value[1], lambda src: src)
+    from_next = moved(partial_value[0], lambda src: src - 1)
+    from_prev = moved(partial_value[2], lambda src: src + 1)
     span = NC * B
-    combined = jnp.pad(partial_value[1], ((0, 0), (span, span)))
-    combined = combined + jnp.pad(from_right_p, ((0, 0), (2 * span, 0)))
-    combined = combined + jnp.pad(from_left_p, ((0, 0), (0, 2 * span)))
-    rows_here = combined.astype(jnp.bfloat16)[None]
-    group = lax.axis_index("grp")
-    joined = rows_here
-    for section_bit in range(lax.axis_size("grp").bit_length() - 1):
-        partner = partner_2(joined, "grp", section_bit)
-        is_upper = group // 2**section_bit % 2 == 1
-        joined = jnp.where(
-            is_upper,
-            jnp.concatenate([partner, joined], axis=0),
-            jnp.concatenate([joined, partner], axis=0),
-        )
-    return joined
+    stacked = []
+    for delta in range(n_grp):
+        combined = jnp.pad(own[delta], ((0, 0), (span, span)))
+        combined = combined + jnp.pad(from_next[delta], ((0, 0), (2 * span, 0)))
+        combined = combined + jnp.pad(from_prev[delta], ((0, 0), (0, 2 * span)))
+        stacked.append(combined.astype(jnp.bfloat16))
+    stacked = jnp.stack(stacked)
+    order = (group - jnp.arange(n_grp, dtype=jnp.int32)) % n_grp
+    return jnp.take(stacked, order, axis=0)
 
 
 def solution(mesh):

time: 48.9 us -> 57.4 us (1.17)
  waiting for transfers between devices: 8.69 us -> 15.9 us
  local copies, waits for them, and re-layouts: 2.05 us -> 2.67 us
    ppermute x1 -> x5, waiting for transfers between devices: 4 us -> 15.4 us  [moved(): lax.ppermute(x, LINE, pairs)]
    ppermute x1 -> x5, starting transfers between devices: 14.4 us -> 24.7 us  [moved(): lax.ppermute(x, LINE, pairs)]
    ppermute x4 -> x2, starting transfers between devices: 14.2 us -> 4.34 us  [shifted(): return lax.ppermute(x, axis, pairs)]
    ppermute x4 -> x2, waiting for transfers between devices: 4.69 us -> 0.52 us  [shifted(): return lax.ppermute(x, axis, pairs)]
    gather x0 -> x1, local copies, waits for them, and re-layouts: none -> 0.62 us  [local(): return jnp.take(stacked, order, axis=0)]
  transfers between devices with their start and end apart: 5 -> 7, of which waited for: 3 -> 2; matrix products, arithmetic and copies ran while one was open for 1% -> 1% of each run, Pallas kernels for 0% -> 0%
where the time goes in v4:
time: 57.4 us; the launch traced here: 57 us
  starting transfers between devices  29 us (51%)
  waiting for transfers between devices  15.9 us (28%)
  Pallas kernels  5.44 us (9%)
  other arithmetic  3.9 us (7%)
  local copies, waits for them, and re-layouts  2.67 us (5%)
    ppermute x5, starting transfers between devices, moved(): lax.ppermute(x, LINE, pairs)  24.7 us
    ppermute x5, waiting for transfers between devices, moved(): lax.ppermute(x, LINE, pairs)  15.4 us
    pallas_call x1, Pallas kernels, products(): pl.pallas_call(product_kernel, out_shape=jax.ShapeDtypeStruct((3 * NC * B...  5.44 us
    ppermute x2, starting transfers between devices, shifted(): return lax.ppermute(x, axis, pairs)  4.34 us
    slice x1, local copies, waits for them, and re-layouts, local(): own = moved(partial_value[1], lambda src: src)  1.23 us
  transfers between devices with their start and end apart: 7, of which 2 were waited for; matrix products, arithmetic and copies ran while one was open for 1% of the time, Pallas kernels for 0%

profile of v4, /device:TPU:0, one launch (start us, length us, event | category | flops | bytes accessed | tf_op | source)
XLA Modules:
  0.0 57.0 jit_solution(578196557872058702)
XLA Ops:
  0.0 0.0 copy-start.1
  0.0 0.7 %copy-done.1 = s32[8,4]{0,1:T(4,128)S(1)} copy-done((s32[8,4]{0,1:T(4,128)S(1)}, s32[8,4]{0,1:T(4,128)}, u32[]{:S(2)}) %copy-start.1) | copy-done | bytes 152
  0.7 0.1 copy.11
  0.8 0.6 %fusion.7 = (bf16[8,4]{1,0:T(8,128)(2,1)S(1)}, s32[8,4]{1,0:T(8,128)}, s32[8,4]{1,0:T(8,128)S(1)}) fusion(s32[8,4]{1,0:T(8,128)S(1)} %copy.11, s32[]{:T(128)S(6)} %mul.15, s32[]{:T(128)S(6)} %mul.16), kind=kLoop, calls=%fused_computation.29 | loop fusion | flops 96 | bytes 456 | tf_op jit(solution)/shard_map/convert_element_type | solution.py:93
  1.4 0.0 copy-start
  1.4 1.0 %fusion.1 = bf16[528,256]{1,0:T(8,128)(2,1)S(1)} fusion(bf16[8,4]{1,0:T(8,128)(2,1)S(1)} %get-tuple-element.17, bf16[512,256]{1,0:T(8,128)(2,1)} %pm_ref.1), kind=kLoop, calls=%fused_computation.7 | loop fusion | flops 811008 | bytes 532544 | tf_op jit(solution)/shard_map/concatenate | solution.py:95
  2.3 1.3 %collective-permute-start.1 = (bf16[528,256]{1,0:T(8,128)(2,1)S(1)}, bf16[528,256]{1,0:T(8,128)(2,1)S(1)}, u32[]{:S(2)}, u32[]{:S(2)}) collective-permute-start(bf16[528,256]{1,0:T(8,128)(2,1)S(1)} %fusion.1), channel_id=1, source_target_pairs={{1,0},{2,1},{3,2},{4,3},{5,4},{6,5},{7,6},{8,7},{9,8},{10,9},{11,1... | collective-permute-start | bytes 811016 | tf_op jit(solution)/shard_map/ppermute | solution.py:20
  3.6 3.0 %collective-permute-start = (bf16[528,256]{1,0:T(8,128)(2,1)S(1)}, bf16[528,256]{1,0:T(8,128)(2,1)S(1)}, u32[]{:S(2)}, u32[]{:S(2)}) collective-permute-start(bf16[528,256]{1,0:T(8,128)(2,1)S(1)} %fusion.1), channel_id=1, source_target_pairs={{0,1},{1,2},{2,3},{3,4},{4,5},{5,6},{6,7},{7,8},{8,9},{9,10},{10,1... | collective-permute-start | bytes 811016 | tf_op jit(solution)/shard_map/ppermute | solution.py:20
  6.7 0.0 copy-done
  6.7 0.6 %broadcast_subtract_fusion.2.lc_ref = s32[8,12]{1,0:T(8,128)} fusion(s32[8,12]{1,0:T(8,128)S(1)} %copy-done, s32[]{:T(128)S(6)} %mul.14), kind=kLoop, calls=%fused_computation.22 | loop fusion | flops 96 | bytes 772 | tf_op jit(solution)/shard_map/sub | solution.py:103
  7.3 0.0 collective-permute-done.1.pr_ref
  7.3 0.0 copy-start.2
  7.3 0.5 collective-permute-done.pl_ref
  7.8 0.0 copy-start.3
  7.8 0.7 %pad_add_fusion.pc_ref = s32[24,4]{1,0:T(8,128)} fusion(s32[8,4]{1,0:T(8,128)S(1)} %convert_add_fusion, s32[8,4]{1,0:T(8,128)S(1)} %get-tuple-element.22, s32[8,4]{1,0:T(8,128)S(1)} %slice_convert_fusion), kind=kLoop, calls=%fused_computation.10 | loop fusion | flops 192 | bytes 768 | tf_op jit(solution)/shard_map/concatenate | solution.py:102
  8.5 0.0 copy-done.2
  8.5 0.0 copy-done.3
  8.6 5.4 %shard_map.46 = f32[384,640]{1,0:T(8,128)} custom-call(s32[8,12]{1,0:T(8,128)} %broadcast_subtract_fusion.2.lc_ref, s32[24,4]{1,0:T(8,128)} %pad_add_fusion.pc_ref, s32[8,4]{1,0:T(8,128)} %get-tuple-element.18.po_ref, bf16[512,768]{1,0:T(8,128)(2,1)} %a_ref.1, bf16[528,256]{1,0:T(8,128)(2,1)} %copy-done.3, bf16[512,256]{1,0:T(8,128)(2,1)} %pm_ref.1, ...), custom_call_target="tpu_custom_call" | custom-call | flops 754974720 | bytes 4194304 | tf_op jit(solution)/shard_map/pallas_call | solution.py:72
  14.0 1.2 %fusion.8 = (f32[128,640]{1,0:T(8,128)S(1)}, f32[128,640]{1,0:T(8,128)S(1)}, f32[128,640]{1,0:T(8,128)S(1)}) fusion(f32[384,640]{1,0:T(8,128)} %shard_map.46), kind=kLoop, calls=%fused_computation.30 | loop fusion | bytes 1966080 | tf_op jit(solution)/shard_map/slice | solution.py:123
  15.2 1.3 %collective-permute-start.2 = (f32[128,640]{1,0:T(8,128)S(1)}, f32[128,640]{1,0:T(8,128)S(1)}, u32[]{:S(2)}, u32[]{:S(2)}) collective-permute-start(f32[128,640]{1,0:T(8,128)S(1)} %get-tuple-element.21), channel_id=1, source_target_pairs={{1,0},{2,1},{3,2},{4,3},{5,4},{6,5},{7,6},{8,7},{9,8},{10,9},{11,1... | collective-permute-start | bytes 983048 | tf_op jit(solution)/shard_map/ppermute | solution.py:120
  16.5 9.2 %collective-permute-start.3 = (f32[128,640]{1,0:T(8,128)S(1)}, f32[128,640]{1,0:T(8,128)S(1)}, u32[]{:S(2)}, u32[]{:S(2)}) collective-permute-start(f32[128,640]{1,0:T(8,128)S(1)} %get-tuple-element.20), channel_id=1, source_target_pairs={{0,1},{1,2},{2,3},{3,4},{4,5},{5,6},{6,7},{7,8},{8,9},{9,10},{10,1... | collective-permute-start | bytes 983048 | tf_op jit(solution)/shard_map/ppermute | solution.py:120
  25.8 1.3 %collective-permute-start.5 = (f32[128,640]{1,0:T(8,128)S(1)}, f32[128,640]{1,0:T(8,128)S(1)}, u32[]{:S(2)}, u32[]{:S(2)}) collective-permute-start(f32[128,640]{1,0:T(8,128)S(1)} %get-tuple-element.21), channel_id=1, source_target_pairs={{1,16},{2,17},{3,18},{4,19},{5,20},{6,21},{7,22},{8,23},{9,24},{10... | collective-permute-start | bytes 983048 | tf_op jit(solution)/shard_map/ppermute | solution.py:120
  27.1 10.6 %collective-permute-start.6 = (f32[128,640]{1,0:T(8,128)S(1)}, f32[128,640]{1,0:T(8,128)S(1)}, u32[]{:S(2)}, u32[]{:S(2)}) collective-permute-start(f32[128,640]{1,0:T(8,128)S(1)} %get-tuple-element.20), channel_id=1, source_target_pairs={{0,17},{1,18},{2,19},{3,20},{4,21},{5,22},{6,23},{7,24},{8,25},{9,... | collective-permute-start | bytes 983048 | tf_op jit(solution)/shard_map/ppermute | solution.py:120
  37.7 2.2 %collective-permute-start.4 = (f32[128,640]{1,0:T(8,128)S(1)}, f32[128,640]{1,0:T(8,128)S(1)}, u32[]{:S(2)}, u32[]{:S(2)}) collective-permute-start(f32[128,640]{1,0:T(8,128)S(1)} %get-tuple-element.19), channel_id=1, source_target_pairs={{0,16},{1,17},{2,18},{3,19},{4,20},{5,21},{6,22},{7,23},{8,24},{9,... | collective-permute-start | bytes 983048 | tf_op jit(solution)/shard_map/ppermute | solution.py:120
  40.0 0.0 collective-permute-done.2
  40.0 0.0 collective-permute-done.3
  40.0 15.4 %collective-permute-done.4 = f32[128,640]{1,0:T(8,128)S(1)} collective-permute-done((f32[128,640]{1,0:T(8,128)S(1)}, f32[128,640]{1,0:T(8,128)S(1)}, u32[]{:S(2)}, u32[]{:S(2)}) %collective-permute-start.4) | collective-permute-done | bytes 327712 | tf_op jit(solution)/shard_map/ppermute | solution.py:120
  55.4 0.0 collective-permute-done.5
  55.4 0.0 collective-permute-done.6
  55.5 0.1 pad_maximum_fusion
  55.5 0.6 %gather_fusion = bf16[2,128,896]{2,1,0:T(8,128)(2,1)S(1)} fusion(bf16[2,128,896]{2,1,0:T(8,128)(2,1)S(1)} %pad_maximum_fusion, s32[1024]{0:T(1024)S(1)} %pad_clamp_fusion), kind=kCustom, calls=%fused_computation | custom fusion | bytes 917512 | tf_op jit(solution)/shard_map/jit(_take)/gather | solution.py:135
  56.2 0.9 %broadcast_select_fusion = bf16[2,128,896]{2,1,0:T(8,128)(2,1)} fusion(bf16[2,128,896]{2,1,0:T(8,128)(2,1)S(1)} %gather_fusion, pred[2]{0:T(512)(128)(4,1)S(1)} %compare_and_fusion), kind=kLoop, calls=%fused_computation.6 | loop fusion | flops 229376 | bytes 917506 | tf_op jit(solution)/shard_map/jit(_take)/select_n | solution.py:135
  (7 shorter events, 0.1 us)
Async XLA Ops:
  0.0 0.7 %copy-start.1 = (s32[8,4]{0,1:T(4,128)S(1)}, s32[8,4]{0,1:T(4,128)}, u32[]{:S(2)}) copy-start(s32[8,4]{0,1:T(4,128)} %param.9) | copy-start | bytes 388
  1.4 5.3 %copy-start = (s32[8,12]{1,0:T(8,128)S(1)}, s32[8,12]{1,0:T(8,128)}, u32[]{:S(2)}) copy-start(s32[8,12]{1,0:T(8,128)} %param.7) | copy-start | bytes 1156
  2.3 5.0 %collective-permute-start.1 = (bf16[528,256]{1,0:T(8,128)(2,1)S(1)}, bf16[528,256]{1,0:T(8,128)(2,1)S(1)}, u32[]{:S(2)}, u32[]{:S(2)}) collective-permute-start(bf16[528,256]{1,0:T(8,128)(2,1)S(1)} %fusion.1), channel_id=1, source_target_pairs={{1,0},{2,1},{3,2},{4,3},{5,4},{6,5},{7,6},{8,7},{9,8},{10,9},{11,1... | collective-permute-start | bytes 811016 | tf_op jit(solution)/shard_map/ppermute | solution.py:20
  3.6 4.2 %collective-permute-start = (bf16[528,256]{1,0:T(8,128)(2,1)S(1)}, bf16[528,256]{1,0:T(8,128)(2,1)S(1)}, u32[]{:S(2)}, u32[]{:S(2)}) collective-permute-start(bf16[528,256]{1,0:T(8,128)(2,1)S(1)} %fusion.1), channel_id=1, source_target_pairs={{0,1},{1,2},{2,3},{3,4},{4,5},{5,6},{6,7},{7,8},{8,9},{9,10},{10,1... | collective-permute-start | bytes 811016 | tf_op jit(solution)/shard_map/ppermute | solution.py:20
  7.3 1.2 %copy-start.2 = (bf16[528,256]{1,0:T(8,128)(2,1)}, bf16[528,256]{1,0:T(8,128)(2,1)S(1)}, u32[]{:S(2)}) copy-start(bf16[528,256]{1,0:T(8,128)(2,1)S(1)} %collective-permute-done.1.pr_ref) | copy-start | bytes 811012
  7.8 0.7 %copy-start.3 = (bf16[528,256]{1,0:T(8,128)(2,1)}, bf16[528,256]{1,0:T(8,128)(2,1)S(1)}, u32[]{:S(2)}) copy-start(bf16[528,256]{1,0:T(8,128)(2,1)S(1)} %collective-permute-done.pl_ref) | copy-start | bytes 811012
  15.2 24.7 %collective-permute-start.2 = (f32[128,640]{1,0:T(8,128)S(1)}, f32[128,640]{1,0:T(8,128)S(1)}, u32[]{:S(2)}, u32[]{:S(2)}) collective-permute-start(f32[128,640]{1,0:T(8,128)S(1)} %get-tuple-element.21), channel_id=1, source_target_pairs={{1,0},{2,1},{3,2},{4,3},{5,4},{6,5},{7,6},{8,7},{9,8},{10,9},{11,1... | collective-permute-start | bytes 983048 | tf_op jit(solution)/shard_map/ppermute | solution.py:120
  16.5 23.4 %collective-permute-start.3 = (f32[128,640]{1,0:T(8,128)S(1)}, f32[128,640]{1,0:T(8,128)S(1)}, u32[]{:S(2)}, u32[]{:S(2)}) collective-permute-start(f32[128,640]{1,0:T(8,128)S(1)} %get-tuple-element.20), channel_id=1, source_target_pairs={{0,1},{1,2},{2,3},{3,4},{4,5},{5,6},{6,7},{7,8},{8,9},{9,10},{10,1... | collective-permute-start | bytes 983048 | tf_op jit(solution)/shard_map/ppermute | solution.py:120
  25.8 29.6 %collective-permute-start.5 = (f32[128,640]{1,0:T(8,128)S(1)}, f32[128,640]{1,0:T(8,128)S(1)}, u32[]{:S(2)}, u32[]{:S(2)}) collective-permute-start(f32[128,640]{1,0:T(8,128)S(1)} %get-tuple-element.21), channel_id=1, source_target_pairs={{1,16},{2,17},{3,18},{4,19},{5,20},{6,21},{7,22},{8,23},{9,24},{10... | collective-permute-start | bytes 983048 | tf_op jit(solution)/shard_map/ppermute | solution.py:120
  27.1 28.3 %collective-permute-start.6 = (f32[128,640]{1,0:T(8,128)S(1)}, f32[128,640]{1,0:T(8,128)S(1)}, u32[]{:S(2)}, u32[]{:S(2)}) collective-permute-start(f32[128,640]{1,0:T(8,128)S(1)} %get-tuple-element.20), channel_id=1, source_target_pairs={{0,17},{1,18},{2,19},{3,20},{4,21},{5,22},{6,23},{7,24},{8,25},{9,... | collective-permute-start | bytes 983048 | tf_op jit(solution)/shard_map/ppermute | solution.py:120
  37.7 17.7 %collective-permute-start.4 = (f32[128,640]{1,0:T(8,128)S(1)}, f32[128,640]{1,0:T(8,128)S(1)}, u32[]{:S(2)}, u32[]{:S(2)}) collective-permute-start(f32[128,640]{1,0:T(8,128)S(1)} %get-tuple-element.19), channel_id=1, source_target_pairs={{0,16},{1,17},{2,18},{3,19},{4,20},{5,21},{6,22},{7,23},{8,24},{9,... | collective-permute-start | bytes 983048 | tf_op jit(solution)/shard_map/ppermute | solution.py:120

commit v5 on v3

--- a/solution.py
+++ b/solution.py
@@ -32,7 +32,9 @@
     return pl.ds(pl.multiple_of(r * B, B), B)
 
 
-def product_kernel(lc_ref, pc_ref, po_ref, a_ref, pl_ref, pm_ref, pr_ref, out_ref, ps_ref, panel_ref, ap_ref, st_ref):
+def product_kernel(
+    lc_ref, pc_ref, po_ref, a_ref, pl_ref, pm_ref, pr_ref, prev_ref, here_ref, next_ref, ps_ref, panel_ref, ap_ref, st_ref
+):
     side = lax.broadcasted_iota(jnp.int32, (B, HALF), 1) // B
     ps_ref[...] = jnp.zeros(ps_ref.shape, ps_ref.dtype)
     sources = (pl_ref, pm_ref, pr_ref)
@@ -60,9 +62,13 @@
             dest = rows_at(po_ref[i, l])
             cur = st_ref[dest, cols]
             st_ref[dest, cols] = jnp.where(side == i % 2, pt[l * B : (l + 1) * B, cols], cur)
-    out_ref[...] = jnp.dot(
-        st_ref[...].astype(jnp.bfloat16), ap_ref[...], preferred_element_type=jnp.float32
-    )
+    span = NC * B
+    for o, out_ref in enumerate((prev_ref, here_ref, next_ref)):
+        out_ref[...] = jnp.dot(
+            st_ref[o * span : (o + 1) * span, :].astype(jnp.bfloat16),
+            ap_ref[...],
+            preferred_element_type=jnp.float32,
+        )
 
 
 def products(lc, pc, po, a_blocks, left, own, right):
@@ -71,9 +77,9 @@
     near = 3 * RB * B
     return pl.pallas_call(
         product_kernel,
-        out_shape=jax.ShapeDtypeStruct((3 * NC * B, 5 * NC * B), jnp.float32),
+        out_shape=[jax.ShapeDtypeStruct((NC * B, 5 * NC * B), jnp.float32)] * 3,
         in_specs=[smem] * 3 + [vmem] * 4,
-        out_specs=vmem,
+        out_specs=[vmem] * 3,
         scratch_shapes=[
             pltpu.VMEM((near, 5 * NC * B), jnp.bfloat16),
             pltpu.VMEM((KA * B, 5 * NC * B), jnp.bfloat16),
@@ -90,25 +96,18 @@
 
 def local(a_blocks, a_cols, p_blocks, p_cols):
     q = lax.axis_index(LINE)
-    rel = (p_cols - (q - 1) * NC).astype(jnp.bfloat16)
-    tag = jnp.zeros((16, KP * B), jnp.bfloat16).at[:RB, :KP].set(rel)
-    payload = jnp.concatenate([p_blocks, tag], axis=0)
-    from_left = shifted(payload, LINE, 1)
-    from_right = shifted(payload, LINE, -1)
-
-    def cols(x, shift):
-        return x[RB * B : RB * B + RB, :KP].astype(jnp.int32) + shift
-
-    pc = jnp.concatenate([cols(from_left, 0), p_cols - (q - 2) * NC, cols(from_right, 2 * NC)], axis=0)
+    from_left = shifted(p_blocks, LINE, 1)
+    from_right = shifted(p_blocks, LINE, -1)
+    rel = p_cols - (q - 1) * NC
+    cols_left = shifted(rel, LINE, 1)
+    cols_right = shifted(rel, LINE, -1)
+    pc = jnp.concatenate([cols_left, rel + NC, cols_right + 2 * NC], axis=0)
     lc = a_cols - (q - 1) * RB
-    po = p_cols - (q - 1) * NC
-    partial_value = products(lc, pc, po, a_blocks, from_left, p_blocks, from_right)
-
-    partial_value = partial_value.reshape(3, NC * B, 5 * NC * B)
-    from_right_p = shifted(partial_value[0], LINE, -1)
-    from_left_p = shifted(partial_value[2], LINE, 1)
+    prev_rows, here_rows, next_rows = products(lc, pc, rel, a_blocks, from_left, p_blocks, from_right)
+    from_right_p = shifted(prev_rows, LINE, -1)
+    from_left_p = shifted(next_rows, LINE, 1)
     span = NC * B
-    combined = jnp.pad(partial_value[1], ((0, 0), (span, span)))
+    combined = jnp.pad(here_rows, ((0, 0), (span, span)))
     combined = combined + jnp.pad(from_right_p, ((0, 0), (2 * span, 0)))
     combined = combined + jnp.pad(from_left_p, ((0, 0), (0, 2 * span)))
     rows_here = combined.astype(jnp.bfloat16)[None]

time: 48.9 us -> 56.8 us (1.16)
  starting transfers between devices: 28.6 us -> 40.1 us
  waiting for transfers between devices: 8.69 us -> 6.54 us
  other arithmetic: 3.73 us -> 3.06 us
  local copies, waits for them, and re-layouts: 2.05 us -> 1.46 us
    ppermute x1, starting transfers between devices: 14.4 us -> 21 us  [partner_2(): lax.ppermute(x, axis, [(i, i ^ 1 << bit) for i in range(lax.axis_size(axi...]
    ppermute x4 -> x6, starting transfers between devices: 14.2 us -> 19 us  [shifted(): return lax.ppermute(x, axis, pairs)]
    ppermute x4 -> x6, waiting for transfers between devices: 4.69 us -> 2.54 us  [shifted(): return lax.ppermute(x, axis, pairs)]
    slice x1 -> x0, local copies, waits for them, and re-layouts: 1.23 us -> none  [local(): combined = jnp.pad(partial_value[1], ((0, 0), (span, span)))]
    concatenate x2 -> x1, other arithmetic: 1.63 us -> 0.6 us  [local(): pc = jnp.concatenate([cols_left, rel + NC, cols_right + 2 * NC], axis=0)]
    broadcast_in_dim x1, other arithmetic: 0.05 us -> 1.02 us  [local(): rows_here = combined.astype(jnp.bfloat16)[None]]
    unnamed x9 -> x11, local copies, waits for them, and re-layouts: 0.82 us -> 1.46 us
    convert_element_type x2 -> x0, other arithmetic: 0.6 us -> none  [the longest x1 0.6 us: local(): rel = (p_cols - (q - 1) * NC).astype(jnp.bfloat16)]
  transfers between devices with their start and end apart: 5 -> 7, of which waited for: 3 -> 3; matrix products, arithmetic and copies ran while one was open for 1% -> 2% of each run, Pallas kernels for 0% -> 0%
where the time goes in v5:
time: 56.8 us; the launch traced here: 56.5 us
  starting transfers between devices  40.1 us (71%)
  waiting for transfers between devices  6.54 us (12%)
  Pallas kernels  5.23 us (9%)
  other arithmetic  3.06 us (5%)
  local copies, waits for them, and re-layouts  1.46 us (3%)
    ppermute x1, starting transfers between devices, partner_2(): lax.ppermute(x, axis, [(i, i ^ 1 << bit) for i in range(lax.axis_size(axi...  21 us
    ppermute x6, starting transfers between devices, shifted(): return lax.ppermute(x, axis, pairs)  19 us
    pallas_call x1, Pallas kernels, products(): pl.pallas_call(product_kernel, out_shape=[jax.ShapeDtypeStruct((NC * B, 5...  5.23 us
    ppermute x1, waiting for transfers between devices, partner_2(): lax.ppermute(x, axis, [(i, i ^ 1 << bit) for i in range(lax.axis_size(axi...  4 us
    ppermute x6, waiting for transfers between devices, shifted(): return lax.ppermute(x, axis, pairs)  2.54 us
    unnamed x11, local copies, waits for them, and re-layouts  1.46 us
  transfers between devices with their start and end apart: 7, of which 3 were waited for; matrix products, arithmetic and copies ran while one was open for 2% of the time, Pallas kernels for 0%

profile of v5, /device:TPU:0, one launch (start us, length us, event | category | flops | bytes accessed | tf_op | source)
XLA Modules:
  0.0 56.5 jit_solution(10852504517138534830)
XLA Ops:
  0.0 0.0 copy-start.2
  0.0 0.7 %copy-done.2 = s32[8,4]{0,1:T(4,128)S(1)} copy-done((s32[8,4]{0,1:T(4,128)S(1)}, s32[8,4]{0,1:T(4,128)}, u32[]{:S(2)}) %copy-start.2) | copy-done | bytes 152
  0.7 0.1 copy.11
  0.8 0.0 copy-start.1
  0.8 0.0 copy-start
  0.8 1.4 %collective-permute-start.1 = (s32[8,4]{1,0:T(8,128)S(1)}, s32[8,4]{1,0:T(8,128)S(1)}, u32[]{:S(2)}, u32[]{:S(2)}) collective-permute-start(s32[8,4]{1,0:T(8,128)S(1)} %get-tuple-element.12.po_ref), channel_id=1, source_target_pairs={{1,0},{2,1},{3,2},{4,3},{5,4},{6,5},{7,6},{8,7},{9,8},{10,9},{11,1... | collective-permute-start | bytes 392 | tf_op jit(solution)/shard_map/ppermute | solution.py:20
  2.2 3.0 %collective-permute-start = (s32[8,4]{1,0:T(8,128)S(1)}, s32[8,4]{1,0:T(8,128)S(1)}, u32[]{:S(2)}, u32[]{:S(2)}) collective-permute-start(s32[8,4]{1,0:T(8,128)S(1)} %get-tuple-element.12.po_ref), channel_id=1, source_target_pairs={{0,1},{1,2},{2,3},{3,4},{4,5},{5,6},{6,7},{7,8},{8,9},{9,10},{10,1... | collective-permute-start | bytes 392 | tf_op jit(solution)/shard_map/ppermute | solution.py:20
  5.2 4.5 %collective-permute-start.2 = (bf16[512,256]{1,0:T(8,128)(2,1)}, bf16[512,256]{1,0:T(8,128)(2,1)S(1)}, u32[]{:S(2)}, u32[]{:S(2)}) collective-permute-start(bf16[512,256]{1,0:T(8,128)(2,1)} %pm_ref.1), channel_id=1, source_target_pairs={{0,1},{1,2},{2,3},{3,4},{4,5},{5,6},{6,7},{7,8},{8,9},{9,10},{10,1... | collective-permute-start | bytes 786440 | tf_op jit(solution)/shard_map/ppermute | solution.py:20
  9.8 1.3 %collective-permute-start.3 = (bf16[512,256]{1,0:T(8,128)(2,1)}, bf16[512,256]{1,0:T(8,128)(2,1)S(1)}, u32[]{:S(2)}, u32[]{:S(2)}) collective-permute-start(bf16[512,256]{1,0:T(8,128)(2,1)} %pm_ref.1), channel_id=1, source_target_pairs={{1,0},{2,1},{3,2},{4,3},{5,4},{6,5},{7,6},{8,7},{9,8},{10,9},{11,1... | collective-permute-start | bytes 786440 | tf_op jit(solution)/shard_map/ppermute | solution.py:20
  11.1 0.0 copy-done.1
  11.1 0.6 %broadcast_subtract_fusion.1.lc_ref = s32[8,12]{1,0:T(8,128)} fusion(s32[8,12]{1,0:T(8,128)S(1)} %copy-done.1, s32[]{:T(128)S(6)} %mul.10), kind=kLoop, calls=%fused_computation.7 | loop fusion | flops 96 | bytes 772 | tf_op jit(solution)/shard_map/sub | solution.py:105
  11.7 0.0 copy-done
  11.7 0.0 collective-permute-done.1
  11.7 0.0 collective-permute-done
  11.7 0.6 %pad_add_fusion.pc_ref = s32[24,4]{1,0:T(8,128)} fusion(s32[8,4]{1,0:T(8,128)S(1)} %broadcast_add_fusion, s32[8,4]{1,0:T(8,128)S(1)} %get-tuple-element.11, s32[8,4]{1,0:T(8,128)S(1)} %collective-permute-done), kind=kLoop, calls=%fused_computation.3 | loop fusion | flops 192 | bytes 768 | tf_op jit(solution)/shard_map/concatenate | solution.py:104
  12.3 0.0 collective-permute-done.2.pl_ref
  12.3 0.0 copy-start.3
  12.3 1.1 %collective-permute-done.3.pr_ref = bf16[512,256]{1,0:T(8,128)(2,1)S(1)} collective-permute-done((bf16[512,256]{1,0:T(8,128)(2,1)}, bf16[512,256]{1,0:T(8,128)(2,1)S(1)}, u32[]{:S(2)}, u32[]{:S(2)}) %collective-permute-start.3) | collective-permute-done | bytes 262176 | tf_op jit(solution)/shard_map/ppermute | solution.py:20
  13.4 0.0 copy-done.3
  13.4 0.0 copy-start.4
  13.4 0.7 %copy-done.4 = bf16[512,256]{1,0:T(8,128)(2,1)} copy-done((bf16[512,256]{1,0:T(8,128)(2,1)}, bf16[512,256]{1,0:T(8,128)(2,1)S(1)}, u32[]{:S(2)}) %copy-start.4) | copy-done | bytes 262168
  14.1 5.2 %shard_map.46 = (f32[128,640]{1,0:T(8,128)}, f32[128,640]{1,0:T(8,128)}, f32[128,640]{1,0:T(8,128)}) custom-call(s32[8,12]{1,0:T(8,128)} %broadcast_subtract_fusion.1.lc_ref, s32[24,4]{1,0:T(8,128)} %pad_add_fusion.pc_ref, s32[8,4]{1,0:T(8,128)} %copy-done, bf16[512,768]{1,0:T(8,128)(2,1)} %a_ref.1, bf16[512,256]{1,0:T(8,128)(2,1)} %copy-done.3, ...), custom_call_target="tpu_custom_call" | custom-call | flops 754974720 | bytes 4194304 | tf_op jit(solution)/shard_map/pallas_call | solution.py:78
  19.4 1.3 %collective-permute-start.4 = (f32[128,640]{1,0:T(8,128)}, f32[128,640]{1,0:T(8,128)S(1)}, u32[]{:S(2)}, u32[]{:S(2)}) collective-permute-start(f32[128,640]{1,0:T(8,128)} %get-tuple-element.9), channel_id=1, source_target_pairs={{1,0},{2,1},{3,2},{4,3},{5,4},{6,5},{7,6},{8,7},{9,8},{10,9},{11,1... | collective-permute-start | bytes 983048 | tf_op jit(solution)/shard_map/ppermute | solution.py:20
  20.6 7.5 %collective-permute-start.5 = (f32[128,640]{1,0:T(8,128)}, f32[128,640]{1,0:T(8,128)S(1)}, u32[]{:S(2)}, u32[]{:S(2)}) collective-permute-start(f32[128,640]{1,0:T(8,128)} %get-tuple-element.10), channel_id=1, source_target_pairs={{0,1},{1,2},{2,3},{3,4},{4,5},{5,6},{6,7},{7,8},{8,9},{9,10},{10,1... | collective-permute-start | bytes 983048 | tf_op jit(solution)/shard_map/ppermute | solution.py:20
  28.1 0.0 collective-permute-done.4
  28.1 1.4 %collective-permute-done.5 = f32[128,640]{1,0:T(8,128)S(1)} collective-permute-done((f32[128,640]{1,0:T(8,128)}, f32[128,640]{1,0:T(8,128)S(1)}, u32[]{:S(2)}, u32[]{:S(2)}) %collective-permute-start.5) | collective-permute-done | bytes 327712 | tf_op jit(solution)/shard_map/ppermute | solution.py:20
  29.6 1.0 %fusion = bf16[1,128,896]{2,1,0:T(8,128)(2,1)S(1)} fusion(f32[128,640]{1,0:T(8,128)S(1)} %collective-permute-done.5, f32[128,640]{1,0:T(8,128)S(1)} %collective-permute-done.4, f32[128,640]{1,0:T(8,128)} %get-tuple-element.8), kind=kLoop, calls=%fused_computation.2 | loop fusion | flops 344064 | bytes 1212416 | tf_op jit(solution)/shard_map/broadcast_in_dim | solution.py:113
  30.6 21.0 %collective-permute-start.6 = (bf16[1,128,896]{2,1,0:T(8,128)(2,1)S(1)}, bf16[1,128,896]{2,1,0:T(8,128)(2,1)S(1)}, u32[]{:S(2)}, u32[]{:S(2)}) collective-permute-start(bf16[1,128,896]{2,1,0:T(8,128)(2,1)S(1)} %fusion), channel_id=1, source_target_pairs={{0,16},{16,0},{1,17},{17,1},{2,18},{18,2},{3,19},{19,3},{4,20},{20... | collective-permute-start | bytes 688136 | tf_op jit(solution)/shard_map/ppermute | solution.py:24
  51.6 4.0 %collective-permute-done.6 = bf16[1,128,896]{2,1,0:T(8,128)(2,1)S(1)} collective-permute-done((bf16[1,128,896]{2,1,0:T(8,128)(2,1)S(1)}, bf16[1,128,896]{2,1,0:T(8,128)(2,1)S(1)}, u32[]{:S(2)}, u32[]{:S(2)}) %collective-permute-start.6) | collective-permute-done | bytes 229408 | tf_op jit(solution)/shard_map/ppermute | solution.py:24
  55.6 0.8 %maximum_select_fusion = bf16[2,128,896]{2,1,0:T(8,128)(2,1)} fusion(bf16[1,128,896]{2,1,0:T(8,128)(2,1)S(1)} %fusion, bf16[1,128,896]{2,1,0:T(8,128)(2,1)S(1)} %collective-permute-done.6, pred[]{:T(512)S(6)} %eq.5), kind=kLoop, calls=%fused_computation | loop fusion | flops 688128 | bytes 917505 | tf_op jit(solution)/shard_map/jit(_where)/select_n | solution.py:119
  (2 shorter events, 0.0 us)
Async XLA Ops:
  0.0 0.7 %copy-start.2 = (s32[8,4]{0,1:T(4,128)S(1)}, s32[8,4]{0,1:T(4,128)}, u32[]{:S(2)}) copy-start(s32[8,4]{0,1:T(4,128)} %param.7) | copy-start | bytes 388
  0.8 10.3 %copy-start.1 = (s32[8,12]{1,0:T(8,128)S(1)}, s32[8,12]{1,0:T(8,128)}, u32[]{:S(2)}) copy-start(s32[8,12]{1,0:T(8,128)} %param.5) | copy-start | bytes 1156
  0.8 10.9 %copy-start = (s32[8,4]{1,0:T(8,128)}, s32[8,4]{1,0:T(8,128)S(1)}, u32[]{:S(2)}) copy-start(s32[8,4]{1,0:T(8,128)S(1)} %get-tuple-element.12.po_ref) | copy-start | bytes 388
  0.8 10.9 %collective-permute-start.1 = (s32[8,4]{1,0:T(8,128)S(1)}, s32[8,4]{1,0:T(8,128)S(1)}, u32[]{:S(2)}, u32[]{:S(2)}) collective-permute-start(s32[8,4]{1,0:T(8,128)S(1)} %get-tuple-element.12.po_ref), channel_id=1, source_target_pairs={{1,0},{2,1},{3,2},{4,3},{5,4},{6,5},{7,6},{8,7},{9,8},{10,9},{11,1... | collective-permute-start | bytes 392 | tf_op jit(solution)/shard_map/ppermute | solution.py:20
  2.2 9.5 %collective-permute-start = (s32[8,4]{1,0:T(8,128)S(1)}, s32[8,4]{1,0:T(8,128)S(1)}, u32[]{:S(2)}, u32[]{:S(2)}) collective-permute-start(s32[8,4]{1,0:T(8,128)S(1)} %get-tuple-element.12.po_ref), channel_id=1, source_target_pairs={{0,1},{1,2},{2,3},{3,4},{4,5},{5,6},{6,7},{7,8},{8,9},{9,10},{10,1... | collective-permute-start | bytes 392 | tf_op jit(solution)/shard_map/ppermute | solution.py:20
  5.2 7.1 %collective-permute-start.2 = (bf16[512,256]{1,0:T(8,128)(2,1)}, bf16[512,256]{1,0:T(8,128)(2,1)S(1)}, u32[]{:S(2)}, u32[]{:S(2)}) collective-permute-start(bf16[512,256]{1,0:T(8,128)(2,1)} %pm_ref.1), channel_id=1, source_target_pairs={{0,1},{1,2},{2,3},{3,4},{4,5},{5,6},{6,7},{7,8},{8,9},{9,10},{10,1... | collective-permute-start | bytes 786440 | tf_op jit(solution)/shard_map/ppermute | solution.py:20
  9.8 3.6 %collective-permute-start.3 = (bf16[512,256]{1,0:T(8,128)(2,1)}, bf16[512,256]{1,0:T(8,128)(2,1)S(1)}, u32[]{:S(2)}, u32[]{:S(2)}) collective-permute-start(bf16[512,256]{1,0:T(8,128)(2,1)} %pm_ref.1), channel_id=1, source_target_pairs={{1,0},{2,1},{3,2},{4,3},{5,4},{6,5},{7,6},{8,7},{9,8},{10,9},{11,1... | collective-permute-start | bytes 786440 | tf_op jit(solution)/shard_map/ppermute | solution.py:20
  12.3 1.1 %copy-start.3 = (bf16[512,256]{1,0:T(8,128)(2,1)}, bf16[512,256]{1,0:T(8,128)(2,1)S(1)}, u32[]{:S(2)}) copy-start(bf16[512,256]{1,0:T(8,128)(2,1)S(1)} %collective-permute-done.2.pl_ref) | copy-start | bytes 786436
  13.4 0.7 %copy-start.4 = (bf16[512,256]{1,0:T(8,128)(2,1)}, bf16[512,256]{1,0:T(8,128)(2,1)S(1)}, u32[]{:S(2)}) copy-start(bf16[512,256]{1,0:T(8,128)(2,1)S(1)} %collective-permute-done.3.pr_ref) | copy-start | bytes 786436
  19.4 8.8 %collective-permute-start.4 = (f32[128,640]{1,0:T(8,128)}, f32[128,640]{1,0:T(8,128)S(1)}, u32[]{:S(2)}, u32[]{:S(2)}) collective-permute-start(f32[128,640]{1,0:T(8,128)} %get-tuple-element.9), channel_id=1, source_target_pairs={{1,0},{2,1},{3,2},{4,3},{5,4},{6,5},{7,6},{8,7},{9,8},{10,9},{11,1... | collective-permute-start | bytes 983048 | tf_op jit(solution)/shard_map/ppermute | solution.py:20
  20.6 8.9 %collective-permute-start.5 = (f32[128,640]{1,0:T(8,128)}, f32[128,640]{1,0:T(8,128)S(1)}, u32[]{:S(2)}, u32[]{:S(2)}) collective-permute-start(f32[128,640]{1,0:T(8,128)} %get-tuple-element.10), channel_id=1, source_target_pairs={{0,1},{1,2},{2,3},{3,4},{4,5},{5,6},{6,7},{7,8},{8,9},{9,10},{10,1... | collective-permute-start | bytes 983048 | tf_op jit(solution)/shard_map/ppermute | solution.py:20
  30.6 25.0 %collective-permute-start.6 = (bf16[1,128,896]{2,1,0:T(8,128)(2,1)S(1)}, bf16[1,128,896]{2,1,0:T(8,128)(2,1)S(1)}, u32[]{:S(2)}, u32[]{:S(2)}) collective-permute-start(bf16[1,128,896]{2,1,0:T(8,128)(2,1)S(1)} %fusion), channel_id=1, source_target_pairs={{0,16},{16,0},{1,17},{17,1},{2,18},{18,2},{3,19},{19,3},{4,20},{20... | collective-permute-start | bytes 688136 | tf_op jit(solution)/shard_map/ppermute | solution.py:24

commit v6 on v5

--- a/solution.py
+++ b/solution.py
@@ -96,12 +96,16 @@
 
 def local(a_blocks, a_cols, p_blocks, p_cols):
     q = lax.axis_index(LINE)
-    from_left = shifted(p_blocks, LINE, 1)
-    from_right = shifted(p_blocks, LINE, -1)
     rel = p_cols - (q - 1) * NC
-    cols_left = shifted(rel, LINE, 1)
-    cols_right = shifted(rel, LINE, -1)
-    pc = jnp.concatenate([cols_left, rel + NC, cols_right + 2 * NC], axis=0)
+    tag = jnp.zeros((16, KP * B), jnp.bfloat16).at[:RB, :KP].set(rel.astype(jnp.bfloat16))
+    payload = jnp.concatenate([p_blocks, tag], axis=0)
+    from_left = shifted(payload, LINE, 1)
+    from_right = shifted(payload, LINE, -1)
+
+    def cols(x, shift):
+        return x[RB * B : RB * B + RB, :KP].astype(jnp.int32) + shift
+
+    pc = jnp.concatenate([cols(from_left, 0), rel + NC, cols(from_right, 2 * NC)], axis=0)
     lc = a_cols - (q - 1) * RB
     prev_rows, here_rows, next_rows = products(lc, pc, rel, a_blocks, from_left, p_blocks, from_right)
     from_right_p = shifted(prev_rows, LINE, -1)

time: 56.8 us -> 48.3 us (0.85)
  starting transfers between devices: 40.1 us -> 31.9 us
  other arithmetic: 3.06 us -> 4.1 us
  local copies, waits for them, and re-layouts: 1.46 us -> 0.82 us
  waiting for transfers between devices: 6.54 us -> 5.94 us
    ppermute x6 -> x4, starting transfers between devices: 19 us -> 14.9 us  [shifted(): return lax.ppermute(x, axis, pairs)]
    ppermute x1, starting transfers between devices: 21 us -> 17 us  [partner_2(): lax.ppermute(x, axis, [(i, i ^ 1 << bit) for i in range(lax.axis_size(axi...]
    concatenate x1 -> x2, other arithmetic: 0.6 us -> 1.62 us  [the longest x1 0.97 us: local(): payload = jnp.concatenate([p_blocks, tag], axis=0)]
    unnamed x11, local copies, waits for them, and re-layouts: 1.46 us -> 0.82 us
    ppermute x6 -> x4, waiting for transfers between devices: 2.54 us -> 1.94 us  [shifted(): return lax.ppermute(x, axis, pairs)]
  transfers between devices with their start and end apart: 7 -> 5, of which waited for: 3 -> 3; matrix products, arithmetic and copies ran while one was open for 2% -> 1% of each run, Pallas kernels for 0% -> 0%
where the time goes in v6:
time: 48.3 us; the launch traced here: 48 us
  starting transfers between devices  31.9 us (66%)
  waiting for transfers between devices  5.94 us (12%)
  Pallas kernels  5.23 us (11%)
  other arithmetic  4.1 us (8%)
  local copies, waits for them, and re-layouts  0.82 us (2%)
    ppermute x1, starting transfers between devices, partner_2(): lax.ppermute(x, axis, [(i, i ^ 1 << bit) for i in range(lax.axis_size(axi...  17 us
    ppermute x4, starting transfers between devices, shifted(): return lax.ppermute(x, axis, pairs)  14.9 us
    pallas_call x1, Pallas kernels, products(): pl.pallas_call(product_kernel, out_shape=[jax.ShapeDtypeStruct((NC * B, 5...  5.23 us
    ppermute x1, waiting for transfers between devices, partner_2(): lax.ppermute(x, axis, [(i, i ^ 1 << bit) for i in range(lax.axis_size(axi...  4 us
    ppermute x4, waiting for transfers between devices, shifted(): return lax.ppermute(x, axis, pairs)  1.94 us
    broadcast_in_dim x1, other arithmetic, local(): rows_here = combined.astype(jnp.bfloat16)[None]  1.02 us
    concatenate x1, other arithmetic, local(): payload = jnp.concatenate([p_blocks, tag], axis=0)  0.97 us
  transfers between devices with their start and end apart: 5, of which 3 were waited for; matrix products, arithmetic and copies ran while one was open for 1% of the time, Pallas kernels for 0%

profile of v6, /device:TPU:0, one launch (start us, length us, event | category | flops | bytes accessed | tf_op | source)
XLA Modules:
  0.0 48.0 jit_solution(13396270892689958432)
XLA Ops:
  0.0 0.0 copy-start.2
  0.0 0.7 %copy-done.2 = s32[8,4]{0,1:T(4,128)S(1)} copy-done((s32[8,4]{0,1:T(4,128)S(1)}, s32[8,4]{0,1:T(4,128)}, u32[]{:S(2)}) %copy-start.2) | copy-done | bytes 152
  0.7 0.1 copy.11
  0.8 0.0 copy-start
  0.8 0.0 copy-start.1
  0.8 1.0 %fusion.1 = bf16[528,256]{1,0:T(8,128)(2,1)S(1)} fusion(bf16[8,4]{1,0:T(8,128)(2,1)S(1)} %convert_element_type.18, bf16[512,256]{1,0:T(8,128)(2,1)} %pm_ref.1), kind=kLoop, calls=%fused_computation.4 | loop fusion | flops 811008 | bytes 532544 | tf_op jit(solution)/shard_map/concatenate | solution.py:101
  1.8 0.0 copy-done
  1.8 1.3 %collective-permute-start.1 = (bf16[528,256]{1,0:T(8,128)(2,1)S(1)}, bf16[528,256]{1,0:T(8,128)(2,1)S(1)}, u32[]{:S(2)}, u32[]{:S(2)}) collective-permute-start(bf16[528,256]{1,0:T(8,128)(2,1)S(1)} %fusion.1), channel_id=1, source_target_pairs={{1,0},{2,1},{3,2},{4,3},{5,4},{6,5},{7,6},{8,7},{9,8},{10,9},{11,1... | collective-permute-start | bytes 811016 | tf_op jit(solution)/shard_map/ppermute | solution.py:20
  3.1 3.0 %collective-permute-start = (bf16[528,256]{1,0:T(8,128)(2,1)S(1)}, bf16[528,256]{1,0:T(8,128)(2,1)S(1)}, u32[]{:S(2)}, u32[]{:S(2)}) collective-permute-start(bf16[528,256]{1,0:T(8,128)(2,1)S(1)} %fusion.1), channel_id=1, source_target_pairs={{0,1},{1,2},{2,3},{3,4},{4,5},{5,6},{6,7},{7,8},{8,9},{9,10},{10,1... | collective-permute-start | bytes 811016 | tf_op jit(solution)/shard_map/ppermute | solution.py:20
  6.1 0.0 copy-done.1
  6.1 0.6 %broadcast_subtract_fusion.1.lc_ref = s32[8,12]{1,0:T(8,128)} fusion(s32[8,12]{1,0:T(8,128)S(1)} %copy-done.1, s32[]{:T(128)S(6)} %mul.10), kind=kLoop, calls=%fused_computation.11 | loop fusion | flops 96 | bytes 772 | tf_op jit(solution)/shard_map/sub | solution.py:109
  6.7 0.0 collective-permute-done.1.pr_ref
  6.7 0.0 copy-start.3
  6.7 0.5 %collective-permute-done.pl_ref = bf16[528,256]{1,0:T(8,128)(2,1)S(1)} collective-permute-done((bf16[528,256]{1,0:T(8,128)(2,1)S(1)}, bf16[528,256]{1,0:T(8,128)(2,1)S(1)}, u32[]{:S(2)}, u32[]{:S(2)}) %collective-permute-start) | collective-permute-done | bytes 270368 | tf_op jit(solution)/shard_map/ppermute | solution.py:20
  7.3 0.0 copy-start.4
  7.3 0.7 %pad_add_fusion.pc_ref = s32[24,4]{1,0:T(8,128)} fusion(s32[8,4]{1,0:T(8,128)S(1)} %convert_add_fusion, s32[8,4]{1,0:T(8,128)S(1)} %get-tuple-element.23, s32[8,4]{1,0:T(8,128)S(1)} %slice_convert_fusion), kind=kLoop, calls=%fused_computation.6 | loop fusion | flops 192 | bytes 768 | tf_op jit(solution)/shard_map/concatenate | solution.py:108
  7.9 0.0 copy-done.3
  7.9 0.0 copy-done.4
  8.0 5.2 %shard_map.46 = (f32[128,640]{1,0:T(8,128)}, f32[128,640]{1,0:T(8,128)}, f32[128,640]{1,0:T(8,128)}) custom-call(s32[8,12]{1,0:T(8,128)} %broadcast_subtract_fusion.1.lc_ref, s32[24,4]{1,0:T(8,128)} %pad_add_fusion.pc_ref, s32[8,4]{1,0:T(8,128)} %copy-done, bf16[512,768]{1,0:T(8,128)(2,1)} %a_ref.1, bf16[528,256]{1,0:T(8,128)(2,1)} %copy-done.4, ...), custom_call_target="tpu_custom_call" | custom-call | flops 754974720 | bytes 4194304 | tf_op jit(solution)/shard_map/pallas_call | solution.py:78
  13.2 1.3 %collective-permute-start.2 = (f32[128,640]{1,0:T(8,128)}, f32[128,640]{1,0:T(8,128)S(1)}, u32[]{:S(2)}, u32[]{:S(2)}) collective-permute-start(f32[128,640]{1,0:T(8,128)} %get-tuple-element.21), channel_id=1, source_target_pairs={{1,0},{2,1},{3,2},{4,3},{5,4},{6,5},{7,6},{8,7},{9,8},{10,9},{11,1... | collective-permute-start | bytes 983048 | tf_op jit(solution)/shard_map/ppermute | solution.py:20
  14.5 9.2 %collective-permute-start.3 = (f32[128,640]{1,0:T(8,128)}, f32[128,640]{1,0:T(8,128)S(1)}, u32[]{:S(2)}, u32[]{:S(2)}) collective-permute-start(f32[128,640]{1,0:T(8,128)} %get-tuple-element.22), channel_id=1, source_target_pairs={{0,1},{1,2},{2,3},{3,4},{4,5},{5,6},{6,7},{7,8},{8,9},{9,10},{10,1... | collective-permute-start | bytes 983048 | tf_op jit(solution)/shard_map/ppermute | solution.py:20
  23.7 0.0 collective-permute-done.2
  23.8 1.4 %collective-permute-done.3 = f32[128,640]{1,0:T(8,128)S(1)} collective-permute-done((f32[128,640]{1,0:T(8,128)}, f32[128,640]{1,0:T(8,128)S(1)}, u32[]{:S(2)}, u32[]{:S(2)}) %collective-permute-start.3) | collective-permute-done | bytes 327712 | tf_op jit(solution)/shard_map/ppermute | solution.py:20
  25.2 1.0 %fusion.2 = bf16[1,128,896]{2,1,0:T(8,128)(2,1)S(1)} fusion(f32[128,640]{1,0:T(8,128)S(1)} %collective-permute-done.3, f32[128,640]{1,0:T(8,128)S(1)} %collective-permute-done.2, f32[128,640]{1,0:T(8,128)} %get-tuple-element.20), kind=kLoop, calls=%fused_computation.5 | loop fusion | flops 344064 | bytes 1212416 | tf_op jit(solution)/shard_map/broadcast_in_dim | solution.py:117
  26.2 17.0 %collective-permute-start.4 = (bf16[1,128,896]{2,1,0:T(8,128)(2,1)S(1)}, bf16[1,128,896]{2,1,0:T(8,128)(2,1)S(1)}, u32[]{:S(2)}, u32[]{:S(2)}) collective-permute-start(bf16[1,128,896]{2,1,0:T(8,128)(2,1)S(1)} %fusion.2), channel_id=1, source_target_pairs={{0,16},{16,0},{1,17},{17,1},{2,18},{18,2},{3,19},{19,3},{4,20},{20... | collective-permute-start | bytes 688136 | tf_op jit(solution)/shard_map/ppermute | solution.py:24
  43.2 4.0 %collective-permute-done.4 = bf16[1,128,896]{2,1,0:T(8,128)(2,1)S(1)} collective-permute-done((bf16[1,128,896]{2,1,0:T(8,128)(2,1)S(1)}, bf16[1,128,896]{2,1,0:T(8,128)(2,1)S(1)}, u32[]{:S(2)}, u32[]{:S(2)}) %collective-permute-start.4) | collective-permute-done | bytes 229408 | tf_op jit(solution)/shard_map/ppermute | solution.py:24
  47.2 0.8 %maximum_select_fusion = bf16[2,128,896]{2,1,0:T(8,128)(2,1)} fusion(bf16[1,128,896]{2,1,0:T(8,128)(2,1)S(1)} %fusion.2, bf16[1,128,896]{2,1,0:T(8,128)(2,1)S(1)} %collective-permute-done.4, pred[]{:T(512)S(6)} %eq.5), kind=kLoop, calls=%fused_computation.2 | loop fusion | flops 688128 | bytes 917505 | tf_op jit(solution)/shard_map/jit(_where)/select_n | solution.py:123
  (4 shorter events, 0.0 us)
Async XLA Ops:
  0.0 0.7 %copy-start.2 = (s32[8,4]{0,1:T(4,128)S(1)}, s32[8,4]{0,1:T(4,128)}, u32[]{:S(2)}) copy-start(s32[8,4]{0,1:T(4,128)} %param.9) | copy-start | bytes 388
  0.8 1.0 %copy-start = (s32[8,4]{1,0:T(8,128)}, s32[8,4]{1,0:T(8,128)S(1)}, u32[]{:S(2)}) copy-start(s32[8,4]{1,0:T(8,128)S(1)} %get-tuple-element.24.po_ref) | copy-start | bytes 388
  0.8 5.4 %copy-start.1 = (s32[8,12]{1,0:T(8,128)S(1)}, s32[8,12]{1,0:T(8,128)}, u32[]{:S(2)}) copy-start(s32[8,12]{1,0:T(8,128)} %param.7) | copy-start | bytes 1156
  1.8 5.0 %collective-permute-start.1 = (bf16[528,256]{1,0:T(8,128)(2,1)S(1)}, bf16[528,256]{1,0:T(8,128)(2,1)S(1)}, u32[]{:S(2)}, u32[]{:S(2)}) collective-permute-start(bf16[528,256]{1,0:T(8,128)(2,1)S(1)} %fusion.1), channel_id=1, source_target_pairs={{1,0},{2,1},{3,2},{4,3},{5,4},{6,5},{7,6},{8,7},{9,8},{10,9},{11,1... | collective-permute-start | bytes 811016 | tf_op jit(solution)/shard_map/ppermute | solution.py:20
  3.1 4.2 %collective-permute-start = (bf16[528,256]{1,0:T(8,128)(2,1)S(1)}, bf16[528,256]{1,0:T(8,128)(2,1)S(1)}, u32[]{:S(2)}, u32[]{:S(2)}) collective-permute-start(bf16[528,256]{1,0:T(8,128)(2,1)S(1)} %fusion.1), channel_id=1, source_target_pairs={{0,1},{1,2},{2,3},{3,4},{4,5},{5,6},{6,7},{7,8},{8,9},{9,10},{10,1... | collective-permute-start | bytes 811016 | tf_op jit(solution)/shard_map/ppermute | solution.py:20
  6.7 1.2 %copy-start.3 = (bf16[528,256]{1,0:T(8,128)(2,1)}, bf16[528,256]{1,0:T(8,128)(2,1)S(1)}, u32[]{:S(2)}) copy-start(bf16[528,256]{1,0:T(8,128)(2,1)S(1)} %collective-permute-done.1.pr_ref) | copy-start | bytes 811012
  7.3 0.7 %copy-start.4 = (bf16[528,256]{1,0:T(8,128)(2,1)}, bf16[528,256]{1,0:T(8,128)(2,1)S(1)}, u32[]{:S(2)}) copy-start(bf16[528,256]{1,0:T(8,128)(2,1)S(1)} %collective-permute-done.pl_ref) | copy-start | bytes 811012
  13.2 10.5 %collective-permute-start.2 = (f32[128,640]{1,0:T(8,128)}, f32[128,640]{1,0:T(8,128)S(1)}, u32[]{:S(2)}, u32[]{:S(2)}) collective-permute-start(f32[128,640]{1,0:T(8,128)} %get-tuple-element.21), channel_id=1, source_target_pairs={{1,0},{2,1},{3,2},{4,3},{5,4},{6,5},{7,6},{8,7},{9,8},{10,9},{11,1... | collective-permute-start | bytes 983048 | tf_op jit(solution)/shard_map/ppermute | solution.py:20
  14.5 10.7 %collective-permute-start.3 = (f32[128,640]{1,0:T(8,128)}, f32[128,640]{1,0:T(8,128)S(1)}, u32[]{:S(2)}, u32[]{:S(2)}) collective-permute-start(f32[128,640]{1,0:T(8,128)} %get-tuple-element.22), channel_id=1, source_target_pairs={{0,1},{1,2},{2,3},{3,4},{4,5},{5,6},{6,7},{7,8},{8,9},{9,10},{10,1... | collective-permute-start | bytes 983048 | tf_op jit(solution)/shard_map/ppermute | solution.py:20
  26.2 21.0 %collective-permute-start.4 = (bf16[1,128,896]{2,1,0:T(8,128)(2,1)S(1)}, bf16[1,128,896]{2,1,0:T(8,128)(2,1)S(1)}, u32[]{:S(2)}, u32[]{:S(2)}) collective-permute-start(bf16[1,128,896]{2,1,0:T(8,128)(2,1)S(1)} %fusion.2), channel_id=1, source_target_pairs={{0,16},{16,0},{1,17},{17,1},{2,18},{18,2},{3,19},{19,3},{4,20},{20... | collective-permute-start | bytes 688136 | tf_op jit(solution)/shard_map/ppermute | solution.py:24

commit v7 on v6

--- a/solution.py
+++ b/solution.py
@@ -68,7 +68,7 @@
             st_ref[o * span : (o + 1) * span, :].astype(jnp.bfloat16),
             ap_ref[...],
             preferred_element_type=jnp.float32,
-        )
+        ).astype(out_ref.dtype)
 
 
 def products(lc, pc, po, a_blocks, left, own, right):
@@ -77,7 +77,10 @@
     near = 3 * RB * B
     return pl.pallas_call(
         product_kernel,
-        out_shape=[jax.ShapeDtypeStruct((NC * B, 5 * NC * B), jnp.float32)] * 3,
+        out_shape=[
+            jax.ShapeDtypeStruct((NC * B, 5 * NC * B), dtype)
+            for dtype in (jnp.bfloat16, jnp.float32, jnp.bfloat16)
+        ],
         in_specs=[smem] * 3 + [vmem] * 4,
         out_specs=[vmem] * 3,
         scratch_shapes=[
@@ -112,8 +115,8 @@
     from_left_p = shifted(next_rows, LINE, 1)
     span = NC * B
     combined = jnp.pad(here_rows, ((0, 0), (span, span)))
-    combined = combined + jnp.pad(from_right_p, ((0, 0), (2 * span, 0)))
-    combined = combined + jnp.pad(from_left_p, ((0, 0), (0, 2 * span)))
+    combined = combined + jnp.pad(from_right_p.astype(jnp.float32), ((0, 0), (2 * span, 0)))
+    combined = combined + jnp.pad(from_left_p.astype(jnp.float32), ((0, 0), (0, 2 * span)))
     rows_here = combined.astype(jnp.bfloat16)[None]
     group = lax.axis_index("grp")
     joined = rows_here

time: 48.3 us -> 46.4 us (0.961)
  starting transfers between devices: 31.9 us -> 30.2 us
    ppermute x1, starting transfers between devices: 17 us -> 15.4 us  [partner_2(): lax.ppermute(x, axis, [(i, i ^ 1 << bit) for i in range(lax.axis_size(axi...]
where the time goes in v7:
time: 46.4 us; the launch traced here: 46.1 us
  starting transfers between devices  30.2 us (65%)
  waiting for transfers between devices  5.72 us (12%)
  Pallas kernels  5.17 us (11%)
  other arithmetic  4.11 us (9%)
  local copies, waits for them, and re-layouts  0.82 us (2%)
    ppermute x1, starting transfers between devices, partner_2(): lax.ppermute(x, axis, [(i, i ^ 1 << bit) for i in range(lax.axis_size(axi...  15.4 us
    ppermute x4, starting transfers between devices, shifted(): return lax.ppermute(x, axis, pairs)  14.8 us
    pallas_call x1, Pallas kernels, products(): pl.pallas_call(product_kernel, out_shape=[jax.ShapeDtypeStruct((NC * B, 5...  5.17 us
    ppermute x1, waiting for transfers between devices, partner_2(): lax.ppermute(x, axis, [(i, i ^ 1 << bit) for i in range(lax.axis_size(axi...  4 us
    ppermute x4, waiting for transfers between devices, shifted(): return lax.ppermute(x, axis, pairs)  1.72 us
    broadcast_in_dim x1, other arithmetic, local(): rows_here = combined.astype(jnp.bfloat16)[None]  1.03 us
    concatenate x1, other arithmetic, local(): payload = jnp.concatenate([p_blocks, tag], axis=0)  0.97 us
  transfers between devices with their start and end apart: 5, of which 3 were waited for; matrix products, arithmetic and copies ran while one was open for 1% of the time, Pallas kernels for 0%

profile of v7, /device:TPU:0, one launch (start us, length us, event | category | flops | bytes accessed | tf_op | source)
XLA Modules:
  0.0 46.1 jit_solution(5649528608097265473)
XLA Ops:
  0.0 0.0 copy-start.2
  0.0 0.7 %copy-done.2 = s32[8,4]{0,1:T(4,128)S(1)} copy-done((s32[8,4]{0,1:T(4,128)S(1)}, s32[8,4]{0,1:T(4,128)}, u32[]{:S(2)}) %copy-start.2) | copy-done | bytes 152
  0.7 0.1 copy.11
  0.8 0.0 copy-start
  0.8 0.0 copy-start.1
  0.8 1.0 %fusion.1 = bf16[528,256]{1,0:T(8,128)(2,1)S(1)} fusion(bf16[8,4]{1,0:T(8,128)(2,1)S(1)} %convert_element_type.20, bf16[512,256]{1,0:T(8,128)(2,1)} %pm_ref.1), kind=kLoop, calls=%fused_computation.4 | loop fusion | flops 811008 | bytes 532544 | tf_op jit(solution)/shard_map/concatenate | solution.py:104
  1.8 0.0 copy-done
  1.8 1.3 %collective-permute-start.1 = (bf16[528,256]{1,0:T(8,128)(2,1)S(1)}, bf16[528,256]{1,0:T(8,128)(2,1)S(1)}, u32[]{:S(2)}, u32[]{:S(2)}) collective-permute-start(bf16[528,256]{1,0:T(8,128)(2,1)S(1)} %fusion.1), channel_id=1, source_target_pairs={{1,0},{2,1},{3,2},{4,3},{5,4},{6,5},{7,6},{8,7},{9,8},{10,9},{11,1... | collective-permute-start | bytes 811016 | tf_op jit(solution)/shard_map/ppermute | solution.py:20
  3.1 3.0 %collective-permute-start = (bf16[528,256]{1,0:T(8,128)(2,1)S(1)}, bf16[528,256]{1,0:T(8,128)(2,1)S(1)}, u32[]{:S(2)}, u32[]{:S(2)}) collective-permute-start(bf16[528,256]{1,0:T(8,128)(2,1)S(1)} %fusion.1), channel_id=1, source_target_pairs={{0,1},{1,2},{2,3},{3,4},{4,5},{5,6},{6,7},{7,8},{8,9},{9,10},{10,1... | collective-permute-start | bytes 811016 | tf_op jit(solution)/shard_map/ppermute | solution.py:20
  6.1 0.0 copy-done.1
  6.1 0.6 %broadcast_subtract_fusion.1.lc_ref = s32[8,12]{1,0:T(8,128)} fusion(s32[8,12]{1,0:T(8,128)S(1)} %copy-done.1, s32[]{:T(128)S(6)} %mul.10), kind=kLoop, calls=%fused_computation.11 | loop fusion | flops 96 | bytes 772 | tf_op jit(solution)/shard_map/sub | solution.py:112
  6.7 0.0 collective-permute-done.1.pr_ref
  6.7 0.0 copy-start.3
  6.8 0.5 %collective-permute-done.pl_ref = bf16[528,256]{1,0:T(8,128)(2,1)S(1)} collective-permute-done((bf16[528,256]{1,0:T(8,128)(2,1)S(1)}, bf16[528,256]{1,0:T(8,128)(2,1)S(1)}, u32[]{:S(2)}, u32[]{:S(2)}) %collective-permute-start) | collective-permute-done | bytes 270368 | tf_op jit(solution)/shard_map/ppermute | solution.py:20
  7.3 0.0 copy-start.4
  7.3 0.6 %pad_add_fusion.pc_ref = s32[24,4]{1,0:T(8,128)} fusion(s32[8,4]{1,0:T(8,128)S(1)} %convert_add_fusion, s32[8,4]{1,0:T(8,128)S(1)} %get-tuple-element.23, s32[8,4]{1,0:T(8,128)S(1)} %slice_convert_fusion), kind=kLoop, calls=%fused_computation.6 | loop fusion | flops 192 | bytes 768 | tf_op jit(solution)/shard_map/concatenate | solution.py:111
  7.9 0.0 copy-done.3
  7.9 0.0 copy-done.4
  8.0 5.2 %shard_map.46 = (bf16[128,640]{1,0:T(8,128)(2,1)}, f32[128,640]{1,0:T(8,128)}, bf16[128,640]{1,0:T(8,128)(2,1)}) custom-call(s32[8,12]{1,0:T(8,128)} %broadcast_subtract_fusion.1.lc_ref, s32[24,4]{1,0:T(8,128)} %pad_add_fusion.pc_ref, s32[8,4]{1,0:T(8,128)} %copy-done, bf16[512,768]{1,0:T(8,128)(2,1)} %a_ref.1, bf16[528,256]{1,0:T(8,128)(2,1)} %copy-done.4, ...), custom_call_target="tpu_custom_call" | custom-call | flops 754974720 | bytes 4194304 | tf_op jit(solution)/shard_map/pallas_call | solution.py:78
  13.1 1.3 %collective-permute-start.2 = (bf16[128,640]{1,0:T(8,128)(2,1)}, bf16[128,640]{1,0:T(8,128)(2,1)S(1)}, u32[]{:S(2)}, u32[]{:S(2)}) collective-permute-start(bf16[128,640]{1,0:T(8,128)(2,1)} %get-tuple-element.21), channel_id=1, source_target_pairs={{1,0},{2,1},{3,2},{4,3},{5,4},{6,5},{7,6},{8,7},{9,8},{10,9},{11,1... | collective-permute-start | bytes 491528 | tf_op jit(solution)/shard_map/ppermute | solution.py:20
  14.4 9.2 %collective-permute-start.3 = (bf16[128,640]{1,0:T(8,128)(2,1)}, bf16[128,640]{1,0:T(8,128)(2,1)S(1)}, u32[]{:S(2)}, u32[]{:S(2)}) collective-permute-start(bf16[128,640]{1,0:T(8,128)(2,1)} %get-tuple-element.22), channel_id=1, source_target_pairs={{0,1},{1,2},{2,3},{3,4},{4,5},{5,6},{6,7},{7,8},{8,9},{9,10},{10,1... | collective-permute-start | bytes 491528 | tf_op jit(solution)/shard_map/ppermute | solution.py:20
  23.7 0.0 collective-permute-done.2
  23.7 1.2 %collective-permute-done.3 = bf16[128,640]{1,0:T(8,128)(2,1)S(1)} collective-permute-done((bf16[128,640]{1,0:T(8,128)(2,1)}, bf16[128,640]{1,0:T(8,128)(2,1)S(1)}, u32[]{:S(2)}, u32[]{:S(2)}) %collective-permute-start.3) | collective-permute-done | bytes 163872 | tf_op jit(solution)/shard_map/ppermute | solution.py:20
  24.9 1.0 %fusion.2 = bf16[1,128,896]{2,1,0:T(8,128)(2,1)S(1)} fusion(f32[128,640]{1,0:T(8,128)} %get-tuple-element.20, bf16[128,640]{1,0:T(8,128)(2,1)S(1)} %collective-permute-done.3, bf16[128,640]{1,0:T(8,128)(2,1)S(1)} %collective-permute-done.2), kind=kLoop, calls=%fused_computation.5 | loop fusion | flops 573440 | bytes 884736 | tf_op jit(solution)/shard_map/broadcast_in_dim | solution.py:120
  25.9 15.4 %collective-permute-start.4 = (bf16[1,128,896]{2,1,0:T(8,128)(2,1)S(1)}, bf16[1,128,896]{2,1,0:T(8,128)(2,1)S(1)}, u32[]{:S(2)}, u32[]{:S(2)}) collective-permute-start(bf16[1,128,896]{2,1,0:T(8,128)(2,1)S(1)} %fusion.2), channel_id=1, source_target_pairs={{0,16},{16,0},{1,17},{17,1},{2,18},{18,2},{3,19},{19,3},{4,20},{20... | collective-permute-start | bytes 688136 | tf_op jit(solution)/shard_map/ppermute | solution.py:24
  41.3 4.0 %collective-permute-done.4 = bf16[1,128,896]{2,1,0:T(8,128)(2,1)S(1)} collective-permute-done((bf16[1,128,896]{2,1,0:T(8,128)(2,1)S(1)}, bf16[1,128,896]{2,1,0:T(8,128)(2,1)S(1)}, u32[]{:S(2)}, u32[]{:S(2)}) %collective-permute-start.4) | collective-permute-done | bytes 229408 | tf_op jit(solution)/shard_map/ppermute | solution.py:24
  45.3 0.8 %maximum_select_fusion = bf16[2,128,896]{2,1,0:T(8,128)(2,1)} fusion(bf16[1,128,896]{2,1,0:T(8,128)(2,1)S(1)} %fusion.2, bf16[1,128,896]{2,1,0:T(8,128)(2,1)S(1)} %collective-permute-done.4, pred[]{:T(512)S(6)} %eq.5), kind=kLoop, calls=%fused_computation.2 | loop fusion | flops 688128 | bytes 917505 | tf_op jit(solution)/shard_map/jit(_where)/select_n | solution.py:126
  (4 shorter events, 0.0 us)
Async XLA Ops:
  0.0 0.7 %copy-start.2 = (s32[8,4]{0,1:T(4,128)S(1)}, s32[8,4]{0,1:T(4,128)}, u32[]{:S(2)}) copy-start(s32[8,4]{0,1:T(4,128)} %param.9) | copy-start | bytes 388
  0.8 1.0 %copy-start = (s32[8,4]{1,0:T(8,128)}, s32[8,4]{1,0:T(8,128)S(1)}, u32[]{:S(2)}) copy-start(s32[8,4]{1,0:T(8,128)S(1)} %get-tuple-element.24.po_ref) | copy-start | bytes 388
  0.8 5.4 %copy-start.1 = (s32[8,12]{1,0:T(8,128)S(1)}, s32[8,12]{1,0:T(8,128)}, u32[]{:S(2)}) copy-start(s32[8,12]{1,0:T(8,128)} %param.7) | copy-start | bytes 1156
  1.8 5.0 %collective-permute-start.1 = (bf16[528,256]{1,0:T(8,128)(2,1)S(1)}, bf16[528,256]{1,0:T(8,128)(2,1)S(1)}, u32[]{:S(2)}, u32[]{:S(2)}) collective-permute-start(bf16[528,256]{1,0:T(8,128)(2,1)S(1)} %fusion.1), channel_id=1, source_target_pairs={{1,0},{2,1},{3,2},{4,3},{5,4},{6,5},{7,6},{8,7},{9,8},{10,9},{11,1... | collective-permute-start | bytes 811016 | tf_op jit(solution)/shard_map/ppermute | solution.py:20
  3.1 4.2 %collective-permute-start = (bf16[528,256]{1,0:T(8,128)(2,1)S(1)}, bf16[528,256]{1,0:T(8,128)(2,1)S(1)}, u32[]{:S(2)}, u32[]{:S(2)}) collective-permute-start(bf16[528,256]{1,0:T(8,128)(2,1)S(1)} %fusion.1), channel_id=1, source_target_pairs={{0,1},{1,2},{2,3},{3,4},{4,5},{5,6},{6,7},{7,8},{8,9},{9,10},{10,1... | collective-permute-start | bytes 811016 | tf_op jit(solution)/shard_map/ppermute | solution.py:20
  6.7 1.2 %copy-start.3 = (bf16[528,256]{1,0:T(8,128)(2,1)}, bf16[528,256]{1,0:T(8,128)(2,1)S(1)}, u32[]{:S(2)}) copy-start(bf16[528,256]{1,0:T(8,128)(2,1)S(1)} %collective-permute-done.1.pr_ref) | copy-start | bytes 811012
  7.3 0.7 %copy-start.4 = (bf16[528,256]{1,0:T(8,128)(2,1)}, bf16[528,256]{1,0:T(8,128)(2,1)S(1)}, u32[]{:S(2)}) copy-start(bf16[528,256]{1,0:T(8,128)(2,1)S(1)} %collective-permute-done.pl_ref) | copy-start | bytes 811012
  13.1 10.5 %collective-permute-start.2 = (bf16[128,640]{1,0:T(8,128)(2,1)}, bf16[128,640]{1,0:T(8,128)(2,1)S(1)}, u32[]{:S(2)}, u32[]{:S(2)}) collective-permute-start(bf16[128,640]{1,0:T(8,128)(2,1)} %get-tuple-element.21), channel_id=1, source_target_pairs={{1,0},{2,1},{3,2},{4,3},{5,4},{6,5},{7,6},{8,7},{9,8},{10,9},{11,1... | collective-permute-start | bytes 491528 | tf_op jit(solution)/shard_map/ppermute | solution.py:20
  14.4 10.4 %collective-permute-start.3 = (bf16[128,640]{1,0:T(8,128)(2,1)}, bf16[128,640]{1,0:T(8,128)(2,1)S(1)}, u32[]{:S(2)}, u32[]{:S(2)}) collective-permute-start(bf16[128,640]{1,0:T(8,128)(2,1)} %get-tuple-element.22), channel_id=1, source_target_pairs={{0,1},{1,2},{2,3},{3,4},{4,5},{5,6},{6,7},{7,8},{8,9},{9,10},{10,1... | collective-permute-start | bytes 491528 | tf_op jit(solution)/shard_map/ppermute | solution.py:20
  25.9 19.4 %collective-permute-start.4 = (bf16[1,128,896]{2,1,0:T(8,128)(2,1)S(1)}, bf16[1,128,896]{2,1,0:T(8,128)(2,1)S(1)}, u32[]{:S(2)}, u32[]{:S(2)}) collective-permute-start(bf16[1,128,896]{2,1,0:T(8,128)(2,1)S(1)} %fusion.2), channel_id=1, source_target_pairs={{0,16},{16,0},{1,17},{17,1},{2,18},{18,2},{3,19},{19,3},{4,20},{20... | collective-permute-start | bytes 688136 | tf_op jit(solution)/shard_map/ppermute | solution.py:24

commit v8 on v6

v8 whole, which is shorter than its diff:
```python
import jax
import jax.numpy as jnp
from jax import lax
from jax.experimental import pallas as pl
from jax.experimental.pallas import tpu as pltpu
from jax.sharding import PartitionSpec as P

B = 64
KA = 12
KP = 4
NC = 2
RB = 8
LINE = ("grp", "dev")
HALF = 128


def shifted(x, axis, by):
    peers = lax.axis_size(axis)
    pairs = [(i, i + by) for i in range(peers) if 0 <= i + by < peers]
    return lax.ppermute(x, axis, pairs)


def partner_2(x, axis, bit):
    return lax.ppermute(x, axis, [(i, i ^ 1 << bit) for i in range(lax.axis_size(axis))])


def chunk(j):
    return pl.ds(pl.multiple_of(j * HALF, HALF), HALF)


def rows_at(r):
    return pl.ds(pl.multiple_of(r * B, B), B)


def spread_rows(ps_ref, base, src_ref, pc_ref, pc_base, side):
    for r in range(RB):
        blk = src_ref[r * B : (r + 1) * B, :].astype(jnp.float32)
        halves = [blk[:, 0:HALF], blk[:, HALF : 2 * HALF]]
        swapped = [pltpu.roll(h, B, 1) for h in halves]
        rows = slice((base + r) * B, (base + r + 1) * B)
        for l in range(KP):
            j = pc_ref[pc_base + r, l]
            h = j % 2
            val = jnp.where(h == l % 2, halves[l // 2], swapped[l // 2])
            cols = chunk(j // 2)
            cur = ps_ref[rows, cols].astype(jnp.float32)
            ps_ref[rows, cols] = jnp.where(side == h, val, cur).astype(ps_ref.dtype)


def own_kernel(po_ref, pm_ref, pso_ref, st_ref):
    side = lax.broadcasted_iota(jnp.int32, (B, HALF), 1) // B
    pso_ref[...] = jnp.zeros(pso_ref.shape, pso_ref.dtype)
    spread_rows(pso_ref, 0, pm_ref, po_ref, 0, side)
    pt = pm_ref[...].astype(jnp.float32).T
    st_ref[...] = jnp.zeros(st_ref.shape, st_ref.dtype)
    for i in range(RB):
        cols = slice((i // 2) * HALF, (i // 2 + 1) * HALF)
        for l in range(KP):
            dest = rows_at(po_ref[RB + i, l])
            cur = st_ref[dest, cols].astype(jnp.float32)
            st_ref[dest, cols] = jnp.where(side == i % 2, pt[l * B : (l + 1) * B, cols], cur).astype(st_ref.dtype)


def product_kernel(
    lc_ref, pc_ref, a_ref, pl_ref, pr_ref, pso_ref, st_ref, prev_ref, here_ref, next_ref, ps_ref, panel_ref, ap_ref
):
    side = lax.broadcasted_iota(jnp.int32, (B, HALF), 1) // B
    near = RB * B
    ps_ref[0:near, :] = jnp.zeros((near, ps_ref.shape[1]), ps_ref.dtype)
    ps_ref[2 * near : 3 * near, :] = jnp.zeros((near, ps_ref.shape[1]), ps_ref.dtype)
    ps_ref[near : 2 * near, :] = pso_ref[...]
    spread_rows(ps_ref, 0, pl_ref, pc_ref, 0, side)
    spread_rows(ps_ref, 2 * RB, pr_ref, pc_ref, RB, side)
    for i in range(RB):
        for k in range(KA):
            panel_ref[k * B : (k + 1) * B, :] = ps_ref[rows_at(lc_ref[i, k]), :]
        ap = jnp.dot(a_ref[i * B : (i + 1) * B, :], panel_ref[...], preferred_element_type=jnp.float32)
        ap_ref[i * B : (i + 1) * B, :] = ap.astype(ap_ref.dtype)
    span = NC * B
    for o, out_ref in enumerate((prev_ref, here_ref, next_ref)):
        out_ref[...] = jnp.dot(
            st_ref[o * span : (o + 1) * span, :], ap_ref[...], preferred_element_type=jnp.float32
        )


def products(lc, pc_side, po, a_blocks, left, own, right):
    smem = pl.BlockSpec(memory_space=pltpu.SMEM)
    vmem = pl.BlockSpec(memory_space=pltpu.VMEM)
    window = 5 * NC * B
    pso, st = pl.pallas_call(
        own_kernel,
        out_shape=[
            jax.ShapeDtypeStruct((RB * B, window), jnp.bfloat16),
            jax.ShapeDtypeStruct((3 * NC * B, RB * B), jnp.bfloat16),
        ],
        in_specs=[smem, vmem],
        out_specs=[vmem] * 2,
    )(po, own)
    return pl.pallas_call(
        product_kernel,
        out_shape=[jax.ShapeDtypeStruct((NC * B, window), jnp.float32)] * 3,
        in_specs=[smem] * 2 + [vmem] * 5,
        out_specs=[vmem] * 3,
        scratch_shapes=[
            pltpu.VMEM((3 * RB * B, window), jnp.bfloat16),
            pltpu.VMEM((KA * B, window), jnp.bfloat16),
            pltpu.VMEM((RB * B, window), jnp.bfloat16),
        ],
        cost_estimate=pl.CostEstimate(
            flops=2 * RB * B * KA * B * window + 2 * 3 * NC * B * RB * B * window,
            bytes_accessed=4 * 1024 * 1024,
            transcendentals=0,
        ),
    )(lc, pc_side, a_blocks, left, right, pso, st)


def local(a_blocks, a_cols, p_blocks, p_cols):
    q = lax.axis_index(LINE)
    rel = p_cols - (q - 1) * NC
    tag = jnp.zeros((16, KP * B), jnp.bfloat16).at[:RB, :KP].set(rel.astype(jnp.bfloat16))
    payload = jnp.concatenate([p_blocks, tag], axis=0)
    from_left = shifted(payload, LINE, 1)
    from_right = shifted(payload, LINE, -1)

    def cols(x, shift):
        return x[RB * B : RB * B + RB, :KP].astype(jnp.int32) + shift

    pc_side = jnp.concatenate([cols(from_left, 0), cols(from_right, 2 * NC)], axis=0)
    po = jnp.concatenate([rel + NC, rel], axis=0)
    lc = a_cols - (q - 1) * RB
    prev_rows, here_rows, next_rows = products(lc, pc_side, po, a_blocks, from_left, p_blocks, from_right)
    from_right_p = shifted(prev_rows, LINE, -1)
    from_left_p = shifted(next_rows, LINE, 1)
    span = NC * B
    combined = jnp.pad(here_rows, ((0, 0), (span, span)))
    combined = combined + jnp.pad(from_right_p, ((0, 0), (2 * span, 0)))
    combined = combined + jnp.pad(from_left_p, ((0, 0), (0, 2 * span)))
    rows_here = combined.astype(jnp.bfloat16)[None]
    group = lax.axis_index("grp")
    joined = rows_here
    for section_bit in range(lax.axis_size("grp").bit_length() - 1):
        partner = partner_2(joined, "grp", section_bit)
        is_upper = group // 2**section_bit % 2 == 1
        joined = jnp.where(
            is_upper,
            jnp.concatenate([partner, joined], axis=0),
            jnp.concatenate([joined, partner], axis=0),
        )
    return joined


def solution(mesh):
    placed = (P(LINE, None),) * 4
    return jax.shard_map(
        local, mesh=mesh, in_specs=placed, out_specs=P(None, "dev", None), check_vma=False
    )
```

time: 48.3 us -> 48.2 us (level)
  starting transfers between devices: 31.9 us -> 29.3 us
  Pallas kernels: 5.23 us -> 7.5 us
  other arithmetic: 4.1 us -> 4.71 us
  waiting for transfers between devices: 5.94 us -> 5.43 us
    ppermute x4, starting transfers between devices: 14.9 us -> 12.3 us  [shifted(): return lax.ppermute(x, axis, pairs)]
    pallas_call x1 -> x2, Pallas kernels: 5.23 us -> 7.5 us  [the longest x1 5.1 us: products(): pl.pallas_call(product_kernel, out_shape=[jax.ShapeDtypeStruct((NC * B, w...]
    concatenate x1 -> x2, other arithmetic: 0.65 us -> 1.27 us  [the longest x1 0.67 us: local(): jnp.concatenate([cols(from_left, 0), cols(from_right, 2 * NC)], axis=0)]
    ppermute x4, waiting for transfers between devices: 1.94 us -> 1.43 us  [shifted(): return lax.ppermute(x, axis, pairs)]
  transfers between devices with their start and end apart: 5 -> 5, of which waited for: 3 -> 2; matrix products, arithmetic and copies ran while one was open for 1% -> 2% of each run, Pallas kernels for 0% -> 5%
where the time goes in v8:
time: 48.2 us; the launch traced here: 47.9 us
  starting transfers between devices  29.3 us (61%)
  Pallas kernels  7.5 us (16%)
  waiting for transfers between devices  5.43 us (11%)
  other arithmetic  4.71 us (10%)
  local copies, waits for them, and re-layouts  0.85 us (2%)
    ppermute x1, starting transfers between devices, partner_2(): lax.ppermute(x, axis, [(i, i ^ 1 << bit) for i in range(lax.axis_size(axi...  17 us
    ppermute x4, starting transfers between devices, shifted(): return lax.ppermute(x, axis, pairs)  12.3 us
    pallas_call x1, Pallas kernels, products(): pl.pallas_call(product_kernel, out_shape=[jax.ShapeDtypeStruct((NC * B, w...  5.1 us
    ppermute x1, waiting for transfers between devices, partner_2(): lax.ppermute(x, axis, [(i, i ^ 1 << bit) for i in range(lax.axis_size(axi...  4 us
    pallas_call x1, Pallas kernels, products(): pl.pallas_call(own_kernel, out_shape=[jax.ShapeDtypeStruct((RB * B, windo...  2.4 us
    ppermute x4, waiting for transfers between devices, shifted(): return lax.ppermute(x, axis, pairs)  1.43 us
    broadcast_in_dim x1, other arithmetic, local(): rows_here = combined.astype(jnp.bfloat16)[None]  1.02 us
    concatenate x1, other arithmetic, local(): payload = jnp.concatenate([p_blocks, tag], axis=0)  0.98 us
  transfers between devices with their start and end apart: 5, of which 2 were waited for; matrix products, arithmetic and copies ran while one was open for 2% of the time, Pallas kernels for 5%

profile of v8, /device:TPU:0, one launch (start us, length us, event | category | flops | bytes accessed | tf_op | source)
XLA Modules:
  0.0 47.9 jit_solution(6553664073850101576)
XLA Ops:
  0.0 0.0 copy-start.1
  0.0 0.7 %copy-done.1 = s32[8,4]{0,1:T(4,128)S(1)} copy-done((s32[8,4]{0,1:T(4,128)S(1)}, s32[8,4]{0,1:T(4,128)}, u32[]{:S(2)}) %copy-start.1) | copy-done | bytes 152
  0.7 0.1 copy.13
  0.8 0.0 copy-start
  0.8 1.0 %fusion.1 = bf16[528,256]{1,0:T(8,128)(2,1)S(1)} fusion(bf16[8,4]{1,0:T(8,128)(2,1)S(1)} %convert_element_type.18, bf16[512,256]{1,0:T(8,128)(2,1)} %pm_ref.1), kind=kLoop, calls=%fused_computation.4 | loop fusion | flops 811008 | bytes 532544 | tf_op jit(solution)/shard_map/concatenate | solution.py:121
  1.8 1.3 %collective-permute-start.1 = (bf16[528,256]{1,0:T(8,128)(2,1)S(1)}, bf16[528,256]{1,0:T(8,128)(2,1)S(1)}, u32[]{:S(2)}, u32[]{:S(2)}) collective-permute-start(bf16[528,256]{1,0:T(8,128)(2,1)S(1)} %fusion.1), channel_id=1, source_target_pairs={{1,0},{2,1},{3,2},{4,3},{5,4},{6,5},{7,6},{8,7},{9,8},{10,9},{11,1... | collective-permute-start | bytes 811016 | tf_op jit(solution)/shard_map/ppermute | solution.py:20
  3.1 3.0 %collective-permute-start = (bf16[528,256]{1,0:T(8,128)(2,1)S(1)}, bf16[528,256]{1,0:T(8,128)(2,1)S(1)}, u32[]{:S(2)}, u32[]{:S(2)}) collective-permute-start(bf16[528,256]{1,0:T(8,128)(2,1)S(1)} %fusion.1), channel_id=1, source_target_pairs={{0,1},{1,2},{2,3},{3,4},{4,5},{5,6},{6,7},{7,8},{8,9},{9,10},{10,1... | collective-permute-start | bytes 811016 | tf_op jit(solution)/shard_map/ppermute | solution.py:20
  6.1 0.0 copy-done
  6.1 0.6 %broadcast_subtract_fusion.1.lc_ref = s32[8,12]{1,0:T(8,128)} fusion(s32[8,12]{1,0:T(8,128)S(1)} %copy-done, s32[]{:T(128)S(6)} %mul.10), kind=kLoop, calls=%fused_computation.12 | loop fusion | flops 96 | bytes 772 | tf_op jit(solution)/shard_map/sub | solution.py:130
  6.7 0.6 %pad_add_fusion.1.po_ref = s32[16,4]{1,0:T(8,128)} fusion(s32[8,4]{1,0:T(8,128)S(1)} %get-tuple-element.28, s32[8,4]{1,0:T(8,128)S(1)} %get-tuple-element.27), kind=kLoop, calls=%fused_computation.7 | loop fusion | flops 64 | bytes 512 | tf_op jit(solution)/shard_map/concatenate | solution.py:129
  7.3 2.4 %shard_map.46 = (bf16[512,640]{1,0:T(8,128)(2,1)}, bf16[384,512]{1,0:T(8,128)(2,1)}) custom-call(s32[16,4]{1,0:T(8,128)} %pad_add_fusion.1.po_ref, bf16[512,256]{1,0:T(8,128)(2,1)} %pm_ref.1), custom_call_target="tpu_custom_call" | custom-call | tf_op jit(solution)/shard_map/pallas_call | solution.py:90
  9.7 0.0 collective-permute-done.1.pr_ref
  9.7 0.0 copy-start.2
  9.7 0.0 collective-permute-done.pl_ref
  9.7 0.0 copy-start.3
  9.8 0.7 %pad_add_fusion.pc_ref = s32[16,4]{1,0:T(8,128)} fusion(s32[8,4]{1,0:T(8,128)S(1)} %convert_add_fusion, s32[8,4]{1,0:T(8,128)S(1)} %slice_convert_fusion), kind=kLoop, calls=%fused_computation.6 | loop fusion | flops 64 | bytes 512 | tf_op jit(solution)/shard_map/concatenate | solution.py:128
  10.4 0.0 copy-done.2
  10.5 0.1 copy-done.3
  10.5 5.1 %shard_map.47 = (f32[128,640]{1,0:T(8,128)}, f32[128,640]{1,0:T(8,128)}, f32[128,640]{1,0:T(8,128)}) custom-call(s32[8,12]{1,0:T(8,128)} %broadcast_subtract_fusion.1.lc_ref, s32[16,4]{1,0:T(8,128)} %pad_add_fusion.pc_ref, bf16[512,768]{1,0:T(8,128)(2,1)} %a_ref.1, bf16[528,256]{1,0:T(8,128)(2,1)} %copy-done.3, bf16[528,256]{1,0:T(8,128)(2,1)} %copy-done.2, ...), custom_call_target="tpu_custom_call" | custom-call | flops 754974720 | bytes 4194304 | tf_op jit(solution)/shard_map/pallas_call | solution.py:99
  15.6 1.3 %collective-permute-start.2 = (f32[128,640]{1,0:T(8,128)}, f32[128,640]{1,0:T(8,128)S(1)}, u32[]{:S(2)}, u32[]{:S(2)}) collective-permute-start(f32[128,640]{1,0:T(8,128)} %get-tuple-element.25), channel_id=1, source_target_pairs={{1,0},{2,1},{3,2},{4,3},{5,4},{6,5},{7,6},{8,7},{9,8},{10,9},{11,1... | collective-permute-start | bytes 983048 | tf_op jit(solution)/shard_map/ppermute | solution.py:20
  16.9 6.7 %collective-permute-start.3 = (f32[128,640]{1,0:T(8,128)}, f32[128,640]{1,0:T(8,128)S(1)}, u32[]{:S(2)}, u32[]{:S(2)}) collective-permute-start(f32[128,640]{1,0:T(8,128)} %get-tuple-element.26), channel_id=1, source_target_pairs={{0,1},{1,2},{2,3},{3,4},{4,5},{5,6},{6,7},{7,8},{8,9},{9,10},{10,1... | collective-permute-start | bytes 983048 | tf_op jit(solution)/shard_map/ppermute | solution.py:20
  23.6 0.0 collective-permute-done.2
  23.6 1.4 %collective-permute-done.3 = f32[128,640]{1,0:T(8,128)S(1)} collective-permute-done((f32[128,640]{1,0:T(8,128)}, f32[128,640]{1,0:T(8,128)S(1)}, u32[]{:S(2)}, u32[]{:S(2)}) %collective-permute-start.3) | collective-permute-done | bytes 327712 | tf_op jit(solution)/shard_map/ppermute | solution.py:20
  25.0 1.0 %fusion.2 = bf16[1,128,896]{2,1,0:T(8,128)(2,1)S(1)} fusion(f32[128,640]{1,0:T(8,128)S(1)} %collective-permute-done.3, f32[128,640]{1,0:T(8,128)S(1)} %collective-permute-done.2, f32[128,640]{1,0:T(8,128)} %get-tuple-element.24), kind=kLoop, calls=%fused_computation.5 | loop fusion | flops 344064 | bytes 1212416 | tf_op jit(solution)/shard_map/broadcast_in_dim | solution.py:138
  26.1 17.0 %collective-permute-start.4 = (bf16[1,128,896]{2,1,0:T(8,128)(2,1)S(1)}, bf16[1,128,896]{2,1,0:T(8,128)(2,1)S(1)}, u32[]{:S(2)}, u32[]{:S(2)}) collective-permute-start(bf16[1,128,896]{2,1,0:T(8,128)(2,1)S(1)} %fusion.2), channel_id=1, source_target_pairs={{0,16},{16,0},{1,17},{17,1},{2,18},{18,2},{3,19},{19,3},{4,20},{20... | collective-permute-start | bytes 688136 | tf_op jit(solution)/shard_map/ppermute | solution.py:24
  43.1 4.0 %collective-permute-done.4 = bf16[1,128,896]{2,1,0:T(8,128)(2,1)S(1)} collective-permute-done((bf16[1,128,896]{2,1,0:T(8,128)(2,1)S(1)}, bf16[1,128,896]{2,1,0:T(8,128)(2,1)S(1)}, u32[]{:S(2)}, u32[]{:S(2)}) %collective-permute-start.4) | collective-permute-done | bytes 229408 | tf_op jit(solution)/shard_map/ppermute | solution.py:24
  47.1 0.8 %maximum_select_fusion = bf16[2,128,896]{2,1,0:T(8,128)(2,1)} fusion(bf16[1,128,896]{2,1,0:T(8,128)(2,1)S(1)} %fusion.2, bf16[1,128,896]{2,1,0:T(8,128)(2,1)S(1)} %collective-permute-done.4, pred[]{:T(512)S(6)} %eq.5), kind=kLoop, calls=%fused_computation.2 | loop fusion | flops 688128 | bytes 917505 | tf_op jit(solution)/shard_map/jit(_where)/select_n | solution.py:144
  (4 shorter events, 0.0 us)
Async XLA Ops:
  0.0 0.7 %copy-start.1 = (s32[8,4]{0,1:T(4,128)S(1)}, s32[8,4]{0,1:T(4,128)}, u32[]{:S(2)}) copy-start(s32[8,4]{0,1:T(4,128)} %param.9) | copy-start | bytes 388
  0.8 5.3 %copy-start = (s32[8,12]{1,0:T(8,128)S(1)}, s32[8,12]{1,0:T(8,128)}, u32[]{:S(2)}) copy-start(s32[8,12]{1,0:T(8,128)} %param.7) | copy-start | bytes 1156
  1.8 7.9 %collective-permute-start.1 = (bf16[528,256]{1,0:T(8,128)(2,1)S(1)}, bf16[528,256]{1,0:T(8,128)(2,1)S(1)}, u32[]{:S(2)}, u32[]{:S(2)}) collective-permute-start(bf16[528,256]{1,0:T(8,128)(2,1)S(1)} %fusion.1), channel_id=1, source_target_pairs={{1,0},{2,1},{3,2},{4,3},{5,4},{6,5},{7,6},{8,7},{9,8},{10,9},{11,1... | collective-permute-start | bytes 811016 | tf_op jit(solution)/shard_map/ppermute | solution.py:20
  3.1 6.7 %collective-permute-start = (bf16[528,256]{1,0:T(8,128)(2,1)S(1)}, bf16[528,256]{1,0:T(8,128)(2,1)S(1)}, u32[]{:S(2)}, u32[]{:S(2)}) collective-permute-start(bf16[528,256]{1,0:T(8,128)(2,1)S(1)} %fusion.1), channel_id=1, source_target_pairs={{0,1},{1,2},{2,3},{3,4},{4,5},{5,6},{6,7},{7,8},{8,9},{9,10},{10,1... | collective-permute-start | bytes 811016 | tf_op jit(solution)/shard_map/ppermute | solution.py:20
  9.7 0.7 %copy-start.2 = (bf16[528,256]{1,0:T(8,128)(2,1)}, bf16[528,256]{1,0:T(8,128)(2,1)S(1)}, u32[]{:S(2)}) copy-start(bf16[528,256]{1,0:T(8,128)(2,1)S(1)} %collective-permute-done.1.pr_ref) | copy-start | bytes 811012
  9.7 0.8 %copy-start.3 = (bf16[528,256]{1,0:T(8,128)(2,1)}, bf16[528,256]{1,0:T(8,128)(2,1)S(1)}, u32[]{:S(2)}) copy-start(bf16[528,256]{1,0:T(8,128)(2,1)S(1)} %collective-permute-done.pl_ref) | copy-start | bytes 811012
  15.6 8.0 %collective-permute-start.2 = (f32[128,640]{1,0:T(8,128)}, f32[128,640]{1,0:T(8,128)S(1)}, u32[]{:S(2)}, u32[]{:S(2)}) collective-permute-start(f32[128,640]{1,0:T(8,128)} %get-tuple-element.25), channel_id=1, source_target_pairs={{1,0},{2,1},{3,2},{4,3},{5,4},{6,5},{7,6},{8,7},{9,8},{10,9},{11,1... | collective-permute-start | bytes 983048 | tf_op jit(solution)/shard_map/ppermute | solution.py:20
  16.9 8.1 %collective-permute-start.3 = (f32[128,640]{1,0:T(8,128)}, f32[128,640]{1,0:T(8,128)S(1)}, u32[]{:S(2)}, u32[]{:S(2)}) collective-permute-start(f32[128,640]{1,0:T(8,128)} %get-tuple-element.26), channel_id=1, source_target_pairs={{0,1},{1,2},{2,3},{3,4},{4,5},{5,6},{6,7},{7,8},{8,9},{9,10},{10,1... | collective-permute-start | bytes 983048 | tf_op jit(solution)/shard_map/ppermute | solution.py:20
  26.1 21.0 %collective-permute-start.4 = (bf16[1,128,896]{2,1,0:T(8,128)(2,1)S(1)}, bf16[1,128,896]{2,1,0:T(8,128)(2,1)S(1)}, u32[]{:S(2)}, u32[]{:S(2)}) collective-permute-start(bf16[1,128,896]{2,1,0:T(8,128)(2,1)S(1)} %fusion.2), channel_id=1, source_target_pairs={{0,16},{16,0},{1,17},{17,1},{2,18},{18,2},{3,19},{19,3},{4,20},{20... | collective-permute-start | bytes 688136 | tf_op jit(solution)/shard_map/ppermute | solution.py:24

commit v9 on v8

--- a/solution.py
+++ b/solution.py
@@ -137,6 +137,10 @@
     combined = combined + jnp.pad(from_left_p, ((0, 0), (0, 2 * span)))
     rows_here = combined.astype(jnp.bfloat16)[None]
     group = lax.axis_index("grp")
+    if lax.axis_size("grp") == 2:
+        partner = partner_2(rows_here, "grp", 0)
+        joined = jnp.concatenate([rows_here, rows_here], axis=0)
+        return lax.dynamic_update_slice_in_dim(joined, partner, 1 - group, axis=0)
     joined = rows_here
     for section_bit in range(lax.axis_size("grp").bit_length() - 1):
         partner = partner_2(joined, "grp", section_bit)

time: 48.2 us -> 48.1 us (level)
  waiting for transfers between devices: 5.43 us -> 4.62 us
  local copies, waits for them, and re-layouts: 0.85 us -> 1.56 us
    select_n x1 -> x0, other arithmetic: 0.84 us -> none  [local(): jnp.where(is_upper, jnp.concatenate([partner, joined], axis=0), jnp.conca...]
    ppermute x1, waiting for transfers between devices: 4 us -> 3.2 us  [partner_2(): lax.ppermute(x, axis, [(i, i ^ 1 << bit) for i in range(lax.axis_size(axi...]
    concatenate x0 -> x1, other arithmetic: none -> 0.8 us  [local(): joined = jnp.concatenate([rows_here, rows_here], axis=0)]
    dynamic_update_slice x0 -> x1, local copies, waits for them, and re-layouts: none -> 0.71 us  [local(): return lax.dynamic_update_slice_in_dim(joined, partner, 1 - group, axis=0)]
  transfers between devices with their start and end apart: 5 -> 5, of which waited for: 2 -> 2; matrix products, arithmetic and copies ran while one was open for 2% -> 4% of each run, Pallas kernels for 5% -> 5%
where the time goes in v9:
time: 48.1 us; the launch traced here: 47.8 us
  starting transfers between devices  29.3 us (61%)
  Pallas kernels  7.52 us (16%)
  other arithmetic  4.67 us (10%)
  waiting for transfers between devices  4.62 us (10%)
  local copies, waits for them, and re-layouts  1.56 us (3%)
    ppermute x1, starting transfers between devices, partner_2(): lax.ppermute(x, axis, [(i, i ^ 1 << bit) for i in range(lax.axis_size(axi...  17 us
    ppermute x4, starting transfers between devices, shifted(): return lax.ppermute(x, axis, pairs)  12.3 us
    pallas_call x1, Pallas kernels, products(): pl.pallas_call(product_kernel, out_shape=[jax.ShapeDtypeStruct((NC * B, w...  5.11 us
    ppermute x1, waiting for transfers between devices, partner_2(): lax.ppermute(x, axis, [(i, i ^ 1 << bit) for i in range(lax.axis_size(axi...  3.2 us
    pallas_call x1, Pallas kernels, products(): pl.pallas_call(own_kernel, out_shape=[jax.ShapeDtypeStruct((RB * B, windo...  2.41 us
    ppermute x4, waiting for transfers between devices, shifted(): return lax.ppermute(x, axis, pairs)  1.43 us
    broadcast_in_dim x1, other arithmetic, local(): rows_here = combined.astype(jnp.bfloat16)[None]  1.02 us
    concatenate x1, other arithmetic, local(): payload = jnp.concatenate([p_blocks, tag], axis=0)  0.98 us
  transfers between devices with their start and end apart: 5, of which 2 were waited for; matrix products, arithmetic and copies ran while one was open for 4% of the time, Pallas kernels for 5%

profile of v9, /device:TPU:0, one launch (start us, length us, event | category | flops | bytes accessed | tf_op | source)
XLA Modules:
  0.0 47.8 jit_solution(18423803013883057323)
XLA Ops:
  0.0 0.0 copy-start.1
  0.0 0.7 %copy-done.1 = s32[8,4]{0,1:T(4,128)S(1)} copy-done((s32[8,4]{0,1:T(4,128)S(1)}, s32[8,4]{0,1:T(4,128)}, u32[]{:S(2)}) %copy-start.1) | copy-done | bytes 152
  0.7 0.1 copy.13
  0.8 0.0 copy-start
  0.8 1.0 %fusion.1 = bf16[528,256]{1,0:T(8,128)(2,1)S(1)} fusion(bf16[8,4]{1,0:T(8,128)(2,1)S(1)} %convert_element_type.18, bf16[512,256]{1,0:T(8,128)(2,1)} %pm_ref.1), kind=kLoop, calls=%fused_computation.4 | loop fusion | flops 811008 | bytes 532544 | tf_op jit(solution)/shard_map/concatenate | solution.py:121
  1.8 1.3 %collective-permute-start.1 = (bf16[528,256]{1,0:T(8,128)(2,1)S(1)}, bf16[528,256]{1,0:T(8,128)(2,1)S(1)}, u32[]{:S(2)}, u32[]{:S(2)}) collective-permute-start(bf16[528,256]{1,0:T(8,128)(2,1)S(1)} %fusion.1), channel_id=1, source_target_pairs={{1,0},{2,1},{3,2},{4,3},{5,4},{6,5},{7,6},{8,7},{9,8},{10,9},{11,1... | collective-permute-start | bytes 811016 | tf_op jit(solution)/shard_map/ppermute | solution.py:20
  3.1 3.0 %collective-permute-start = (bf16[528,256]{1,0:T(8,128)(2,1)S(1)}, bf16[528,256]{1,0:T(8,128)(2,1)S(1)}, u32[]{:S(2)}, u32[]{:S(2)}) collective-permute-start(bf16[528,256]{1,0:T(8,128)(2,1)S(1)} %fusion.1), channel_id=1, source_target_pairs={{0,1},{1,2},{2,3},{3,4},{4,5},{5,6},{6,7},{7,8},{8,9},{9,10},{10,1... | collective-permute-start | bytes 811016 | tf_op jit(solution)/shard_map/ppermute | solution.py:20
  6.1 0.0 copy-done
  6.1 0.6 %broadcast_subtract_fusion.1.lc_ref = s32[8,12]{1,0:T(8,128)} fusion(s32[8,12]{1,0:T(8,128)S(1)} %copy-done, s32[]{:T(128)S(6)} %mul.10), kind=kLoop, calls=%fused_computation.12 | loop fusion | flops 96 | bytes 772 | tf_op jit(solution)/shard_map/sub | solution.py:130
  6.7 0.6 %pad_add_fusion.1.po_ref = s32[16,4]{1,0:T(8,128)} fusion(s32[8,4]{1,0:T(8,128)S(1)} %get-tuple-element.28, s32[8,4]{1,0:T(8,128)S(1)} %get-tuple-element.27), kind=kLoop, calls=%fused_computation.7 | loop fusion | flops 64 | bytes 512 | tf_op jit(solution)/shard_map/concatenate | solution.py:129
  7.3 2.4 %shard_map.46 = (bf16[512,640]{1,0:T(8,128)(2,1)}, bf16[384,512]{1,0:T(8,128)(2,1)}) custom-call(s32[16,4]{1,0:T(8,128)} %pad_add_fusion.1.po_ref, bf16[512,256]{1,0:T(8,128)(2,1)} %pm_ref.1), custom_call_target="tpu_custom_call" | custom-call | tf_op jit(solution)/shard_map/pallas_call | solution.py:90
  9.7 0.0 collective-permute-done.1.pr_ref
  9.7 0.0 copy-start.2
  9.7 0.0 collective-permute-done.pl_ref
  9.7 0.0 copy-start.3
  9.8 0.7 %pad_add_fusion.pc_ref = s32[16,4]{1,0:T(8,128)} fusion(s32[8,4]{1,0:T(8,128)S(1)} %convert_add_fusion, s32[8,4]{1,0:T(8,128)S(1)} %slice_convert_fusion), kind=kLoop, calls=%fused_computation.6 | loop fusion | flops 64 | bytes 512 | tf_op jit(solution)/shard_map/concatenate | solution.py:128
  10.4 0.0 copy-done.2
  10.5 0.1 copy-done.3
  10.5 5.1 %shard_map.47 = (f32[128,640]{1,0:T(8,128)}, f32[128,640]{1,0:T(8,128)}, f32[128,640]{1,0:T(8,128)}) custom-call(s32[8,12]{1,0:T(8,128)} %broadcast_subtract_fusion.1.lc_ref, s32[16,4]{1,0:T(8,128)} %pad_add_fusion.pc_ref, bf16[512,768]{1,0:T(8,128)(2,1)} %a_ref.1, bf16[528,256]{1,0:T(8,128)(2,1)} %copy-done.3, bf16[528,256]{1,0:T(8,128)(2,1)} %copy-done.2, ...), custom_call_target="tpu_custom_call" | custom-call | flops 754974720 | bytes 4194304 | tf_op jit(solution)/shard_map/pallas_call | solution.py:99
  15.6 1.3 %collective-permute-start.2 = (f32[128,640]{1,0:T(8,128)}, f32[128,640]{1,0:T(8,128)S(1)}, u32[]{:S(2)}, u32[]{:S(2)}) collective-permute-start(f32[128,640]{1,0:T(8,128)} %get-tuple-element.25), channel_id=1, source_target_pairs={{1,0},{2,1},{3,2},{4,3},{5,4},{6,5},{7,6},{8,7},{9,8},{10,9},{11,1... | collective-permute-start | bytes 983048 | tf_op jit(solution)/shard_map/ppermute | solution.py:20
  16.9 6.7 %collective-permute-start.3 = (f32[128,640]{1,0:T(8,128)}, f32[128,640]{1,0:T(8,128)S(1)}, u32[]{:S(2)}, u32[]{:S(2)}) collective-permute-start(f32[128,640]{1,0:T(8,128)} %get-tuple-element.26), channel_id=1, source_target_pairs={{0,1},{1,2},{2,3},{3,4},{4,5},{5,6},{6,7},{7,8},{8,9},{9,10},{10,1... | collective-permute-start | bytes 983048 | tf_op jit(solution)/shard_map/ppermute | solution.py:20
  23.6 0.0 collective-permute-done.2
  23.6 1.4 %collective-permute-done.3 = f32[128,640]{1,0:T(8,128)S(1)} collective-permute-done((f32[128,640]{1,0:T(8,128)}, f32[128,640]{1,0:T(8,128)S(1)}, u32[]{:S(2)}, u32[]{:S(2)}) %collective-permute-start.3) | collective-permute-done | bytes 327712 | tf_op jit(solution)/shard_map/ppermute | solution.py:20
  25.1 1.0 %fusion.2 = bf16[1,128,896]{2,1,0:T(8,128)(2,1)S(1)} fusion(f32[128,640]{1,0:T(8,128)S(1)} %collective-permute-done.3, f32[128,640]{1,0:T(8,128)S(1)} %collective-permute-done.2, f32[128,640]{1,0:T(8,128)} %get-tuple-element.24), kind=kLoop, calls=%fused_computation.5 | loop fusion | flops 344064 | bytes 1212416 | tf_op jit(solution)/shard_map/broadcast_in_dim | solution.py:138
  26.1 17.0 %collective-permute-start.4 = (bf16[1,128,896]{2,1,0:T(8,128)(2,1)S(1)}, bf16[1,128,896]{2,1,0:T(8,128)(2,1)S(1)}, u32[]{:S(2)}, u32[]{:S(2)}) collective-permute-start(bf16[1,128,896]{2,1,0:T(8,128)(2,1)S(1)} %fusion.2), channel_id=1, source_target_pairs={{0,16},{16,0},{1,17},{17,1},{2,18},{18,2},{3,19},{19,3},{4,20},{20... | collective-permute-start | bytes 688136 | tf_op jit(solution)/shard_map/ppermute | solution.py:24
  43.1 0.8 %pad_maximum_fusion = bf16[2,128,896]{2,1,0:T(8,128)(2,1)} fusion(bf16[1,128,896]{2,1,0:T(8,128)(2,1)S(1)} %fusion.2), kind=kLoop, calls=%fused_computation.2 | loop fusion | flops 229376 | bytes 688128 | tf_op jit(solution)/shard_map/concatenate | solution.py:142
  43.9 3.2 %collective-permute-done.4 = bf16[1,128,896]{2,1,0:T(8,128)(2,1)S(1)} collective-permute-done((bf16[1,128,896]{2,1,0:T(8,128)(2,1)S(1)}, bf16[1,128,896]{2,1,0:T(8,128)(2,1)S(1)}, u32[]{:S(2)}, u32[]{:S(2)}) %collective-permute-start.4) | collective-permute-done | bytes 229408 | tf_op jit(solution)/shard_map/ppermute | solution.py:24
  47.1 0.7 %constant_dynamic-update-slice_fusion = bf16[2,128,896]{2,1,0:T(8,128)(2,1)} fusion(bf16[2,128,896]{2,1,0:T(8,128)(2,1)} %pad_maximum_fusion, bf16[1,128,896]{2,1,0:T(8,128)(2,1)S(1)} %collective-permute-done.4, s32[]{:T(128)S(6)} %select_n.3), kind=kLoop, calls=%fused_computation.13 | loop fusion | bytes 458756 | tf_op jit(solution)/shard_map/dynamic_update_slice | solution.py:143
  (4 shorter events, 0.0 us)
Async XLA Ops:
  0.0 0.7 %copy-start.1 = (s32[8,4]{0,1:T(4,128)S(1)}, s32[8,4]{0,1:T(4,128)}, u32[]{:S(2)}) copy-start(s32[8,4]{0,1:T(4,128)} %param.9) | copy-start | bytes 388
  0.8 5.3 %copy-start = (s32[8,12]{1,0:T(8,128)S(1)}, s32[8,12]{1,0:T(8,128)}, u32[]{:S(2)}) copy-start(s32[8,12]{1,0:T(8,128)} %param.7) | copy-start | bytes 1156
  1.8 8.0 %collective-permute-start.1 = (bf16[528,256]{1,0:T(8,128)(2,1)S(1)}, bf16[528,256]{1,0:T(8,128)(2,1)S(1)}, u32[]{:S(2)}, u32[]{:S(2)}) collective-permute-start(bf16[528,256]{1,0:T(8,128)(2,1)S(1)} %fusion.1), channel_id=1, source_target_pairs={{1,0},{2,1},{3,2},{4,3},{5,4},{6,5},{7,6},{8,7},{9,8},{10,9},{11,1... | collective-permute-start | bytes 811016 | tf_op jit(solution)/shard_map/ppermute | solution.py:20
  3.1 6.7 %collective-permute-start = (bf16[528,256]{1,0:T(8,128)(2,1)S(1)}, bf16[528,256]{1,0:T(8,128)(2,1)S(1)}, u32[]{:S(2)}, u32[]{:S(2)}) collective-permute-start(bf16[528,256]{1,0:T(8,128)(2,1)S(1)} %fusion.1), channel_id=1, source_target_pairs={{0,1},{1,2},{2,3},{3,4},{4,5},{5,6},{6,7},{7,8},{8,9},{9,10},{10,1... | collective-permute-start | bytes 811016 | tf_op jit(solution)/shard_map/ppermute | solution.py:20
  9.7 0.7 %copy-start.2 = (bf16[528,256]{1,0:T(8,128)(2,1)}, bf16[528,256]{1,0:T(8,128)(2,1)S(1)}, u32[]{:S(2)}) copy-start(bf16[528,256]{1,0:T(8,128)(2,1)S(1)} %collective-permute-done.1.pr_ref) | copy-start | bytes 811012
  9.7 0.8 %copy-start.3 = (bf16[528,256]{1,0:T(8,128)(2,1)}, bf16[528,256]{1,0:T(8,128)(2,1)S(1)}, u32[]{:S(2)}) copy-start(bf16[528,256]{1,0:T(8,128)(2,1)S(1)} %collective-permute-done.pl_ref) | copy-start | bytes 811012
  15.6 8.0 %collective-permute-start.2 = (f32[128,640]{1,0:T(8,128)}, f32[128,640]{1,0:T(8,128)S(1)}, u32[]{:S(2)}, u32[]{:S(2)}) collective-permute-start(f32[128,640]{1,0:T(8,128)} %get-tuple-element.25), channel_id=1, source_target_pairs={{1,0},{2,1},{3,2},{4,3},{5,4},{6,5},{7,6},{8,7},{9,8},{10,9},{11,1... | collective-permute-start | bytes 983048 | tf_op jit(solution)/shard_map/ppermute | solution.py:20
  16.9 8.1 %collective-permute-start.3 = (f32[128,640]{1,0:T(8,128)}, f32[128,640]{1,0:T(8,128)S(1)}, u32[]{:S(2)}, u32[]{:S(2)}) collective-permute-start(f32[128,640]{1,0:T(8,128)} %get-tuple-element.26), channel_id=1, source_target_pairs={{0,1},{1,2},{2,3},{3,4},{4,5},{5,6},{6,7},{7,8},{8,9},{9,10},{10,1... | collective-permute-start | bytes 983048 | tf_op jit(solution)/shard_map/ppermute | solution.py:20
  26.1 21.0 %collective-permute-start.4 = (bf16[1,128,896]{2,1,0:T(8,128)(2,1)S(1)}, bf16[1,128,896]{2,1,0:T(8,128)(2,1)S(1)}, u32[]{:S(2)}, u32[]{:S(2)}) collective-permute-start(bf16[1,128,896]{2,1,0:T(8,128)(2,1)S(1)} %fusion.2), channel_id=1, source_target_pairs={{0,16},{16,0},{1,17},{17,1},{2,18},{18,2},{3,19},{19,3},{4,20},{20... | collective-permute-start | bytes 688136 | tf_op jit(solution)/shard_map/ppermute | solution.py:24

commit v10 on v9

--- a/solution.py
+++ b/solution.py
@@ -20,6 +20,20 @@
     return lax.ppermute(x, axis, pairs)
 
 
+def inside(x, by):
+    n_dev, n = lax.axis_size("dev"), lax.axis_size(LINE)
+    pairs = [(i, i + by) for i in range(n) if 0 <= i + by < n and i // n_dev == (i + by) // n_dev]
+    return lax.ppermute(x, LINE, pairs)
+
+
+def across(x):
+    n_dev, n = lax.axis_size("dev"), lax.axis_size(LINE)
+    pairs = []
+    for b in range(n_dev, n, n_dev):
+        pairs += [(b - 1, b), (b, b - 1)]
+    return lax.ppermute(x, LINE, pairs)
+
+
 def partner_2(x, axis, bit):
     return lax.ppermute(x, axis, [(i, i ^ 1 << bit) for i in range(lax.axis_size(axis))])
 
@@ -32,9 +46,13 @@
     return pl.ds(pl.multiple_of(r * B, B), B)
 
 
-def spread_rows(ps_ref, base, src_ref, pc_ref, pc_base, side):
+def spread_rows(ps_ref, base, src_ref, pc_ref, pc_base, side, edge=None):
     for r in range(RB):
-        blk = src_ref[r * B : (r + 1) * B, :].astype(jnp.float32)
+        blk = src_ref[r * B : (r + 1) * B, :]
+        if edge is not None:
+            edge_ref, use_edge = edge
+            blk = jnp.where(use_edge, edge_ref[r * B : (r + 1) * B, :], blk)
+        blk = blk.astype(jnp.float32)
         halves = [blk[:, 0:HALF], blk[:, HALF : 2 * HALF]]
         swapped = [pltpu.roll(h, B, 1) for h in halves]
         rows = slice((base + r) * B, (base + r + 1) * B)
@@ -62,28 +80,32 @@
 
 
 def product_kernel(
-    lc_ref, pc_ref, a_ref, pl_ref, pr_ref, pso_ref, st_ref, prev_ref, here_ref, next_ref, ps_ref, panel_ref, ap_ref
+    flag_ref, lc_ref, pc_ref, a_ref, pl_ref, pr_ref, pe_ref, pso_ref, st_ref,
+    prev_ref, here_ref, next_ref, edge_ref, ps_ref, panel_ref, ap_ref,
 ):
+    first = flag_ref[0] == 1
+    last = flag_ref[1] == 1
     side = lax.broadcasted_iota(jnp.int32, (B, HALF), 1) // B
     near = RB * B
     ps_ref[0:near, :] = jnp.zeros((near, ps_ref.shape[1]), ps_ref.dtype)
     ps_ref[2 * near : 3 * near, :] = jnp.zeros((near, ps_ref.shape[1]), ps_ref.dtype)
     ps_ref[near : 2 * near, :] = pso_ref[...]
-    spread_rows(ps_ref, 0, pl_ref, pc_ref, 0, side)
-    spread_rows(ps_ref, 2 * RB, pr_ref, pc_ref, RB, side)
+    spread_rows(ps_ref, 0, pl_ref, pc_ref, 0, side, (pe_ref, first))
+    spread_rows(ps_ref, 2 * RB, pr_ref, pc_ref, RB, side, (pe_ref, last))
     for i in range(RB):
         for k in range(KA):
             panel_ref[k * B : (k + 1) * B, :] = ps_ref[rows_at(lc_ref[i, k]), :]
         ap = jnp.dot(a_ref[i * B : (i + 1) * B, :], panel_ref[...], preferred_element_type=jnp.float32)
         ap_ref[i * B : (i + 1) * B, :] = ap.astype(ap_ref.dtype)
     span = NC * B
-    for o, out_ref in enumerate((prev_ref, here_ref, next_ref)):
-        out_ref[...] = jnp.dot(
-            st_ref[o * span : (o + 1) * span, :], ap_ref[...], preferred_element_type=jnp.float32
-        )
+    res = jnp.dot(st_ref[...], ap_ref[...], preferred_element_type=jnp.float32)
+    prev_ref[...] = res[0:span]
+    here_ref[...] = res[span : 2 * span]
+    next_ref[...] = res[2 * span : 3 * span]
+    edge_ref[...] = jnp.where(last, res[2 * span : 3 * span], res[0:span])
 
 
-def products(lc, pc_side, po, a_blocks, left, own, right):
+def products(flags, lc, pc_side, po, a_blocks, left, own, right, edge):
     smem = pl.BlockSpec(memory_space=pltpu.SMEM)
     vmem = pl.BlockSpec(memory_space=pltpu.VMEM)
     window = 5 * NC * B
@@ -98,9 +120,9 @@
     )(po, own)
     return pl.pallas_call(
         product_kernel,
-        out_shape=[jax.ShapeDtypeStruct((NC * B, window), jnp.float32)] * 3,
-        in_specs=[smem] * 2 + [vmem] * 5,
-        out_specs=[vmem] * 3,
+        out_shape=[jax.ShapeDtypeStruct((NC * B, window), jnp.float32)] * 4,
+        in_specs=[smem] * 3 + [vmem] * 6,
+        out_specs=[vmem] * 4,
         scratch_shapes=[
             pltpu.VMEM((3 * RB * B, window), jnp.bfloat16),
             pltpu.VMEM((KA * B, window), jnp.bfloat16),
@@ -111,7 +133,7 @@
             bytes_accessed=4 * 1024 * 1024,
             transcendentals=0,
         ),
-    )(lc, pc_side, a_blocks, left, right, pso, st)
+    )(flags, lc, pc_side, a_blocks, left, right, edge, pso, st)
 
 
 def local(a_blocks, a_cols, p_blocks, p_cols):
@@ -119,18 +141,33 @@
     rel = p_cols - (q - 1) * NC
     tag = jnp.zeros((16, KP * B), jnp.bfloat16).at[:RB, :KP].set(rel.astype(jnp.bfloat16))
     payload = jnp.concatenate([p_blocks, tag], axis=0)
-    from_left = shifted(payload, LINE, 1)
-    from_right = shifted(payload, LINE, -1)
+    n_dev, n = lax.axis_size("dev"), lax.axis_size(LINE)
+    d, g = lax.axis_index("dev"), lax.axis_index("grp")
+    first = (d == 0) & (q > 0)
+    last = (d == n_dev - 1) & (q < n - 1)
+    flags = jnp.stack([first, last]).astype(jnp.int32)
+    from_left = inside(payload, 1)
+    from_right = inside(payload, -1)
+    edge = across(payload)
 
     def cols(x, shift):
         return x[RB * B : RB * B + RB, :KP].astype(jnp.int32) + shift
 
-    pc_side = jnp.concatenate([cols(from_left, 0), cols(from_right, 2 * NC)], axis=0)
+    pc_side = jnp.concatenate(
+        [
+            jnp.where(first, cols(edge, 0), cols(from_left, 0)),
+            jnp.where(last, cols(edge, 2 * NC), cols(from_right, 2 * NC)),
+        ],
+        axis=0,
+    )
     po = jnp.concatenate([rel + NC, rel], axis=0)
     lc = a_cols - (q - 1) * RB
-    prev_rows, here_rows, next_rows = products(lc, pc_side, po, a_blocks, from_left, p_blocks, from_right)
-    from_right_p = shifted(prev_rows, LINE, -1)
-    from_left_p = shifted(next_rows, LINE, 1)
+    prev_rows, here_rows, next_rows, edge_rows = products(
+        flags, lc, pc_side, po, a_blocks, from_left, p_blocks, from_right, edge
+    )
+    edge_p = across(edge_rows)
+    from_right_p = jnp.where(last, edge_p, inside(prev_rows, -1))
+    from_left_p = jnp.where(first, edge_p, inside(next_rows, 1))
     span = NC * B
     combined = jnp.pad(here_rows, ((0, 0), (span, span)))
     combined = combined + jnp.pad(from_right_p, ((0, 0), (2 * span, 0)))

time: 48.1 us -> 45.8 us (0.952); the launches traced: 47.8 us -> 45 us
  starting transfers between devices: 29.3 us -> 25.1 us
  waiting for transfers between devices: 4.62 us -> 5.82 us
    ppermute x1, starting transfers between devices: 17 us -> 12.6 us  [partner_2(): lax.ppermute(x, axis, [(i, i ^ 1 << bit) for i in range(lax.axis_size(axi...]
    ppermute x1, waiting for transfers between devices: 3.2 us -> 4.4 us  [partner_2(): lax.ppermute(x, axis, [(i, i ^ 1 << bit) for i in range(lax.axis_size(axi...]
    broadcast_in_dim x1, other arithmetic: 1.02 us -> 0.05 us  [local(): rows_here = combined.astype(jnp.bfloat16)[None]]
    convert_element_type x1, other arithmetic: 0.01 us -> 0.6 us  [local(): flags = jnp.stack([first, last]).astype(jnp.int32)]
    ppermute x4 -> x6, starting transfers between devices: 12.3 us -> 12.5 us  [the longest x4 11.1 us: inside(): return lax.ppermute(x, LINE, pairs)]
    ppermute x4 -> x6, waiting for transfers between devices: 1.43 us -> 1.42 us  [the longest x4 1.42 us: inside(): return lax.ppermute(x, LINE, pairs)]
  transfers between devices with their start and end apart: 5 -> 7, of which waited for: 2 -> 2; matrix products, arithmetic and copies ran while one was open for 4% -> 6% of each run, Pallas kernels for 5% -> 5%
where the time goes in v10:
time: 45.8 us; the launch traced here: 45 us
  starting transfers between devices  25.1 us (55%)
  Pallas kernels  7.83 us (17%)
  waiting for transfers between devices  5.82 us (13%)
  other arithmetic  4.37 us (10%)
  local copies, waits for them, and re-layouts  1.66 us (4%)
    ppermute x1, starting transfers between devices, partner_2(): lax.ppermute(x, axis, [(i, i ^ 1 << bit) for i in range(lax.axis_size(axi...  12.6 us
    ppermute x4, starting transfers between devices, inside(): return lax.ppermute(x, LINE, pairs)  11.1 us
    pallas_call x1, Pallas kernels, products(): pl.pallas_call(product_kernel, out_shape=[jax.ShapeDtypeStruct((NC * B, w...  5.42 us
    ppermute x1, waiting for transfers between devices, partner_2(): lax.ppermute(x, axis, [(i, i ^ 1 << bit) for i in range(lax.axis_size(axi...  4.4 us
    pallas_call x1, Pallas kernels, products(): pl.pallas_call(own_kernel, out_shape=[jax.ShapeDtypeStruct((RB * B, windo...  2.42 us
    ppermute x4, waiting for transfers between devices, inside(): return lax.ppermute(x, LINE, pairs)  1.42 us
    ppermute x2, starting transfers between devices, across(): return lax.ppermute(x, LINE, pairs)  1.35 us
    concatenate x1, other arithmetic, local(): payload = jnp.concatenate([p_blocks, tag], axis=0)  0.97 us
  transfers between devices with their start and end apart: 7, of which 2 were waited for; matrix products, arithmetic and copies ran while one was open for 6% of the time, Pallas kernels for 5%

profile of v10, /device:TPU:0, one launch (start us, length us, event | category | flops | bytes accessed | tf_op | source)
XLA Modules:
  0.0 45.0 jit_solution(8396909462824910568)
XLA Ops:
  0.0 0.7 %copy-done.2 = s32[8,4]{0,1:T(4,128)S(1)} copy-done((s32[8,4]{0,1:T(4,128)S(1)}, s32[8,4]{0,1:T(4,128)}, u32[]{:S(2)}) %copy-start.2) | copy-done | bytes 152
  0.7 0.1 copy.13
  0.8 1.0 %fusion.1 = bf16[528,256]{1,0:T(8,128)(2,1)S(1)} fusion(bf16[8,4]{1,0:T(8,128)(2,1)S(1)} %convert_element_type.26, bf16[512,256]{1,0:T(8,128)(2,1)} %pm_ref.1), kind=kLoop, calls=%fused_computation.4 | loop fusion | flops 811008 | bytes 532544 | tf_op jit(solution)/shard_map/concatenate | solution.py:143
  1.7 1.3 %collective-permute-start.2 = (bf16[528,256]{1,0:T(8,128)(2,1)S(1)}, bf16[528,256]{1,0:T(8,128)(2,1)S(1)}, u32[]{:S(2)}, u32[]{:S(2)}) collective-permute-start(bf16[528,256]{1,0:T(8,128)(2,1)S(1)} %fusion.1), channel_id=1, source_target_pairs={{1,0},{2,1},{3,2},{4,3},{5,4},{6,5},{7,6},{8,7},{9,8},{10,9},{11,1... | collective-permute-start | bytes 811016 | tf_op jit(solution)/shard_map/ppermute | solution.py:26
  3.0 3.0 %collective-permute-start.1 = (bf16[528,256]{1,0:T(8,128)(2,1)S(1)}, bf16[528,256]{1,0:T(8,128)(2,1)S(1)}, u32[]{:S(2)}, u32[]{:S(2)}) collective-permute-start(bf16[528,256]{1,0:T(8,128)(2,1)S(1)} %fusion.1), channel_id=1, source_target_pairs={{0,1},{1,2},{2,3},{3,4},{4,5},{5,6},{6,7},{7,8},{8,9},{9,10},{10,1... | collective-permute-start | bytes 811016 | tf_op jit(solution)/shard_map/ppermute | solution.py:26
  6.1 0.7 %collective-permute-start = (bf16[528,256]{1,0:T(8,128)(2,1)S(1)}, bf16[528,256]{1,0:T(8,128)(2,1)S(1)}, u32[]{:S(2)}, u32[]{:S(2)}) collective-permute-start(bf16[528,256]{1,0:T(8,128)(2,1)S(1)} %fusion.1), channel_id=1, source_target_pairs={{15,16},{16,15}} | collective-permute-start | bytes 811016 | tf_op jit(solution)/shard_map/ppermute | solution.py:34
  6.8 0.6 %pad_add_fusion.1.po_ref = s32[16,4]{1,0:T(8,128)} fusion(s32[8,4]{1,0:T(8,128)S(1)} %get-tuple-element.30, s32[8,4]{1,0:T(8,128)S(1)} %get-tuple-element.29), kind=kLoop, calls=%fused_computation.9 | loop fusion | flops 64 | bytes 512 | tf_op jit(solution)/shard_map/concatenate | solution.py:163
  7.4 0.6 %add_convert_fusion.1.flag_ref = s32[2]{0:T(128)} fusion(pred[1]{0:T(512)(128)(4,1)} %bitcast.1, pred[1]{0:T(512)(128)(4,1)} %bitcast), kind=kLoop, calls=%fused_computation.16 | loop fusion | flops 4 | bytes 10 | tf_op jit(solution)/shard_map/convert_element_type | solution.py:148
  8.0 2.4 %shard_map.46 = (bf16[512,640]{1,0:T(8,128)(2,1)}, bf16[384,512]{1,0:T(8,128)(2,1)}) custom-call(s32[16,4]{1,0:T(8,128)} %pad_add_fusion.1.po_ref, bf16[512,256]{1,0:T(8,128)(2,1)} %pm_ref.1), custom_call_target="tpu_custom_call" | custom-call | tf_op jit(solution)/shard_map/pallas_call | solution.py:112
  10.4 0.0 copy-done.1
  10.4 0.6 %broadcast_subtract_fusion.1.lc_ref = s32[8,12]{1,0:T(8,128)} fusion(s32[8,12]{1,0:T(8,128)S(1)} %copy-done.1, s32[]{:T(128)S(6)} %mul.10), kind=kLoop, calls=%fused_computation.15 | loop fusion | flops 96 | bytes 772 | tf_op jit(solution)/shard_map/sub | solution.py:164
  11.0 0.0 collective-permute-done.2.pr_ref
  11.0 0.0 collective-permute-done.1.pl_ref
  11.0 0.0 collective-permute-done.pe_ref
  11.1 0.7 %pad_add_fusion.pc_ref = s32[16,4]{1,0:T(8,128)} fusion(s32[8,4]{1,0:T(8,128)S(1)} %get-tuple-element.34, s32[8,4]{1,0:T(8,128)S(1)} %get-tuple-element.33), kind=kLoop, calls=%fused_computation.8 | loop fusion | flops 64 | bytes 512 | tf_op jit(solution)/shard_map/concatenate | solution.py:156
  11.8 0.0 copy-done.3
  11.8 0.1 copy-done.4
  11.9 0.1 copy-done.5
  11.9 5.4 %shard_map.47 = (f32[128,640]{1,0:T(8,128)}, f32[128,640]{1,0:T(8,128)}, f32[128,640]{1,0:T(8,128)}, f32[128,640]{1,0:T(8,128)}) custom-call(s32[2]{0:T(128)} %add_convert_fusion.1.flag_ref, s32[8,12]{1,0:T(8,128)} %broadcast_subtract_fusion.1.lc_ref, s32[16,4]{1,0:T(8,128)} %pad_add_fusion.pc_ref, bf16[512,768]{1,0:T(8,128)(2,1)} %a_ref.1, ...), custom_call_target="tpu_custom_call" | custom-call | flops 754974720 | bytes 4194304 | tf_op jit(solution)/shard_map/pallas_call | solution.py:121
  17.4 0.7 %collective-permute-start.3 = (f32[128,640]{1,0:T(8,128)}, f32[128,640]{1,0:T(8,128)S(1)}, u32[]{:S(2)}, u32[]{:S(2)}) collective-permute-start(f32[128,640]{1,0:T(8,128)} %get-tuple-element.26), channel_id=1, source_target_pairs={{15,16},{16,15}} | collective-permute-start | bytes 983048 | tf_op jit(solution)/shard_map/ppermute | solution.py:34
  18.0 1.3 %collective-permute-start.4 = (f32[128,640]{1,0:T(8,128)}, f32[128,640]{1,0:T(8,128)S(1)}, u32[]{:S(2)}, u32[]{:S(2)}) collective-permute-start(f32[128,640]{1,0:T(8,128)} %get-tuple-element.27), channel_id=1, source_target_pairs={{1,0},{2,1},{3,2},{4,3},{5,4},{6,5},{7,6},{8,7},{9,8},{10,9},{11,1... | collective-permute-start | bytes 983048 | tf_op jit(solution)/shard_map/ppermute | solution.py:26
  19.3 0.0 copy-start
  19.3 5.5 %collective-permute-start.5 = (f32[128,640]{1,0:T(8,128)}, f32[128,640]{1,0:T(8,128)S(1)}, u32[]{:S(2)}, u32[]{:S(2)}) collective-permute-start(f32[128,640]{1,0:T(8,128)} %get-tuple-element.28), channel_id=1, source_target_pairs={{0,1},{1,2},{2,3},{3,4},{4,5},{5,6},{6,7},{7,8},{8,9},{9,10},{10,1... | collective-permute-start | bytes 983048 | tf_op jit(solution)/shard_map/ppermute | solution.py:26
  24.8 0.0 collective-permute-done.3
  24.9 0.0 collective-permute-done.4
  24.9 1.4 %collective-permute-done.5 = f32[128,640]{1,0:T(8,128)S(1)} collective-permute-done((f32[128,640]{1,0:T(8,128)}, f32[128,640]{1,0:T(8,128)S(1)}, u32[]{:S(2)}, u32[]{:S(2)}) %collective-permute-start.5) | collective-permute-done | bytes 327712 | tf_op jit(solution)/shard_map/ppermute | solution.py:26
  26.3 0.1 broadcast_select_fusion.1
  26.3 0.0 copy-done
  26.4 12.6 %collective-permute-start.6 = (bf16[1,128,896]{2,1,0:T(8,128)(2,1)S(1)}, bf16[1,128,896]{2,1,0:T(8,128)(2,1)S(1)}, u32[]{:S(2)}, u32[]{:S(2)}) collective-permute-start(bf16[1,128,896]{2,1,0:T(8,128)(2,1)S(1)} %fusion.2), channel_id=1, source_target_pairs={{0,16},{16,0},{1,17},{17,1},{2,18},{18,2},{3,19},{19,3},{4,20},{20... | collective-permute-start | bytes 688136 | tf_op jit(solution)/shard_map/ppermute | solution.py:38
  39.0 0.8 %pad_maximum_fusion = bf16[2,128,896]{2,1,0:T(8,128)(2,1)} fusion(bf16[1,128,896]{2,1,0:T(8,128)(2,1)S(1)} %fusion.2), kind=kLoop, calls=%fused_computation.2 | loop fusion | flops 229376 | bytes 688128 | tf_op jit(solution)/shard_map/concatenate | solution.py:179
  39.8 4.4 %collective-permute-done.6 = bf16[1,128,896]{2,1,0:T(8,128)(2,1)S(1)} collective-permute-done((bf16[1,128,896]{2,1,0:T(8,128)(2,1)S(1)}, bf16[1,128,896]{2,1,0:T(8,128)(2,1)S(1)}, u32[]{:S(2)}, u32[]{:S(2)}) %collective-permute-start.6) | collective-permute-done | bytes 229408 | tf_op jit(solution)/shard_map/ppermute | solution.py:38
  44.2 0.7 %constant_dynamic-update-slice_fusion = bf16[2,128,896]{2,1,0:T(8,128)(2,1)} fusion(bf16[2,128,896]{2,1,0:T(8,128)(2,1)} %pad_maximum_fusion, bf16[1,128,896]{2,1,0:T(8,128)(2,1)S(1)} %collective-permute-done.6, s32[]{:T(128)S(6)} %select_n.39), kind=kLoop, calls=%fused_computation.17 | loop fusion | bytes 458756 | tf_op jit(solution)/shard_map/dynamic_update_slice | solution.py:180
  (9 shorter events, 0.1 us)
Async XLA Ops:
  0.0 0.7 %copy-start.2 = (s32[8,4]{0,1:T(4,128)S(1)}, s32[8,4]{0,1:T(4,128)}, u32[]{:S(2)}) copy-start(s32[8,4]{0,1:T(4,128)} %param.9) | copy-start | bytes 388
  1.7 9.3 %collective-permute-start.2 = (bf16[528,256]{1,0:T(8,128)(2,1)S(1)}, bf16[528,256]{1,0:T(8,128)(2,1)S(1)}, u32[]{:S(2)}, u32[]{:S(2)}) collective-permute-start(bf16[528,256]{1,0:T(8,128)(2,1)S(1)} %fusion.1), channel_id=1, source_target_pairs={{1,0},{2,1},{3,2},{4,3},{5,4},{6,5},{7,6},{8,7},{9,8},{10,9},{11,1... | collective-permute-start | bytes 811016 | tf_op jit(solution)/shard_map/ppermute | solution.py:26
  3.0 8.0 %collective-permute-start.1 = (bf16[528,256]{1,0:T(8,128)(2,1)S(1)}, bf16[528,256]{1,0:T(8,128)(2,1)S(1)}, u32[]{:S(2)}, u32[]{:S(2)}) collective-permute-start(bf16[528,256]{1,0:T(8,128)(2,1)S(1)} %fusion.1), channel_id=1, source_target_pairs={{0,1},{1,2},{2,3},{3,4},{4,5},{5,6},{6,7},{7,8},{8,9},{9,10},{10,1... | collective-permute-start | bytes 811016 | tf_op jit(solution)/shard_map/ppermute | solution.py:26
  6.1 4.9 %collective-permute-start = (bf16[528,256]{1,0:T(8,128)(2,1)S(1)}, bf16[528,256]{1,0:T(8,128)(2,1)S(1)}, u32[]{:S(2)}, u32[]{:S(2)}) collective-permute-start(bf16[528,256]{1,0:T(8,128)(2,1)S(1)} %fusion.1), channel_id=1, source_target_pairs={{15,16},{16,15}} | collective-permute-start | bytes 811016 | tf_op jit(solution)/shard_map/ppermute | solution.py:34
  8.0 2.4 %copy-start.1 = (s32[8,12]{1,0:T(8,128)S(1)}, s32[8,12]{1,0:T(8,128)}, u32[]{:S(2)}) copy-start(s32[8,12]{1,0:T(8,128)} %param.7) | copy-start | bytes 1156
  11.0 0.7 %copy-start.3 = (bf16[528,256]{1,0:T(8,128)(2,1)}, bf16[528,256]{1,0:T(8,128)(2,1)S(1)}, u32[]{:S(2)}) copy-start(bf16[528,256]{1,0:T(8,128)(2,1)S(1)} %collective-permute-done.2.pr_ref) | copy-start | bytes 811012
  11.0 0.8 %copy-start.4 = (bf16[528,256]{1,0:T(8,128)(2,1)}, bf16[528,256]{1,0:T(8,128)(2,1)S(1)}, u32[]{:S(2)}) copy-start(bf16[528,256]{1,0:T(8,128)(2,1)S(1)} %collective-permute-done.1.pl_ref) | copy-start | bytes 811012
  11.0 0.9 %copy-start.5 = (bf16[528,256]{1,0:T(8,128)(2,1)}, bf16[528,256]{1,0:T(8,128)(2,1)S(1)}, u32[]{:S(2)}) copy-start(bf16[528,256]{1,0:T(8,128)(2,1)S(1)} %collective-permute-done.pe_ref) | copy-start | bytes 811012
  17.4 7.5 %collective-permute-start.3 = (f32[128,640]{1,0:T(8,128)}, f32[128,640]{1,0:T(8,128)S(1)}, u32[]{:S(2)}, u32[]{:S(2)}) collective-permute-start(f32[128,640]{1,0:T(8,128)} %get-tuple-element.26), channel_id=1, source_target_pairs={{15,16},{16,15}} | collective-permute-start | bytes 983048 | tf_op jit(solution)/shard_map/ppermute | solution.py:34
  18.0 6.8 %collective-permute-start.4 = (f32[128,640]{1,0:T(8,128)}, f32[128,640]{1,0:T(8,128)S(1)}, u32[]{:S(2)}, u32[]{:S(2)}) collective-permute-start(f32[128,640]{1,0:T(8,128)} %get-tuple-element.27), channel_id=1, source_target_pairs={{1,0},{2,1},{3,2},{4,3},{5,4},{6,5},{7,6},{8,7},{9,8},{10,9},{11,1... | collective-permute-start | bytes 983048 | tf_op jit(solution)/shard_map/ppermute | solution.py:26
  19.3 7.0 %copy-start = (f32[128,640]{1,0:T(8,128)S(1)}, f32[128,640]{1,0:T(8,128)}, u32[]{:S(2)}) copy-start(f32[128,640]{1,0:T(8,128)} %get-tuple-element.25) | copy-start | bytes 983044
  19.3 6.9 %collective-permute-start.5 = (f32[128,640]{1,0:T(8,128)}, f32[128,640]{1,0:T(8,128)S(1)}, u32[]{:S(2)}, u32[]{:S(2)}) collective-permute-start(f32[128,640]{1,0:T(8,128)} %get-tuple-element.28), channel_id=1, source_target_pairs={{0,1},{1,2},{2,3},{3,4},{4,5},{5,6},{6,7},{7,8},{8,9},{9,10},{10,1... | collective-permute-start | bytes 983048 | tf_op jit(solution)/shard_map/ppermute | solution.py:26
  26.4 17.8 %collective-permute-start.6 = (bf16[1,128,896]{2,1,0:T(8,128)(2,1)S(1)}, bf16[1,128,896]{2,1,0:T(8,128)(2,1)S(1)}, u32[]{:S(2)}, u32[]{:S(2)}) collective-permute-start(bf16[1,128,896]{2,1,0:T(8,128)(2,1)S(1)} %fusion.2), channel_id=1, source_target_pairs={{0,16},{16,0},{1,17},{17,1},{2,18},{18,2},{3,19},{19,3},{4,20},{20... | collective-permute-start | bytes 688136 | tf_op jit(solution)/shard_map/ppermute | solution.py:38

commit v11 on v10

--- a/solution.py
+++ b/solution.py
@@ -4,6 +4,7 @@
 from jax.experimental import pallas as pl
 from jax.experimental.pallas import tpu as pltpu
 from jax.sharding import PartitionSpec as P
+
 
 B = 64
 KA = 12
@@ -12,12 +13,6 @@
 RB = 8
 LINE = ("grp", "dev")
 HALF = 128
-
-
-def shifted(x, axis, by):
-    peers = lax.axis_size(axis)
-    pairs = [(i, i + by) for i in range(peers) if 0 <= i + by < peers]
-    return lax.ppermute(x, axis, pairs)
 
 
 def inside(x, by):
@@ -142,13 +137,13 @@
     tag = jnp.zeros((16, KP * B), jnp.bfloat16).at[:RB, :KP].set(rel.astype(jnp.bfloat16))
     payload = jnp.concatenate([p_blocks, tag], axis=0)
     n_dev, n = lax.axis_size("dev"), lax.axis_size(LINE)
-    d, g = lax.axis_index("dev"), lax.axis_index("grp")
+    d = lax.axis_index("dev")
     first = (d == 0) & (q > 0)
     last = (d == n_dev - 1) & (q < n - 1)
     flags = jnp.stack([first, last]).astype(jnp.int32)
+    edge = across(payload)
     from_left = inside(payload, 1)
     from_right = inside(payload, -1)
-    edge = across(payload)
 
     def cols(x, shift):
         return x[RB * B : RB * B + RB, :KP].astype(jnp.int32) + shift

time: 45.8 us -> 45.8 us (level)
  no operation moved by 1% of the time
where the time goes in v11:
time: 45.8 us; the launch traced here: 45 us
  starting transfers between devices  25.1 us (55%)
  Pallas kernels  7.83 us (17%)
  waiting for transfers between devices  5.82 us (13%)
  other arithmetic  4.37 us (10%)
  local copies, waits for them, and re-layouts  1.66 us (4%)
    ppermute x1, starting transfers between devices, partner_2(): lax.ppermute(x, axis, [(i, i ^ 1 << bit) for i in range(lax.axis_size(axi...  12.6 us
    ppermute x4, starting transfers between devices, inside(): return lax.ppermute(x, LINE, pairs)  11.1 us
    pallas_call x1, Pallas kernels, products(): pl.pallas_call(product_kernel, out_shape=[jax.ShapeDtypeStruct((NC * B, w...  5.41 us
    ppermute x1, waiting for transfers between devices, partner_2(): lax.ppermute(x, axis, [(i, i ^ 1 << bit) for i in range(lax.axis_size(axi...  4.4 us
    pallas_call x1, Pallas kernels, products(): pl.pallas_call(own_kernel, out_shape=[jax.ShapeDtypeStruct((RB * B, windo...  2.42 us
    ppermute x4, waiting for transfers between devices, inside(): return lax.ppermute(x, LINE, pairs)  1.42 us
    ppermute x2, starting transfers between devices, across(): return lax.ppermute(x, LINE, pairs)  1.35 us
    concatenate x1, other arithmetic, local(): payload = jnp.concatenate([p_blocks, tag], axis=0)  0.97 us
  transfers between devices with their start and end apart: 7, of which 2 were waited for; matrix products, arithmetic and copies ran while one was open for 6% of the time, Pallas kernels for 5%

profile of v11, /device:TPU:0, one launch (start us, length us, event | category | flops | bytes accessed | tf_op | source)
XLA Modules:
  0.0 45.0 jit_solution(8396909462824910568)
XLA Ops:
  0.0 0.7 %copy-done.2 = s32[8,4]{0,1:T(4,128)S(1)} copy-done((s32[8,4]{0,1:T(4,128)S(1)}, s32[8,4]{0,1:T(4,128)}, u32[]{:S(2)}) %copy-start.2) | copy-done | bytes 152
  0.7 0.1 copy.13
  0.8 1.0 %fusion.1 = bf16[528,256]{1,0:T(8,128)(2,1)S(1)} fusion(bf16[8,4]{1,0:T(8,128)(2,1)S(1)} %convert_element_type.26, bf16[512,256]{1,0:T(8,128)(2,1)} %pm_ref.1), kind=kLoop, calls=%fused_computation.4 | loop fusion | flops 811008 | bytes 532544 | tf_op jit(solution)/shard_map/concatenate | solution.py:138
  1.7 1.3 %collective-permute-start.2 = (bf16[528,256]{1,0:T(8,128)(2,1)S(1)}, bf16[528,256]{1,0:T(8,128)(2,1)S(1)}, u32[]{:S(2)}, u32[]{:S(2)}) collective-permute-start(bf16[528,256]{1,0:T(8,128)(2,1)S(1)} %fusion.1), channel_id=1, source_target_pairs={{1,0},{2,1},{3,2},{4,3},{5,4},{6,5},{7,6},{8,7},{9,8},{10,9},{11,1... | collective-permute-start | bytes 811016 | tf_op jit(solution)/shard_map/ppermute | solution.py:21
  3.0 3.0 %collective-permute-start.1 = (bf16[528,256]{1,0:T(8,128)(2,1)S(1)}, bf16[528,256]{1,0:T(8,128)(2,1)S(1)}, u32[]{:S(2)}, u32[]{:S(2)}) collective-permute-start(bf16[528,256]{1,0:T(8,128)(2,1)S(1)} %fusion.1), channel_id=1, source_target_pairs={{0,1},{1,2},{2,3},{3,4},{4,5},{5,6},{6,7},{7,8},{8,9},{9,10},{10,1... | collective-permute-start | bytes 811016 | tf_op jit(solution)/shard_map/ppermute | solution.py:21
  6.1 0.7 %collective-permute-start = (bf16[528,256]{1,0:T(8,128)(2,1)S(1)}, bf16[528,256]{1,0:T(8,128)(2,1)S(1)}, u32[]{:S(2)}, u32[]{:S(2)}) collective-permute-start(bf16[528,256]{1,0:T(8,128)(2,1)S(1)} %fusion.1), channel_id=1, source_target_pairs={{15,16},{16,15}} | collective-permute-start | bytes 811016 | tf_op jit(solution)/shard_map/ppermute | solution.py:29
  6.8 0.6 %pad_add_fusion.1.po_ref = s32[16,4]{1,0:T(8,128)} fusion(s32[8,4]{1,0:T(8,128)S(1)} %get-tuple-element.30, s32[8,4]{1,0:T(8,128)S(1)} %get-tuple-element.29), kind=kLoop, calls=%fused_computation.9 | loop fusion | flops 64 | bytes 512 | tf_op jit(solution)/shard_map/concatenate | solution.py:158
  7.4 0.6 %add_convert_fusion.1.flag_ref = s32[2]{0:T(128)} fusion(pred[1]{0:T(512)(128)(4,1)} %bitcast.1, pred[1]{0:T(512)(128)(4,1)} %bitcast), kind=kLoop, calls=%fused_computation.16 | loop fusion | flops 4 | bytes 10 | tf_op jit(solution)/shard_map/convert_element_type | solution.py:143
  8.0 2.4 %shard_map.46 = (bf16[512,640]{1,0:T(8,128)(2,1)}, bf16[384,512]{1,0:T(8,128)(2,1)}) custom-call(s32[16,4]{1,0:T(8,128)} %pad_add_fusion.1.po_ref, bf16[512,256]{1,0:T(8,128)(2,1)} %pm_ref.1), custom_call_target="tpu_custom_call" | custom-call | tf_op jit(solution)/shard_map/pallas_call | solution.py:107
  10.4 0.0 copy-done.1
  10.4 0.6 %broadcast_subtract_fusion.1.lc_ref = s32[8,12]{1,0:T(8,128)} fusion(s32[8,12]{1,0:T(8,128)S(1)} %copy-done.1, s32[]{:T(128)S(6)} %mul.10), kind=kLoop, calls=%fused_computation.15 | loop fusion | flops 96 | bytes 772 | tf_op jit(solution)/shard_map/sub | solution.py:159
  11.0 0.0 collective-permute-done.2.pr_ref
  11.0 0.0 collective-permute-done.1.pl_ref
  11.0 0.0 copy-start.4
  11.0 0.0 collective-permute-done.pe_ref
  11.0 0.0 copy-start.5
  11.1 0.7 %pad_add_fusion.pc_ref = s32[16,4]{1,0:T(8,128)} fusion(s32[8,4]{1,0:T(8,128)S(1)} %get-tuple-element.34, s32[8,4]{1,0:T(8,128)S(1)} %get-tuple-element.33), kind=kLoop, calls=%fused_computation.8 | loop fusion | flops 64 | bytes 512 | tf_op jit(solution)/shard_map/concatenate | solution.py:151
  11.8 0.1 copy-done.4
  11.9 0.1 copy-done.5
  11.9 5.4 %shard_map.47 = (f32[128,640]{1,0:T(8,128)}, f32[128,640]{1,0:T(8,128)}, f32[128,640]{1,0:T(8,128)}, f32[128,640]{1,0:T(8,128)}) custom-call(s32[2]{0:T(128)} %add_convert_fusion.1.flag_ref, s32[8,12]{1,0:T(8,128)} %broadcast_subtract_fusion.1.lc_ref, s32[16,4]{1,0:T(8,128)} %pad_add_fusion.pc_ref, bf16[512,768]{1,0:T(8,128)(2,1)} %a_ref.1, ...), custom_call_target="tpu_custom_call" | custom-call | flops 754974720 | bytes 4194304 | tf_op jit(solution)/shard_map/pallas_call | solution.py:116
  17.4 0.7 %collective-permute-start.3 = (f32[128,640]{1,0:T(8,128)}, f32[128,640]{1,0:T(8,128)S(1)}, u32[]{:S(2)}, u32[]{:S(2)}) collective-permute-start(f32[128,640]{1,0:T(8,128)} %get-tuple-element.26), channel_id=1, source_target_pairs={{15,16},{16,15}} | collective-permute-start | bytes 983048 | tf_op jit(solution)/shard_map/ppermute | solution.py:29
  18.0 1.3 %collective-permute-start.4 = (f32[128,640]{1,0:T(8,128)}, f32[128,640]{1,0:T(8,128)S(1)}, u32[]{:S(2)}, u32[]{:S(2)}) collective-permute-start(f32[128,640]{1,0:T(8,128)} %get-tuple-element.27), channel_id=1, source_target_pairs={{1,0},{2,1},{3,2},{4,3},{5,4},{6,5},{7,6},{8,7},{9,8},{10,9},{11,1... | collective-permute-start | bytes 983048 | tf_op jit(solution)/shard_map/ppermute | solution.py:21
  19.3 0.0 copy-start
  19.3 5.5 %collective-permute-start.5 = (f32[128,640]{1,0:T(8,128)}, f32[128,640]{1,0:T(8,128)S(1)}, u32[]{:S(2)}, u32[]{:S(2)}) collective-permute-start(f32[128,640]{1,0:T(8,128)} %get-tuple-element.28), channel_id=1, source_target_pairs={{0,1},{1,2},{2,3},{3,4},{4,5},{5,6},{6,7},{7,8},{8,9},{9,10},{10,1... | collective-permute-start | bytes 983048 | tf_op jit(solution)/shard_map/ppermute | solution.py:21
  24.9 0.0 collective-permute-done.3
  24.9 0.0 collective-permute-done.4
  24.9 1.4 %collective-permute-done.5 = f32[128,640]{1,0:T(8,128)S(1)} collective-permute-done((f32[128,640]{1,0:T(8,128)}, f32[128,640]{1,0:T(8,128)S(1)}, u32[]{:S(2)}, u32[]{:S(2)}) %collective-permute-start.5) | collective-permute-done | bytes 327712 | tf_op jit(solution)/shard_map/ppermute | solution.py:21
  26.3 0.1 broadcast_select_fusion.1
  26.4 12.6 %collective-permute-start.6 = (bf16[1,128,896]{2,1,0:T(8,128)(2,1)S(1)}, bf16[1,128,896]{2,1,0:T(8,128)(2,1)S(1)}, u32[]{:S(2)}, u32[]{:S(2)}) collective-permute-start(bf16[1,128,896]{2,1,0:T(8,128)(2,1)S(1)} %fusion.2), channel_id=1, source_target_pairs={{0,16},{16,0},{1,17},{17,1},{2,18},{18,2},{3,19},{19,3},{4,20},{20... | collective-permute-start | bytes 688136 | tf_op jit(solution)/shard_map/ppermute | solution.py:33
  39.0 0.8 %pad_maximum_fusion = bf16[2,128,896]{2,1,0:T(8,128)(2,1)} fusion(bf16[1,128,896]{2,1,0:T(8,128)(2,1)S(1)} %fusion.2), kind=kLoop, calls=%fused_computation.2 | loop fusion | flops 229376 | bytes 688128 | tf_op jit(solution)/shard_map/concatenate | solution.py:174
  39.8 4.4 %collective-permute-done.6 = bf16[1,128,896]{2,1,0:T(8,128)(2,1)S(1)} collective-permute-done((bf16[1,128,896]{2,1,0:T(8,128)(2,1)S(1)}, bf16[1,128,896]{2,1,0:T(8,128)(2,1)S(1)}, u32[]{:S(2)}, u32[]{:S(2)}) %collective-permute-start.6) | collective-permute-done | bytes 229408 | tf_op jit(solution)/shard_map/ppermute | solution.py:33
  44.2 0.7 %constant_dynamic-update-slice_fusion = bf16[2,128,896]{2,1,0:T(8,128)(2,1)} fusion(bf16[2,128,896]{2,1,0:T(8,128)(2,1)} %pad_maximum_fusion, bf16[1,128,896]{2,1,0:T(8,128)(2,1)S(1)} %collective-permute-done.6, s32[]{:T(128)S(6)} %select_n.39), kind=kLoop, calls=%fused_computation.17 | loop fusion | bytes 458756 | tf_op jit(solution)/shard_map/dynamic_update_slice | solution.py:175
  (9 shorter events, 0.1 us)
Async XLA Ops:
  0.0 0.7 %copy-start.2 = (s32[8,4]{0,1:T(4,128)S(1)}, s32[8,4]{0,1:T(4,128)}, u32[]{:S(2)}) copy-start(s32[8,4]{0,1:T(4,128)} %param.9) | copy-start | bytes 388
  1.7 9.3 %collective-permute-start.2 = (bf16[528,256]{1,0:T(8,128)(2,1)S(1)}, bf16[528,256]{1,0:T(8,128)(2,1)S(1)}, u32[]{:S(2)}, u32[]{:S(2)}) collective-permute-start(bf16[528,256]{1,0:T(8,128)(2,1)S(1)} %fusion.1), channel_id=1, source_target_pairs={{1,0},{2,1},{3,2},{4,3},{5,4},{6,5},{7,6},{8,7},{9,8},{10,9},{11,1... | collective-permute-start | bytes 811016 | tf_op jit(solution)/shard_map/ppermute | solution.py:21
  3.0 8.0 %collective-permute-start.1 = (bf16[528,256]{1,0:T(8,128)(2,1)S(1)}, bf16[528,256]{1,0:T(8,128)(2,1)S(1)}, u32[]{:S(2)}, u32[]{:S(2)}) collective-permute-start(bf16[528,256]{1,0:T(8,128)(2,1)S(1)} %fusion.1), channel_id=1, source_target_pairs={{0,1},{1,2},{2,3},{3,4},{4,5},{5,6},{6,7},{7,8},{8,9},{9,10},{10,1... | collective-permute-start | bytes 811016 | tf_op jit(solution)/shard_map/ppermute | solution.py:21
  6.1 4.9 %collective-permute-start = (bf16[528,256]{1,0:T(8,128)(2,1)S(1)}, bf16[528,256]{1,0:T(8,128)(2,1)S(1)}, u32[]{:S(2)}, u32[]{:S(2)}) collective-permute-start(bf16[528,256]{1,0:T(8,128)(2,1)S(1)} %fusion.1), channel_id=1, source_target_pairs={{15,16},{16,15}} | collective-permute-start | bytes 811016 | tf_op jit(solution)/shard_map/ppermute | solution.py:29
  8.0 2.4 %copy-start.1 = (s32[8,12]{1,0:T(8,128)S(1)}, s32[8,12]{1,0:T(8,128)}, u32[]{:S(2)}) copy-start(s32[8,12]{1,0:T(8,128)} %param.7) | copy-start | bytes 1156
  11.0 0.7 %copy-start.3 = (bf16[528,256]{1,0:T(8,128)(2,1)}, bf16[528,256]{1,0:T(8,128)(2,1)S(1)}, u32[]{:S(2)}) copy-start(bf16[528,256]{1,0:T(8,128)(2,1)S(1)} %collective-permute-done.2.pr_ref) | copy-start | bytes 811012
  11.0 0.8 %copy-start.4 = (bf16[528,256]{1,0:T(8,128)(2,1)}, bf16[528,256]{1,0:T(8,128)(2,1)S(1)}, u32[]{:S(2)}) copy-start(bf16[528,256]{1,0:T(8,128)(2,1)S(1)} %collective-permute-done.1.pl_ref) | copy-start | bytes 811012
  11.0 0.9 %copy-start.5 = (bf16[528,256]{1,0:T(8,128)(2,1)}, bf16[528,256]{1,0:T(8,128)(2,1)S(1)}, u32[]{:S(2)}) copy-start(bf16[528,256]{1,0:T(8,128)(2,1)S(1)} %collective-permute-done.pe_ref) | copy-start | bytes 811012
  17.4 7.5 %collective-permute-start.3 = (f32[128,640]{1,0:T(8,128)}, f32[128,640]{1,0:T(8,128)S(1)}, u32[]{:S(2)}, u32[]{:S(2)}) collective-permute-start(f32[128,640]{1,0:T(8,128)} %get-tuple-element.26), channel_id=1, source_target_pairs={{15,16},{16,15}} | collective-permute-start | bytes 983048 | tf_op jit(solution)/shard_map/ppermute | solution.py:29
  18.0 6.8 %collective-permute-start.4 = (f32[128,640]{1,0:T(8,128)}, f32[128,640]{1,0:T(8,128)S(1)}, u32[]{:S(2)}, u32[]{:S(2)}) collective-permute-start(f32[128,640]{1,0:T(8,128)} %get-tuple-element.27), channel_id=1, source_target_pairs={{1,0},{2,1},{3,2},{4,3},{5,4},{6,5},{7,6},{8,7},{9,8},{10,9},{11,1... | collective-permute-start | bytes 983048 | tf_op jit(solution)/shard_map/ppermute | solution.py:21
  19.3 7.0 %copy-start = (f32[128,640]{1,0:T(8,128)S(1)}, f32[128,640]{1,0:T(8,128)}, u32[]{:S(2)}) copy-start(f32[128,640]{1,0:T(8,128)} %get-tuple-element.25) | copy-start | bytes 983044
  19.3 6.9 %collective-permute-start.5 = (f32[128,640]{1,0:T(8,128)}, f32[128,640]{1,0:T(8,128)S(1)}, u32[]{:S(2)}, u32[]{:S(2)}) collective-permute-start(f32[128,640]{1,0:T(8,128)} %get-tuple-element.28), channel_id=1, source_target_pairs={{0,1},{1,2},{2,3},{3,4},{4,5},{5,6},{6,7},{7,8},{8,9},{9,10},{10,1... | collective-permute-start | bytes 983048 | tf_op jit(solution)/shard_map/ppermute | solution.py:21
  26.4 17.8 %collective-permute-start.6 = (bf16[1,128,896]{2,1,0:T(8,128)(2,1)S(1)}, bf16[1,128,896]{2,1,0:T(8,128)(2,1)S(1)}, u32[]{:S(2)}, u32[]{:S(2)}) collective-permute-start(bf16[1,128,896]{2,1,0:T(8,128)(2,1)S(1)} %fusion.2), channel_id=1, source_target_pairs={{0,16},{16,0},{1,17},{17,1},{2,18},{18,2},{3,19},{19,3},{4,20},{20... | collective-permute-start | bytes 688136 | tf_op jit(solution)/shard_map/ppermute | solution.py:33
